TPU v7x, 32 devices: a whole 2x2x4 slice. The times are simulated.
32 devices in a mesh: dp: 8 (over z, x), group: 4 (over y, core).
Axes of the slice: x: 2, y: 2, z: 4, core: 2. Of those that a mesh axis runs over, the one named last changes fastest.
Arguments:
- partials: float32 [4, 54, 1024, 1024], P('group', None, 'dp'), may hold values from -0.3 to 0.3
- second_moment: float32 [54, 1024, 1024], P(None, 'dp', 'group'), may hold values from 0.0001 to 0.01
- left_stats: float32 [54, 1024, 1024], P(None, 'dp', 'group'), may hold values from -3 to 3
- right_stats: float32 [54, 1024, 1024], P(None, 'dp', 'group'), may hold values from -3 to 3
- left_roots: bfloat16 [54, 1024, 1024], P(None, 'dp', 'group'), may hold values from -0.2 to 2.1
- right_roots: bfloat16 [54, 1024, 1024], P(None, 'dp', 'group'), may hold values from -0.2 to 2.1
- norm_partials: float32 [8, 4, 2, 2048], P('dp', 'group'), may hold values from -0.012 to 0.012
- norm_moment: float32 [2, 2048], replicated, may hold values from 0.0001 to 0.01
Outputs:
- block_step: bfloat16 [54, 1024, 1024], P(None, 'dp', 'group')
- new_moment: float32 [54, 1024, 1024], P(None, 'dp', 'group')
- new_left: float32 [54, 1024, 1024], P(None, 'dp', 'group')
- new_right: float32 [54, 1024, 1024], P(None, 'dp', 'group')
- norm_step: float32 [2, 2048], replicated
- new_norm_moment: float32 [2, 2048], replicated
All inputs are finite; a program needn't handle non-finite values.
Results may differ from a plain program's by a relative error of at most 0.0042.
The roundings to bfloat16 on the way count: a program that leaves them out, or rounds other values in their place, can miss the bound.
Values may be sent and summed in bfloat16 or wider, within the bound.
No kernel may reach another device: no remote copies, remote signals or barrier semaphores. Data moves between devices by JAX's collectives and lax.ppermute only.
A program may use at most 384 MiB of HBM per device.

v0:
```python
import jax
import jax.numpy as jnp
from jax import lax
from jax.sharding import PartitionSpec as P

EPS_ADAM = 1e-08
EPS_GRAFT = 1e-06


def gram_step(piece, source, lower, quarter):
    own_rows = lax.dynamic_slice_in_dim(piece, lower, quarter, 1)
    gram_left = jnp.einsum("cim,cjm->cij", piece, own_rows, preferred_element_type=jnp.float32)
    block = jnp.einsum("cim,cij->cmj", piece, source, preferred_element_type=jnp.float32)
    return (gram_left, block)


def right_step(piece, right_root):
    return jnp.einsum("cim,cmj->cij", piece, right_root, preferred_element_type=jnp.float32)


def on_device(
    partials,
    second_moment,
    left_stats,
    right_stats,
    left_roots,
    right_roots,
    norm_partials,
    norm_moment,
):
    n_dp = lax.axis_size("dp")
    me_dp = lax.axis_index("dp")
    me_group = lax.axis_index("group")
    count = second_moment.shape[0]
    rows = partials.shape[2]
    quarter = second_moment.shape[2]
    width = rows * n_dp
    cap = 2 * -(-count // n_dp)
    lower = me_group * quarter
    local_norm = norm_partials[0, 0]
    norm_grad = lax.psum(local_norm, ("dp", "group"))
    grad = lax.psum_scatter(partials[0], "group", scatter_dimension=2, tiled=True)
    new_moment = 0.99 * second_moment + 0.01 * grad * grad
    adam = grad / (jnp.sqrt(new_moment) + EPS_ADAM)
    adam_part = jnp.sum(adam * adam, axis=(1, 2))
    adam_sq = lax.psum(adam_part, ("dp", "group"))
    grad_low = grad.astype(jnp.bfloat16)
    blocks_idx = jnp.arange(count, dtype=jnp.int32)
    owner = blocks_idx // cap
    slot = blocks_idx % cap
    slot_id = slot * n_dp + owner
    places = jnp.arange(cap * n_dp, dtype=jnp.int32)
    match = slot_id[None, :] == places[:, None]
    sender = jnp.max(jnp.where(match, blocks_idx[None, :], -1), axis=1)
    sender = jnp.where(sender < 0, count, sender)

    def to_slots(blocks):
        padded = jnp.concatenate([blocks, jnp.zeros((1, rows, quarter), blocks.dtype)], axis=0)
        return jnp.take(padded, sender, axis=0).reshape(cap, width, quarter)

    mine, left_root, right_root = (
        lax.all_to_all(to_slots(grad_low), "dp", split_axis=1, concat_axis=1, tiled=True),
        lax.all_to_all(to_slots(left_roots), "dp", split_axis=1, concat_axis=1, tiled=True),
        lax.all_to_all(to_slots(right_roots), "dp", split_axis=1, concat_axis=1, tiled=True),
    )
    piece = lax.all_gather(mine, "group", axis=2, tiled=True)
    grams = gram_step(piece, mine, lower, quarter)
    gram_left = grams[0]
    gram_right = grams[1]
    right_done = right_step(piece, right_root)
    back_left, back_right = (
        lax.all_to_all(
            gram_left.astype(jnp.bfloat16), "dp", split_axis=1, concat_axis=1, tiled=True
        ).astype(gram_left.dtype),
        lax.all_to_all(
            gram_right.astype(jnp.bfloat16), "dp", split_axis=1, concat_axis=1, tiled=True
        ).astype(gram_right.dtype),
    )
    left_term = jnp.take(back_left.reshape(cap * n_dp, rows, quarter), slot_id, axis=0)
    right_term = jnp.take(back_right.reshape(cap * n_dp, rows, quarter), slot_id, axis=0)
    half = right_done.astype(jnp.bfloat16)
    direction = jnp.einsum(
        "cim,cmj->cij",
        lax.all_gather(left_root, "group", axis=2, tiled=True),
        half,
        preferred_element_type=jnp.float32,
    )
    direction_sq = lax.psum(jnp.sum(direction * direction, axis=(1, 2)), "group")
    own_places = jnp.arange(cap, dtype=jnp.int32) * n_dp + me_dp
    own_match = slot_id[None, :] == own_places[:, None]
    adam_owned = jnp.sum(jnp.where(own_match, adam_sq[None, :], 0.0), axis=1)
    ratio = jnp.sqrt(adam_owned / (direction_sq + EPS_GRAFT))
    scaled = (ratio[:, None, None] * direction).astype(jnp.bfloat16)
    steps_home = lax.all_to_all(scaled, "dp", split_axis=1, concat_axis=1, tiled=True)
    block_step = jnp.take(steps_home.reshape(cap * n_dp, rows, quarter), slot_id, axis=0)
    new_left = 0.95 * left_stats + 0.05 * left_term
    new_right = 0.95 * right_stats + 0.05 * right_term
    new_norm_moment = 0.99 * norm_moment + 0.01 * norm_grad * norm_grad
    norm_step = norm_grad / (jnp.sqrt(new_norm_moment) + EPS_ADAM)
    return (block_step, new_moment, new_left, new_right, norm_step, new_norm_moment)


def solution(mesh):
    return jax.shard_map(
        on_device,
        mesh=mesh,
        in_specs=(
            P("group", None, "dp", None),
            P(None, "dp", "group"),
            P(None, "dp", "group"),
            P(None, "dp", "group"),
            P(None, "dp", "group"),
            P(None, "dp", "group"),
            P("dp", "group", None, None),
            P(),
        ),
        out_specs=(
            P(None, "dp", "group"),
            P(None, "dp", "group"),
            P(None, "dp", "group"),
            P(None, "dp", "group"),
            P(),
            P(),
        ),
        check_vma=False,
    )
```

profile of v0, /device:TPU:0, one launch (start us, length us, event | category | flops | bytes accessed | tf_op | source)
XLA Modules:
  0.0 1543.1 jit_solution(14697825940211796568)
XLA Ops:
  14.9 9.2 gather_fusion.3
  24.2 10.3 gather_fusion.1
  34.5 179.8 %reduce-scatter.2.cloned.1.call-done = f32[54,128,256]{2,1,0:T(8,128)} async-done(((f32[54,128,1024]{2,1,0:T(8,128)}), f32[54,128,256]{2,1,0:T(8,128)}) %reduce-scatter.2.cloned.1.call-update) | async-done | bytes 7077904 | tf_op jit(solution)/shard_map/reduce_scatter | solution.py:42
  214.3 12.0 multiply_reduce_fusion.1
  228.4 8.3 gather_fusion.2
  236.7 12.5 broadcast_select_fusion
  249.2 7.6 copy.57
  256.8 188.6 %all_to_all.30 = bf16[14,1024,256]{2,0,1:T(8,128)(2,1)S(1)} all-to-all(bf16[14,1024,256]{2,0,1:T(8,128)(2,1)} %copy.57), channel_id=1, replica_groups=mesh['dp'=8,'group'=4] {'dp'}, dimensions={1} | all-to-all | bytes 14680064 | tf_op jit(solution)/shard_map/all_to_all | solution.py:62
  451.2 12.5 copy.55
  463.7 187.3 %all_to_all.31 = bf16[14,1024,256]{2,0,1:T(8,128)(2,1)S(1)} all-to-all(bf16[14,1024,256]{2,0,1:T(8,128)(2,1)} %copy.55), channel_id=1, replica_groups=mesh['dp'=8,'group'=4] {'dp'}, dimensions={1} | all-to-all | bytes 14680064 | tf_op jit(solution)/shard_map/all_to_all | solution.py:63
  651.0 5.9 copy.56
  657.0 12.4 copy.59
  675.0 16.1 %convolution_convert_fusion = bf16[14,1024,256]{2,1,0:T(8,128)(2,1)S(1)} fusion(bf16[14,1024,1024]{2,1,0:T(8,128)(2,1)} %all-gather.5.cloned.1.call-done, bf16[14,1024,256]{2,1,0:T(8,128)(2,1)} %copy.58), kind=kOutput, calls=%fused_computation.24 | convolution fusion | flops 7519862784 | bytes 44040192 | tf_op jit(solution)/shard_map/cim,cij->cmj/dot_general | solution.py:13
  691.2 7.7 copy.67
  698.8 158.8 %all-to-all-done.2 = bf16[14,1024,256]{2,0,1:T(8,128)(2,1)} async-done(((bf16[14,1024,256]{2,0,1:T(8,128)(2,1)}), bf16[14,1024,256]{2,0,1:T(8,128)(2,1)}, u32[]{:S(2)}, u32[]{:S(2)}) %all-to-all-start.2) | async-done | bytes 7340064 | tf_op jit(solution)/shard_map/all_to_all | solution.py:64
  862.7 17.8 %fusion.9 = bf16[14,1024,256]{2,1,0:T(8,128)(2,1)} fusion(bf16[14,1024,1024]{2,1,0:T(8,128)(2,1)} %all-gather.5.cloned.1.call-done, s32[]{:T(128)S(6)} %select_n.115), kind=kOutput, calls=%fused_computation.25 | convolution fusion | flops 7519862784 | bytes 44040196 | tf_op jit(solution)/shard_map/cim,cjm->cij/dot_general | solution.py:12
  880.5 10.6 copy.63
  891.1 153.7 %all-to-all-done.5 = bf16[14,1024,256]{2,0,1:T(8,128)(2,1)} async-done(((bf16[14,1024,256]{2,0,1:T(8,128)(2,1)}), bf16[14,1024,256]{2,0,1:T(8,128)(2,1)}, u32[]{:S(2)}, u32[]{:S(2)}) %all-to-all-start.5) | async-done | bytes 7340064 | tf_op jit(solution)/shard_map/all_to_all | solution.py:75
  1049.8 202.5 %all-reduce.3 = (f32[54]{0:T(128)S(1)}, f32[2,2048]{1,0:T(2,128)S(1)}) all-reduce(f32[54]{0:T(128)S(1)} %get-tuple-element.12, f32[2,2048]{1,0:T(2,128)S(1)} %bitcast.29), channel_id=1, replica_groups=mesh['dp'=8,'group'=4] {'dp','group'}, use_global_device_ids=true, to_apply=%region_2.0 | all-reduce | flops 4150 | bytes 33200 | tf_op jit(solution)/shard_map/psum | solution.py:46
  1252.5 19.4 %fusion.5.clone.4 = bf16[14,1024,256]{2,1,0:T(8,128)(2,1)} fusion(bf16[14,1024,1024]{2,1,0:T(8,128)(2,1)} %all-gather.5.cloned.1.call-done, bf16[14,1024,256]{2,0,1:T(8,128)(2,1)} %all-to-all-done.2), kind=kOutput, calls=%fused_computation.14.clone.clone.clone.1 | convolution fusion | flops 7519862784 | bytes 44040192 | tf_op jit(solution)/shard_map/cim,cmj->cij/dot_general | solution.py:18
  1271.9 18.5 %multiply_reduce_fusion = (f32[14]{0:T(128)S(1)}, f32[14,1024,256]{2,1,0:T(8,128)}) fusion(bf16[14,1024,1024]{2,1,0:T(8,128)(2,1)} %all-gather.3.cloned.1.call-done, bf16[14,1024,256]{2,1,0:T(8,128)(2,1)} %fusion.5.clone.4), kind=kOutput, calls=%fused_computation.7 | convolution fusion | flops 7523532800 | bytes 51380280 | tf_op jit(solution)/shard_map/cim,cmj->cij/dot_general | solution.py:82
  1296.2 9.6 multiply_convert_fusion
  1305.8 10.7 copy.61
  1322.5 6.0 copy.64
  1328.5 7.2 convert.2
  1335.7 6.0 copy.68
  1341.7 7.2 convert.3
  1348.9 9.1 gather_fusion.4
  1358.1 9.1 gather_fusion.5
  1367.2 138.2 %all-to-all-done.3 = bf16[14,1024,256]{2,0,1:T(8,128)(2,1)} async-done(((bf16[14,1024,256]{2,0,1:T(8,128)(2,1)}), bf16[14,1024,256]{2,0,1:T(8,128)(2,1)}, u32[]{:S(2)}, u32[]{:S(2)}) %all-to-all-start.3) | async-done | bytes 7340064 | tf_op jit(solution)/shard_map/all_to_all | solution.py:94
  1505.4 8.9 copy.62
  1520.4 16.0 %fusion.7 = (f32[54,128,256]{2,1,0:T(8,128)}, f32[54,128,256]{2,1,0:T(8,128)}) fusion(f32[54,128,256]{2,1,0:T(8,128)} %gather_fusion.5, f32[54,128,256]{2,1,0:T(8,128)} %param.15, pred[54]{0:T(512)(128)(4,1)S(1)} %compare_and_fusion.1, f32[54,128,256]{2,1,0:T(8,128)} %gather_fusion.4, f32[54,128,256]{2,1,0:T(8,128)} %param.14), kind=kLoop, calls=%fused_computation.20 | loop fusion | flops 14155776 | bytes 42467384 | tf_op jit(solution)/shard_map/add | solution.py:97
  (41 shorter events, 49.5 us)
Async XLA Ops:
  7.2 207.1 %reduce-scatter.2.cloned.1.call-start = ((), (), s32[]{:S(2)}) async-start(), calls=%async_computation.7 | async-start | bytes 35389440 | tf_op jit(solution)/shard_map/reduce_scatter | solution.py:42
  7.2 2.0 copy-start
  7.9 667.1 %all-gather.5.cloned.1.call-start = ((), (), s32[]{:S(2)}) async-start(), calls=%async_computation.9 | async-start | bytes 36700160 | tf_op jit(solution)/shard_map/all_gather | solution.py:66
  9.2 3.3 copy-start.1
  451.2 820.7 %all-gather.3.cloned.1.call-start = ((), (), s32[]{:S(2)}) async-start(), calls=%async_computation.8 | async-start | bytes 36700160 | tf_op jit(solution)/shard_map/all_gather | solution.py:84
  669.4 188.2 %all-to-all-start.2 = ((bf16[14,1024,256]{2,0,1:T(8,128)(2,1)}), bf16[14,1024,256]{2,0,1:T(8,128)(2,1)}, u32[]{:S(2)}, u32[]{:S(2)}) async-start(bf16[14,1024,256]{2,0,1:T(8,128)(2,1)} %copy.59), calls=%async_computation.3 | async-start | bytes 16777216 | tf_op jit(solution)/shard_map/all_to_all | solution.py:64
  857.6 187.1 %all-to-all-start.5 = ((bf16[14,1024,256]{2,0,1:T(8,128)(2,1)}), bf16[14,1024,256]{2,0,1:T(8,128)(2,1)}, u32[]{:S(2)}, u32[]{:S(2)}) async-start(bf16[14,1024,256]{2,0,1:T(8,128)(2,1)} %copy.67), calls=%async_computation.6 | async-start | bytes 16777216 | tf_op jit(solution)/shard_map/all_to_all | solution.py:75
  891.1 158.7 %copy-start.2 = (f32[1,1,2,2048]{3,2,1,0:T(2,128)S(1)}, f32[1,1,2,2048]{3,2,1,0:T(2,128)}, u32[]{:S(2)}) copy-start(f32[1,1,2,2048]{3,2,1,0:T(2,128)} %param.18) | copy-start | bytes 49156
  1044.7 271.8 %all-to-all-start.4 = ((bf16[14,1024,256]{2,0,1:T(8,128)(2,1)}), bf16[14,1024,256]{2,0,1:T(8,128)(2,1)}, u32[]{:S(2)}, u32[]{:S(2)}) async-start(bf16[14,1024,256]{2,0,1:T(8,128)(2,1)} %copy.63), calls=%async_computation.5 | async-start | bytes 16777216 | tf_op jit(solution)/shard_map/all_to_all | solution.py:72
  1316.5 5.3 copy-start.3
  1316.5 188.9 %all-to-all-start.3 = ((bf16[14,1024,256]{2,0,1:T(8,128)(2,1)}), bf16[14,1024,256]{2,0,1:T(8,128)(2,1)}, u32[]{:S(2)}, u32[]{:S(2)}) async-start(bf16[14,1024,256]{2,0,1:T(8,128)(2,1)} %copy.61), calls=%async_computation.4 | async-start | bytes 16777216 | tf_op jit(solution)/shard_map/all_to_all | solution.py:94
Sparse Core Ops, SparseCore 0:
  10.6 203.6 reduce-scatter.1
  451.3 180.0 all-gather.4
  657.1 179.5 all-gather.2
where the time goes:
time: 1550 us; the launch traced here: 1540 us
  waiting for transfers between devices  631 us (41%)
  blocking collectives  584 us (38%)
  local copies, waits for them, and re-layouts  153 us (10%)
  matrix products  71.8 us (5%)
  other arithmetic  67.7 us (4%)
  starting transfers between devices  21.1 us (1%)
    psum x1, blocking collectives, on_device(): adam_sq = lax.psum(adam_part, ('dp', 'group'))  203 us
    all_to_all x1, blocking collectives, on_device(): lax.all_to_all(to_slots(grad_low), 'dp', split_axis=1, concat_axis=1, til...  189 us
    all_to_all x1, blocking collectives, on_device(): lax.all_to_all(to_slots(left_roots), 'dp', split_axis=1, concat_axis=1, t...  187 us
    reduce_scatter x1, waiting for transfers between devices, on_device(): lax.psum_scatter(partials[0], 'group', scatter_dimension=2, tiled=True)  180 us
    all_to_all x1, waiting for transfers between devices, on_device(): lax.all_to_all(to_slots(right_roots), 'dp', split_axis=1, concat_axis=1,...  159 us
    all_to_all x1, waiting for transfers between devices, on_device(): lax.all_to_all(gram_right.astype(jnp.bfloat16), 'dp', split_axis=1, conca...  154 us
    all_to_all x1, waiting for transfers between devices, on_device(): lax.all_to_all(scaled, 'dp', split_axis=1, concat_axis=1, tiled=True)  138 us
    reshape x3, local copies, waits for them, and re-layouts, to_slots(): return jnp.take(padded, sender, axis=0).reshape(cap, width, quarter)  32.5 us
  transfers between devices with their start and end apart: 7, of which 4 were waited for; matrix products, arithmetic and copies ran while one was open for 14% of the time, Pallas kernels for 0%

commit v1 on v0

v1 whole, which is shorter than its diff:
```python
import jax
import jax.numpy as jnp
from jax import lax
from jax.sharding import PartitionSpec as P

EPS_ADAM = 1e-08
EPS_GRAFT = 1e-06


def on_device(
    partials,
    second_moment,
    left_stats,
    right_stats,
    left_roots,
    right_roots,
    norm_partials,
    norm_moment,
):
    n_dp = lax.axis_size("dp")
    me_dp = lax.axis_index("dp")
    me_group = lax.axis_index("group")
    count = second_moment.shape[0]
    rows = partials.shape[2]
    quarter = second_moment.shape[2]
    width = rows * n_dp
    cap = -(-count // n_dp)
    slots = cap * n_dp
    lower = me_group * quarter

    def to_owners(blocks):
        padded = jnp.pad(blocks, ((0, slots - count), (0, 0), (0, 0)))
        sent = lax.all_to_all(padded.reshape(n_dp, cap, rows, quarter), "dp", 0, 0, tiled=True)
        return sent.transpose(1, 0, 2, 3).reshape(cap, width, quarter)

    def to_keepers(owned):
        back = lax.all_to_all(owned, "dp", 0, 0, tiled=True)
        return back.reshape(slots, rows, quarter)[:count]

    left_root = to_owners(left_roots)
    right_root = to_owners(right_roots)

    local_norm = norm_partials[0, 0]
    norm_grad = lax.psum(local_norm, ("dp", "group"))
    grad = lax.psum_scatter(partials[0], "group", scatter_dimension=2, tiled=True)
    new_moment = 0.99 * second_moment + 0.01 * grad * grad
    adam = grad / (jnp.sqrt(new_moment) + EPS_ADAM)
    adam_part = jnp.sum(adam * adam, axis=(1, 2))
    adam_sq = lax.psum(adam_part, ("dp", "group"))
    grad_low = grad.astype(jnp.bfloat16)

    mine = to_owners(grad_low)
    piece = lax.all_gather(mine, "group", axis=2, tiled=True)
    own_rows = lax.dynamic_slice_in_dim(piece, lower, quarter, 1)
    piece4 = piece.reshape(cap, n_dp, rows, width)
    gram_left = jnp.einsum("cdim,cjm->dcij", piece4, own_rows, preferred_element_type=jnp.float32)
    gram_right = jnp.einsum("cim,cij->cmj", piece, mine, preferred_element_type=jnp.float32)
    gram_right = gram_right.reshape(cap, n_dp, rows, quarter).transpose(1, 0, 2, 3)
    left_term = to_keepers(gram_left.astype(jnp.bfloat16)).astype(jnp.float32)
    right_term = to_keepers(gram_right.astype(jnp.bfloat16)).astype(jnp.float32)

    half = jnp.einsum("cim,cmj->cij", piece, right_root, preferred_element_type=jnp.float32)
    half = half.astype(jnp.bfloat16)
    full_left = lax.all_gather(left_root, "group", axis=2, tiled=True)
    full_left4 = full_left.reshape(cap, n_dp, rows, width)
    direction = jnp.einsum("cdim,cmj->dcij", full_left4, half, preferred_element_type=jnp.float32)
    direction_sq = lax.psum(jnp.sum(direction * direction, axis=(0, 2, 3)), "group")
    adam_pad = jnp.pad(adam_sq, (0, slots - count))
    adam_owned = lax.dynamic_slice_in_dim(adam_pad, me_dp * cap, cap)
    ratio = jnp.sqrt(adam_owned / (direction_sq + EPS_GRAFT))
    scaled = (ratio[None, :, None, None] * direction).astype(jnp.bfloat16)
    block_step = to_keepers(scaled)

    new_left = 0.95 * left_stats + 0.05 * left_term
    new_right = 0.95 * right_stats + 0.05 * right_term
    new_norm_moment = 0.99 * norm_moment + 0.01 * norm_grad * norm_grad
    norm_step = norm_grad / (jnp.sqrt(new_norm_moment) + EPS_ADAM)
    return (block_step, new_moment, new_left, new_right, norm_step, new_norm_moment)


def solution(mesh):
    return jax.shard_map(
        on_device,
        mesh=mesh,
        in_specs=(
            P("group", None, "dp", None),
            P(None, "dp", "group"),
            P(None, "dp", "group"),
            P(None, "dp", "group"),
            P(None, "dp", "group"),
            P(None, "dp", "group"),
            P("dp", "group", None, None),
            P(),
        ),
        out_specs=(
            P(None, "dp", "group"),
            P(None, "dp", "group"),
            P(None, "dp", "group"),
            P(None, "dp", "group"),
            P(),
            P(),
        ),
        check_vma=False,
    )
```

time: 1550 us -> 753 us (0.49)
  blocking collectives: 584 us -> 220 us
  waiting for transfers between devices: 631 us -> 392 us
  local copies, waits for them, and re-layouts: 153 us -> 37.2 us
  matrix products: 71.8 us -> 35 us
  other arithmetic: 67.7 us -> 33.9 us
    all_to_all x2, blocking collectives: 376 us -> 176 us  [to_owners(): lax.all_to_all(padded.reshape(n_dp, cap, rows, quarter), 'dp', 0, 0, tile...]
    all_to_all x4, waiting for transfers between devices: 451 us -> 278 us  [the longest x3 197 us: to_keepers(): back = lax.all_to_all(owned, 'dp', 0, 0, tiled=True)]
    psum x1, blocking collectives: 203 us -> 37.8 us  [on_device(): adam_sq = lax.psum(adam_part, ('dp', 'group'))]
    reduce_scatter x1, waiting for transfers between devices: 180 us -> 113 us  [on_device(): lax.psum_scatter(partials[0], 'group', scatter_dimension=2, tiled=True)]
    gather x6 -> x0, local copies, waits for them, and re-layouts: 49.9 us -> none  [the longest x3 27.8 us: to_slots(): return jnp.take(padded, sender, axis=0).reshape(cap, width, quarter)]
    dot_general x4 -> x3, matrix products: 71.8 us -> 35 us  [the longest x1 17.6 us: on_device(): jnp.einsum('cdim,cmj->dcij', full_left4, half, preferred_element_type=jnp...]
    reshape x3 -> x0, local copies, waits for them, and re-layouts: 32.5 us -> none  [to_slots(): return jnp.take(padded, sender, axis=0).reshape(cap, width, quarter)]
    convert_element_type x3, local copies, waits for them, and re-layouts: 28.9 us -> 6.44 us  [the longest x1 2.27 us: on_device(): scaled = (ratio[None, :, None, None] * direction).astype(jnp.bfloat16)]
  transfers between devices with their start and end apart: 7 -> 7, of which waited for: 4 -> 5; matrix products, arithmetic and copies ran while one was open for 14% -> 9% of each run, Pallas kernels for 0% -> 0%
where the time goes in v1:
time: 753 us; the launch traced here: 752 us
  waiting for transfers between devices  392 us (52%)
  blocking collectives  220 us (29%)
  local copies, waits for them, and re-layouts  37.2 us (5%)
  matrix products  35 us (5%)
  other arithmetic  33.9 us (5%)
  starting transfers between devices  19.8 us (3%)
  between operations  13.9 us (2%)
    all_to_all x3, waiting for transfers between devices, to_keepers(): back = lax.all_to_all(owned, 'dp', 0, 0, tiled=True)  197 us
    all_to_all x2, blocking collectives, to_owners(): lax.all_to_all(padded.reshape(n_dp, cap, rows, quarter), 'dp', 0, 0, tile...  176 us
    reduce_scatter x1, waiting for transfers between devices, on_device(): lax.psum_scatter(partials[0], 'group', scatter_dimension=2, tiled=True)  113 us
    all_to_all x1, waiting for transfers between devices, to_owners(): lax.all_to_all(padded.reshape(n_dp, cap, rows, quarter), 'dp', 0, 0, tile...  81.1 us
    psum x1, blocking collectives, on_device(): adam_sq = lax.psum(adam_part, ('dp', 'group'))  37.8 us
    dot_general x1, matrix products, on_device(): jnp.einsum('cdim,cmj->dcij', full_left4, half, preferred_element_type=jnp...  17.6 us
  transfers between devices with their start and end apart: 7, of which 5 were waited for; matrix products, arithmetic and copies ran while one was open for 9% of the time, Pallas kernels for 0%

profile of v1, /device:TPU:0, one launch (start us, length us, event | category | flops | bytes accessed | tf_op | source)
XLA Modules:
  0.0 751.8 jit_solution(357297306929678431)
XLA Ops:
  7.9 1.3 copy-done
  9.6 89.0 %all_to_all.30 = bf16[8,7,128,256]{3,2,1,0:T(8,128)(2,1)S(1)} all-to-all(bf16[8,7,128,256]{3,2,1,0:T(8,128)(2,1)S(1)} %bitcast.47), channel_id=1, replica_groups=mesh['dp'=8,'group'=4] {'dp'}, dimensions={0} | all-to-all | bytes 7340032 | tf_op jit(solution)/shard_map/all_to_all | solution.py:33
  98.6 2.3 copy.34
  100.9 113.3 %reduce-scatter.2.cloned.1.call-done = f32[54,128,256]{2,1,0:T(8,128)} async-done(((f32[54,128,1024]{2,1,0:T(8,128)}), f32[54,128,256]{2,1,0:T(8,128)}) %reduce-scatter.2.cloned.1.call-update) | async-done | bytes 7077904 | tf_op jit(solution)/shard_map/reduce_scatter | solution.py:45
  214.3 11.8 %multiply_reduce_fusion.1 = (f32[54]{0:T(128)S(1)}, f32[54,128,256]{2,1,0:T(8,128)}, bf16[54,128,256]{2,1,0:T(8,128)(2,1)S(1)}) fusion(f32[54,128,256]{2,1,0:T(8,128)} %reduce-scatter.2.cloned.1.call-done, f32[54,128,256]{2,1,0:T(8,128)} %param.9), kind=kLoop, calls=%fused_computation.6 | loop fusion | flops 15925194 | bytes 24772824 | tf_op jit(solution)/shard_map/reduce_sum | solution.py:48
  226.6 87.2 %all_to_all.31 = bf16[8,7,128,256]{3,2,1,0:T(8,128)(2,1)S(1)} all-to-all(bf16[8,7,128,256]{3,2,1,0:T(8,128)(2,1)S(1)} %bitcast.46), channel_id=1, replica_groups=mesh['dp'=8,'group'=4] {'dp'}, dimensions={0} | all-to-all | bytes 7340032 | tf_op jit(solution)/shard_map/all_to_all | solution.py:33
  313.8 2.3 copy.32
  316.2 1.0 copy-done.1
  317.2 2.2 pad.16
  319.3 4.7 all-to-all-start.1
  324.1 81.1 %all-to-all-done.1 = bf16[8,7,128,256]{3,2,1,0:T(8,128)(2,1)} async-done(((bf16[8,7,128,256]{3,2,1,0:T(8,128)(2,1)}), bf16[8,7,128,256]{3,2,1,0:T(8,128)(2,1)}, u32[]{:S(2)}, u32[]{:S(2)}) %all-to-all-start.1) | async-done | bytes 3670048 | tf_op jit(solution)/shard_map/all_to_all | solution.py:33
  405.1 4.3 copy.33
  409.4 37.8 %all-reduce.4 = (f32[54]{0:T(128)S(1)}, f32[2,2048]{1,0:T(2,128)S(1)}) all-reduce(f32[54]{0:T(128)S(1)} %get-tuple-element.10, f32[2,2048]{1,0:T(2,128)S(1)} %bitcast.58), channel_id=1, replica_groups=mesh['dp'=8,'group'=4] {'dp','group'}, use_global_device_ids=true, to_apply=%region_2.3 | all-reduce | flops 4150 | bytes 33200 | tf_op jit(solution)/shard_map/psum | solution.py:49
  447.2 17.6 %multiply_reduce_fusion = (f32[7]{0:T(128)S(1)}, f32[7,256,8,128]{3,1,2,0:T(8,128)}) fusion(bf16[7,8,128,1024]{3,2,1,0:T(8,128)(2,1)} %bitcast.60, bf16[7,1024,1024]{2,1,0:T(8,128)(2,1)} %all-gather.3.cloned.1.call-done, bf16[7,1024,256]{2,1,0:T(8,128)(2,1)} %bitcast.56), kind=kOutput, calls=%fused_computation.2 | convolution fusion | flops 7521697792 | bytes 40370204 | tf_op jit(solution)/shard_map/cdim,cmj->dcij/dot_general | solution.py:66
  464.8 5.9 psum.22
  470.8 4.1 fusion.1
  474.9 2.3 copy.36
  477.1 5.8 all-to-all-start.3
  482.9 8.5 %convert_bitcast_fusion = bf16[8,7,128,256]{2,3,0,1:T(8,128)(2,1)S(1)} fusion(bf16[7,8,128,1024]{3,2,1,0:T(8,128)(2,1)} %bitcast.59, bf16[7,1024,1024]{2,1,0:T(8,128)(2,1)} %all-gather.3.cloned.1.call-done, s32[]{:T(128)S(6)} %select_n.7), kind=kOutput, calls=%fused_computation.13 | convolution fusion | flops 3759931392 | bytes 22020100 | tf_op jit(solution)/shard_map/cdim,cjm->dcij/dot_general | solution.py:56
  491.4 2.1 copy.38
  493.5 71.5 %all-to-all-done.3 = bf16[8,7,128,256]{2,3,1,0:T(8,128)(2,1)} async-done(((bf16[8,7,128,256]{2,3,1,0:T(8,128)(2,1)}), bf16[8,7,128,256]{2,3,1,0:T(8,128)(2,1)}, u32[]{:S(2)}, u32[]{:S(2)}) %all-to-all-start.3) | async-done | bytes 3670048 | tf_op jit(solution)/shard_map/all_to_all | solution.py:37
  565.0 4.7 all-to-all-start.4
  569.6 9.0 %convolution_convert_fusion = bf16[7,1024,256]{2,1,0:T(8,128)(2,1)S(1)} fusion(bf16[7,1024,1024]{2,1,0:T(8,128)(2,1)} %all-gather.3.cloned.1.call-done, bf16[7,1024,256]{2,1,0:T(8,128)(2,1)} %bitcast.49), kind=kOutput, calls=%fused_computation.17 | convolution fusion | flops 3759931392 | bytes 22020096 | tf_op jit(solution)/shard_map/cim,cij->cmj/dot_general | solution.py:57
  578.7 2.0 copy.48
  580.7 70.2 %all-to-all-done.4 = bf16[8,7,128,256]{2,3,1,0:T(8,128)(2,1)} async-done(((bf16[8,7,128,256]{2,3,1,0:T(8,128)(2,1)}), bf16[8,7,128,256]{2,3,1,0:T(8,128)(2,1)}, u32[]{:S(2)}, u32[]{:S(2)}) %all-to-all-start.4) | async-done | bytes 3670048 | tf_op jit(solution)/shard_map/all_to_all | solution.py:37
  650.9 4.5 all-to-all-start.5
  656.1 6.2 copy.37
  662.3 4.2 slice.12
  666.5 6.2 copy.39
  672.7 8.6 %multiply_add_fusion.1 = f32[54,128,256]{2,1,0:T(8,128)} fusion(f32[54,128,256]{2,1,0:T(8,128)} %param.10, bf16[56,128,256]{2,1,0:T(8,128)(2,1)} %bitcast.55), kind=kLoop, calls=%fused_computation.5 | loop fusion | flops 7077888 | bytes 17694720 | tf_op jit(solution)/shard_map/add | solution.py:74
  681.3 55.4 %all-to-all-done.5 = bf16[8,7,128,256]{3,2,1,0:T(8,128)(2,1)} async-done(((bf16[8,7,128,256]{3,2,1,0:T(8,128)(2,1)}), bf16[8,7,128,256]{3,2,1,0:T(8,128)(2,1)}, u32[]{:S(2)}, u32[]{:S(2)}) %all-to-all-start.5) | async-done | bytes 3670048 | tf_op jit(solution)/shard_map/all_to_all | solution.py:37
  736.7 8.6 %multiply_add_fusion = f32[54,128,256]{2,1,0:T(8,128)} fusion(f32[54,128,256]{2,1,0:T(8,128)} %param.11, bf16[56,128,256]{2,1,0:T(8,128)(2,1)} %bitcast.21), kind=kLoop, calls=%fused_computation.4 | loop fusion | flops 7077888 | bytes 17694720 | tf_op jit(solution)/shard_map/add | solution.py:75
  (18 shorter events, 2.5 us)
Async XLA Ops:
  7.2 207.1 %reduce-scatter.2.cloned.1.call-start = ((), (), s32[]{:S(2)}) async-start(), calls=%async_computation.7 | async-start | bytes 35389440 | tf_op jit(solution)/shard_map/reduce_scatter | solution.py:45
  7.2 2.0 copy-start
  7.9 439.3 %all-gather.5.cloned.1.call-start = ((), (), s32[]{:S(2)}) async-start(), calls=%async_computation.9 | async-start | bytes 18350080 | tf_op jit(solution)/shard_map/all_gather | solution.py:64
  100.9 346.4 %all-gather.3.cloned.1.call-start = ((), (), s32[]{:S(2)}) async-start(), calls=%async_computation.8 | async-start | bytes 18350080 | tf_op jit(solution)/shard_map/all_gather | solution.py:53
  313.8 3.3 copy-start.1
  319.3 90.1 %copy-start.2 = (f32[1,1,2,2048]{3,2,1,0:T(2,128)S(1)}, f32[1,1,2,2048]{3,2,1,0:T(2,128)}, u32[]{:S(2)}) copy-start(f32[1,1,2,2048]{3,2,1,0:T(2,128)} %param.14) | copy-start | bytes 49156
  319.3 85.8 %all-to-all-start.1 = ((bf16[8,7,128,256]{3,2,1,0:T(8,128)(2,1)}), bf16[8,7,128,256]{3,2,1,0:T(8,128)(2,1)}, u32[]{:S(2)}, u32[]{:S(2)}) async-start(bf16[8,7,128,256]{3,2,1,0:T(8,128)(2,1)} %bitcast.45), calls=%async_computation.2 | async-start | bytes 7340032 | tf_op jit(solution)/shard_map/all_to_all | solution.py:33
  477.1 87.8 %all-to-all-start.3 = ((bf16[8,7,128,256]{2,3,1,0:T(8,128)(2,1)}), bf16[8,7,128,256]{2,3,1,0:T(8,128)(2,1)}, u32[]{:S(2)}, u32[]{:S(2)}) async-start(bf16[8,7,128,256]{2,3,1,0:T(8,128)(2,1)} %copy.36), calls=%async_computation.4 | async-start | bytes 7340032 | tf_op jit(solution)/shard_map/all_to_all | solution.py:37
  565.0 86.0 %all-to-all-start.4 = ((bf16[8,7,128,256]{2,3,1,0:T(8,128)(2,1)}), bf16[8,7,128,256]{2,3,1,0:T(8,128)(2,1)}, u32[]{:S(2)}, u32[]{:S(2)}) async-start(bf16[8,7,128,256]{2,3,1,0:T(8,128)(2,1)} %copy.38), calls=%async_computation.5 | async-start | bytes 7340032 | tf_op jit(solution)/shard_map/all_to_all | solution.py:37
  578.7 76.8 %copy-start.3 = (f32[2,2048]{1,0:T(2,128)S(1)}, f32[2,2048]{1,0:T(2,128)}, u32[]{:S(2)}) copy-start(f32[2,2048]{1,0:T(2,128)} %param.15) | copy-start | bytes 49156
  650.9 85.8 %all-to-all-start.5 = ((bf16[8,7,128,256]{3,2,1,0:T(8,128)(2,1)}), bf16[8,7,128,256]{3,2,1,0:T(8,128)(2,1)}, u32[]{:S(2)}, u32[]{:S(2)}) async-start(bf16[8,7,128,256]{3,2,1,0:T(8,128)(2,1)} %bitcast.51), calls=%async_computation.6 | async-start | bytes 7340032 | tf_op jit(solution)/shard_map/all_to_all | solution.py:37
Sparse Core Ops, SparseCore 0:
  10.6 203.6 reduce-scatter.1
  216.5 95.9 all-gather.4
  316.3 94.3 all-gather.2

commit v2 on v1

--- a/solution.py
+++ b/solution.py
@@ -41,12 +41,13 @@
     right_root = to_owners(right_roots)
 
     local_norm = norm_partials[0, 0]
-    norm_grad = lax.psum(local_norm, ("dp", "group"))
+    norm_grad = jnp.sum(lax.all_gather(local_norm, ("dp", "group")), axis=0)
     grad = lax.psum_scatter(partials[0], "group", scatter_dimension=2, tiled=True)
+    grad, left_root, right_root = lax.optimization_barrier((grad, left_root, right_root))
     new_moment = 0.99 * second_moment + 0.01 * grad * grad
     adam = grad / (jnp.sqrt(new_moment) + EPS_ADAM)
     adam_part = jnp.sum(adam * adam, axis=(1, 2))
-    adam_sq = lax.psum(adam_part, ("dp", "group"))
+    adam_sq = jnp.sum(lax.all_gather(adam_part, ("dp", "group")), axis=0)
     grad_low = grad.astype(jnp.bfloat16)
 
     mine = to_owners(grad_low)

time: 753 us -> 768 us (1.020)
  blocking collectives: 220 us -> 234 us
  waiting for transfers between devices: 392 us -> 378 us
    all_gather x0 -> x1, blocking collectives: none -> 102 us  [on_device(): norm_grad = jnp.sum(lax.all_gather(local_norm, ('dp', 'group')), axis=0)]
    reduce_scatter x1, waiting for transfers between devices: 113 us -> 23.1 us  [on_device(): lax.psum_scatter(partials[0], 'group', scatter_dimension=2, tiled=True)]
    all_to_all x2 -> x1, blocking collectives: 176 us -> 87.2 us  [to_owners(): lax.all_to_all(padded.reshape(n_dp, cap, rows, quarter), 'dp', 0, 0, tile...]
    all_to_all x1 -> x2, waiting for transfers between devices: 81.1 us -> 157 us  [to_owners(): lax.all_to_all(padded.reshape(n_dp, cap, rows, quarter), 'dp', 0, 0, tile...]
    all_to_all x3, waiting for transfers between devices: 197 us -> 141 us  [to_keepers(): back = lax.all_to_all(owned, 'dp', 0, 0, tiled=True)]
    all_gather x1, waiting for transfers between devices: 0.01 us -> 55.7 us  [on_device(): piece = lax.all_gather(mine, 'group', axis=2, tiled=True)]
    unnamed x0 -> x1, blocking collectives: none -> 39.3 us
    psum x1 -> x0, blocking collectives: 37.8 us -> none  [on_device(): adam_sq = lax.psum(adam_part, ('dp', 'group'))]
  transfers between devices with their start and end apart: 7 -> 8, of which waited for: 5 -> 6; matrix products, arithmetic and copies ran while one was open for 9% -> 10% of each run, Pallas kernels for 0% -> 0%
where the time goes in v2:
time: 768 us; the launch traced here: 762 us
  waiting for transfers between devices  378 us (49%)
  blocking collectives  234 us (30%)
  local copies, waits for them, and re-layouts  40.5 us (5%)
  matrix products  35 us (5%)
  other arithmetic  34.1 us (4%)
  starting transfers between devices  26.9 us (4%)
  between operations  13.9 us (2%)
    all_to_all x2, waiting for transfers between devices, to_owners(): lax.all_to_all(padded.reshape(n_dp, cap, rows, quarter), 'dp', 0, 0, tile...  157 us
    all_to_all x3, waiting for transfers between devices, to_keepers(): back = lax.all_to_all(owned, 'dp', 0, 0, tiled=True)  141 us
    all_gather x1, blocking collectives, on_device(): norm_grad = jnp.sum(lax.all_gather(local_norm, ('dp', 'group')), axis=0)  102 us
    all_to_all x1, blocking collectives, to_owners(): lax.all_to_all(padded.reshape(n_dp, cap, rows, quarter), 'dp', 0, 0, tile...  87.2 us
    all_gather x1, waiting for transfers between devices, on_device(): piece = lax.all_gather(mine, 'group', axis=2, tiled=True)  55.7 us
    unnamed x1, blocking collectives  39.3 us
    reduce_scatter x1, waiting for transfers between devices, on_device(): lax.psum_scatter(partials[0], 'group', scatter_dimension=2, tiled=True)  23.1 us
    dot_general x1, matrix products, on_device(): jnp.einsum('cdim,cmj->dcij', full_left4, half, preferred_element_type=jnp...  17.6 us
  transfers between devices with their start and end apart: 8, of which 6 were waited for; matrix products, arithmetic and copies ran while one was open for 10% of the time, Pallas kernels for 0%

profile of v2, /device:TPU:0, one launch (start us, length us, event | category | flops | bytes accessed | tf_op | source)
XLA Modules:
  0.0 762.4 jit_solution(13714949214837697143)
XLA Ops:
  9.2 2.2 pad.14
  11.4 7.5 all-to-all-start
  18.9 2.2 pad.15
  21.2 79.8 %all-to-all-done = bf16[8,7,128,256]{3,2,1,0:T(8,128)(2,1)} async-done(((bf16[8,7,128,256]{3,2,1,0:T(8,128)(2,1)}), bf16[8,7,128,256]{3,2,1,0:T(8,128)(2,1)}, u32[]{:S(2)}, u32[]{:S(2)}) %all-to-all-start) | async-done | bytes 3670048 | tf_op jit(solution)/shard_map/all_to_all | solution.py:33
  101.0 4.5 all-to-all-start.1
  105.5 4.3 copy.42
  109.8 77.0 %all-to-all-done.1 = bf16[8,7,128,256]{3,2,1,0:T(8,128)(2,1)} async-done(((bf16[8,7,128,256]{3,2,1,0:T(8,128)(2,1)}), bf16[8,7,128,256]{3,2,1,0:T(8,128)(2,1)}, u32[]{:S(2)}, u32[]{:S(2)}) %all-to-all-start.1) | async-done | bytes 3670048 | tf_op jit(solution)/shard_map/all_to_all | solution.py:33
  186.9 4.3 copy.43
  191.2 23.1 %reduce-scatter.2.cloned.1.call-done = f32[54,128,256]{2,1,0:T(8,128)} async-done(((f32[54,128,1024]{2,1,0:T(8,128)}), f32[54,128,256]{2,1,0:T(8,128)}) %reduce-scatter.2.cloned.1.call-update) | async-done | bytes 7077904 | tf_op jit(solution)/shard_map/reduce_scatter | solution.py:45
  214.3 11.8 %multiply_reduce_fusion.1 = (f32[54]{0:T(128)S(1)}, f32[54,128,256]{2,1,0:T(8,128)}, bf16[54,128,256]{2,1,0:T(8,128)(2,1)S(1)}) fusion(f32[54,128,256]{2,1,0:T(8,128)} %reduce-scatter.2.cloned.1.call-done, f32[54,128,256]{2,1,0:T(8,128)} %param.9), kind=kLoop, calls=%fused_computation.6 | loop fusion | flops 15925194 | bytes 24772824 | tf_op jit(solution)/shard_map/reduce_sum | solution.py:49
  226.7 87.2 %all_to_all.30 = bf16[8,7,128,256]{3,2,1,0:T(8,128)(2,1)S(1)} all-to-all(bf16[8,7,128,256]{3,2,1,0:T(8,128)(2,1)S(1)} %bitcast.46), channel_id=1, replica_groups=mesh['dp'=8,'group'=4] {'dp'}, dimensions={0} | all-to-all | bytes 7340032 | tf_op jit(solution)/shard_map/all_to_all | solution.py:33
  313.9 2.3 copy.44
  316.5 39.3 %all-reduce.4 = f32[1728]{0:T(1024)S(1)} all-reduce(f32[1728]{0:T(1024)S(1)} %dynamic-update-slice), channel_id=2, replica_groups=mesh['dp'=8,'group'=4] {'dp','group'}, use_global_device_ids=true, to_apply=%add.4 | all-reduce | flops 1728 | bytes 13824
  355.9 55.7 %all-gather.5.cloned.1.call-done = bf16[7,1024,1024]{2,1,0:T(8,128)(2,1)} async-done(((bf16[7,1024,256]{2,1,0:T(8,128)(2,1)}), bf16[7,1024,1024]{2,1,0:T(8,128)(2,1)}) %all-gather.5.cloned.1.call-update) | async-done | bytes 14680080 | tf_op jit(solution)/shard_map/all_gather | solution.py:54
  411.6 17.6 %multiply_reduce_fusion = (f32[7]{0:T(128)S(1)}, f32[7,256,8,128]{3,1,2,0:T(8,128)}) fusion(bf16[7,8,128,1024]{3,2,1,0:T(8,128)(2,1)} %bitcast.57, bf16[7,1024,1024]{2,1,0:T(8,128)(2,1)} %all-gather.5.cloned.1.call-done, bf16[7,1024,256]{2,1,0:T(8,128)(2,1)} %bitcast.54), kind=kOutput, calls=%fused_computation.2 | convolution fusion | flops 7521697792 | bytes 40370204 | tf_op jit(solution)/shard_map/cdim,cmj->dcij/dot_general | solution.py:67
  429.1 5.9 psum.7
  435.1 4.1 fusion.1
  439.2 2.3 copy.46
  441.5 5.6 all-to-all-start.3
  447.1 8.5 %convert_bitcast_fusion = bf16[8,7,128,256]{2,3,0,1:T(8,128)(2,1)S(1)} fusion(bf16[7,8,128,1024]{3,2,1,0:T(8,128)(2,1)} %bitcast.56, bf16[7,1024,1024]{2,1,0:T(8,128)(2,1)} %all-gather.5.cloned.1.call-done, s32[]{:T(128)S(6)} %select_n.7), kind=kOutput, calls=%fused_computation.13 | convolution fusion | flops 3759931392 | bytes 22020100 | tf_op jit(solution)/shard_map/cdim,cjm->dcij/dot_general | solution.py:57
  455.5 2.1 copy.48
  457.7 71.1 %all-to-all-done.3 = bf16[8,7,128,256]{2,3,1,0:T(8,128)(2,1)} async-done(((bf16[8,7,128,256]{2,3,1,0:T(8,128)(2,1)}), bf16[8,7,128,256]{2,3,1,0:T(8,128)(2,1)}, u32[]{:S(2)}, u32[]{:S(2)}) %all-to-all-start.3) | async-done | bytes 3670048 | tf_op jit(solution)/shard_map/all_to_all | solution.py:37
  528.8 4.7 all-to-all-start.4
  533.4 9.0 %convolution_convert_fusion = bf16[7,1024,256]{2,1,0:T(8,128)(2,1)S(1)} fusion(bf16[7,1024,1024]{2,1,0:T(8,128)(2,1)} %all-gather.5.cloned.1.call-done, bf16[7,1024,256]{2,1,0:T(8,128)(2,1)} %bitcast.48), kind=kOutput, calls=%fused_computation.17 | convolution fusion | flops 3759931392 | bytes 22020096 | tf_op jit(solution)/shard_map/cim,cij->cmj/dot_general | solution.py:58
  544.5 70.1 %all-to-all-done.4 = bf16[8,7,128,256]{2,3,1,0:T(8,128)(2,1)} async-done(((bf16[8,7,128,256]{2,3,1,0:T(8,128)(2,1)}), bf16[8,7,128,256]{2,3,1,0:T(8,128)(2,1)}, u32[]{:S(2)}, u32[]{:S(2)}) %all-to-all-start.4) | async-done | bytes 3670048 | tf_op jit(solution)/shard_map/all_to_all | solution.py:37
  614.6 4.5 all-to-all-start.5
  619.2 102.0 %all-gather.1 = f32[32,1,2,2048]{3,2,1,0:T(2,128)S(1)} all-gather(f32[1,1,2,2048]{3,2,1,0:T(2,128)S(1)} %copy-done.2), channel_id=3, replica_groups=mesh['dp'=8,'group'=4] {'dp','group'}, dimensions={0}, use_global_device_ids=true | all-gather | bytes 540672 | tf_op jit(solution)/shard_map/all_gather | solution.py:44
  722.0 6.2 copy.47
  728.2 4.2 slice.12
  732.4 6.2 copy.49
  738.6 8.6 %multiply_add_fusion.1 = f32[54,128,256]{2,1,0:T(8,128)} fusion(f32[54,128,256]{2,1,0:T(8,128)} %param.10, bf16[56,128,256]{2,1,0:T(8,128)(2,1)} %bitcast.53), kind=kLoop, calls=%fused_computation.5 | loop fusion | flops 7077888 | bytes 17694720 | tf_op jit(solution)/shard_map/add | solution.py:75
  747.2 8.6 %multiply_add_fusion = f32[54,128,256]{2,1,0:T(8,128)} fusion(f32[54,128,256]{2,1,0:T(8,128)} %param.11, bf16[56,128,256]{2,1,0:T(8,128)(2,1)} %bitcast.21), kind=kLoop, calls=%fused_computation.4 | loop fusion | flops 7077888 | bytes 17694720 | tf_op jit(solution)/shard_map/add | solution.py:76
  (25 shorter events, 6.0 us)
Async XLA Ops:
  7.2 207.1 %reduce-scatter.2.cloned.1.call-start = ((), (), s32[]{:S(2)}) async-start(), calls=%async_computation.7 | async-start | bytes 35389440 | tf_op jit(solution)/shard_map/reduce_scatter | solution.py:45
  7.2 2.0 copy-start
  11.4 7.5 copy-start.1
  11.4 89.6 %all-to-all-start = ((bf16[8,7,128,256]{3,2,1,0:T(8,128)(2,1)}), bf16[8,7,128,256]{3,2,1,0:T(8,128)(2,1)}, u32[]{:S(2)}, u32[]{:S(2)}) async-start(bf16[8,7,128,256]{3,2,1,0:T(8,128)(2,1)} %bitcast.45), calls=%async_computation.1 | async-start | bytes 7340032 | tf_op jit(solution)/shard_map/all_to_all | solution.py:33
  101.0 85.9 %all-to-all-start.1 = ((bf16[8,7,128,256]{3,2,1,0:T(8,128)(2,1)}), bf16[8,7,128,256]{3,2,1,0:T(8,128)(2,1)}, u32[]{:S(2)}, u32[]{:S(2)}) async-start(bf16[8,7,128,256]{3,2,1,0:T(8,128)(2,1)} %bitcast.44), calls=%async_computation.2 | async-start | bytes 7340032 | tf_op jit(solution)/shard_map/all_to_all | solution.py:33
  105.5 250.4 %all-gather.7.cloned.1.call-start = ((), (), s32[]{:S(2)}) async-start(), calls=%async_computation.9 | async-start | bytes 18350080 | tf_op jit(solution)/shard_map/all_gather | solution.py:65
  214.3 197.3 %all-gather.5.cloned.1.call-start = ((), (), s32[]{:S(2)}) async-start(), calls=%async_computation.8 | async-start | bytes 18350080 | tf_op jit(solution)/shard_map/all_gather | solution.py:54
  441.5 87.3 %all-to-all-start.3 = ((bf16[8,7,128,256]{2,3,1,0:T(8,128)(2,1)}), bf16[8,7,128,256]{2,3,1,0:T(8,128)(2,1)}, u32[]{:S(2)}, u32[]{:S(2)}) async-start(bf16[8,7,128,256]{2,3,1,0:T(8,128)(2,1)} %copy.46), calls=%async_computation.4 | async-start | bytes 7340032 | tf_op jit(solution)/shard_map/all_to_all | solution.py:37
  528.8 85.9 %all-to-all-start.4 = ((bf16[8,7,128,256]{2,3,1,0:T(8,128)(2,1)}), bf16[8,7,128,256]{2,3,1,0:T(8,128)(2,1)}, u32[]{:S(2)}, u32[]{:S(2)}) async-start(bf16[8,7,128,256]{2,3,1,0:T(8,128)(2,1)} %copy.48), calls=%async_computation.5 | async-start | bytes 7340032 | tf_op jit(solution)/shard_map/all_to_all | solution.py:37
  542.5 76.7 %copy-start.2 = (f32[1,1,2,2048]{3,2,1,0:T(2,128)S(1)}, f32[1,1,2,2048]{3,2,1,0:T(2,128)}, u32[]{:S(2)}) copy-start(f32[1,1,2,2048]{3,2,1,0:T(2,128)} %param.14) | copy-start | bytes 49156
  542.5 178.9 %copy-start.3 = (f32[2,2048]{1,0:T(2,128)S(1)}, f32[2,2048]{1,0:T(2,128)}, u32[]{:S(2)}) copy-start(f32[2,2048]{1,0:T(2,128)} %param.15) | copy-start | bytes 49156
  614.6 132.6 %all-to-all-start.5 = ((bf16[8,7,128,256]{3,2,1,0:T(8,128)(2,1)}), bf16[8,7,128,256]{3,2,1,0:T(8,128)(2,1)}, u32[]{:S(2)}, u32[]{:S(2)}) async-start(bf16[8,7,128,256]{3,2,1,0:T(8,128)(2,1)} %bitcast.50), calls=%async_computation.6 | async-start | bytes 7340032 | tf_op jit(solution)/shard_map/all_to_all | solution.py:37
Sparse Core Ops, SparseCore 0:
  10.6 203.6 reduce-scatter.1
  216.5 95.9 all-gather.6
  316.3 95.2 all-gather.4

commit v3 on v1

--- a/solution.py
+++ b/solution.py
@@ -43,6 +43,7 @@
     local_norm = norm_partials[0, 0]
     norm_grad = lax.psum(local_norm, ("dp", "group"))
     grad = lax.psum_scatter(partials[0], "group", scatter_dimension=2, tiled=True)
+    grad, left_root, right_root = lax.optimization_barrier((grad, left_root, right_root))
     new_moment = 0.99 * second_moment + 0.01 * grad * grad
     adam = grad / (jnp.sqrt(new_moment) + EPS_ADAM)
     adam_part = jnp.sum(adam * adam, axis=(1, 2))

time: 753 us -> 717 us (0.952)
  blocking collectives: 220 us -> 132 us
  waiting for transfers between devices: 392 us -> 433 us
    reduce_scatter x1, waiting for transfers between devices: 113 us -> 23.1 us  [on_device(): lax.psum_scatter(partials[0], 'group', scatter_dimension=2, tiled=True)]
    all_to_all x2 -> x1, blocking collectives: 176 us -> 87.2 us  [to_owners(): lax.all_to_all(padded.reshape(n_dp, cap, rows, quarter), 'dp', 0, 0, tile...]
    all_to_all x1 -> x2, waiting for transfers between devices: 81.1 us -> 157 us  [to_owners(): lax.all_to_all(padded.reshape(n_dp, cap, rows, quarter), 'dp', 0, 0, tile...]
    all_gather x1, waiting for transfers between devices: 0.01 us -> 55.9 us  [on_device(): piece = lax.all_gather(mine, 'group', axis=2, tiled=True)]
  transfers between devices with their start and end apart: 7 -> 8, of which waited for: 5 -> 7; matrix products, arithmetic and copies ran while one was open for 9% -> 10% of each run, Pallas kernels for 0% -> 0%
where the time goes in v3:
time: 717 us; the launch traced here: 716 us
  waiting for transfers between devices  433 us (60%)
  blocking collectives  132 us (18%)
  local copies, waits for them, and re-layouts  40.1 us (6%)
  matrix products  35 us (5%)
  other arithmetic  33.9 us (5%)
  starting transfers between devices  26.9 us (4%)
  between operations  13.9 us (2%)
    all_to_all x3, waiting for transfers between devices, to_keepers(): back = lax.all_to_all(owned, 'dp', 0, 0, tiled=True)  197 us
    all_to_all x2, waiting for transfers between devices, to_owners(): lax.all_to_all(padded.reshape(n_dp, cap, rows, quarter), 'dp', 0, 0, tile...  157 us
    all_to_all x1, blocking collectives, to_owners(): lax.all_to_all(padded.reshape(n_dp, cap, rows, quarter), 'dp', 0, 0, tile...  87.2 us
    all_gather x1, waiting for transfers between devices, on_device(): piece = lax.all_gather(mine, 'group', axis=2, tiled=True)  55.9 us
    psum x1, blocking collectives, on_device(): adam_sq = lax.psum(adam_part, ('dp', 'group'))  39.3 us
    reduce_scatter x1, waiting for transfers between devices, on_device(): lax.psum_scatter(partials[0], 'group', scatter_dimension=2, tiled=True)  23.1 us
    dot_general x1, matrix products, on_device(): jnp.einsum('cdim,cmj->dcij', full_left4, half, preferred_element_type=jnp...  17.6 us
    all_to_all x3, starting transfers between devices, to_keepers(): back = lax.all_to_all(owned, 'dp', 0, 0, tiled=True)  14.8 us
  transfers between devices with their start and end apart: 8, of which 7 were waited for; matrix products, arithmetic and copies ran while one was open for 10% of the time, Pallas kernels for 0%

profile of v3, /device:TPU:0, one launch (start us, length us, event | category | flops | bytes accessed | tf_op | source)
XLA Modules:
  0.0 715.6 jit_solution(10480204326388501611)
XLA Ops:
  9.2 2.2 pad.14
  11.4 7.5 %all-to-all-start = ((bf16[8,7,128,256]{3,2,1,0:T(8,128)(2,1)}), bf16[8,7,128,256]{3,2,1,0:T(8,128)(2,1)}, u32[]{:S(2)}, u32[]{:S(2)}) async-start(bf16[8,7,128,256]{3,2,1,0:T(8,128)(2,1)} %bitcast.46), calls=%async_computation.1 | async-start | bytes 7340032 | tf_op jit(solution)/shard_map/all_to_all | solution.py:33
  18.9 2.2 pad.15
  21.2 79.8 %all-to-all-done = bf16[8,7,128,256]{3,2,1,0:T(8,128)(2,1)} async-done(((bf16[8,7,128,256]{3,2,1,0:T(8,128)(2,1)}), bf16[8,7,128,256]{3,2,1,0:T(8,128)(2,1)}, u32[]{:S(2)}, u32[]{:S(2)}) %all-to-all-start) | async-done | bytes 3670048 | tf_op jit(solution)/shard_map/all_to_all | solution.py:33
  101.0 4.5 all-to-all-start.1
  105.5 4.3 copy.32
  109.8 77.0 %all-to-all-done.1 = bf16[8,7,128,256]{3,2,1,0:T(8,128)(2,1)} async-done(((bf16[8,7,128,256]{3,2,1,0:T(8,128)(2,1)}), bf16[8,7,128,256]{3,2,1,0:T(8,128)(2,1)}, u32[]{:S(2)}, u32[]{:S(2)}) %all-to-all-start.1) | async-done | bytes 3670048 | tf_op jit(solution)/shard_map/all_to_all | solution.py:33
  186.9 4.3 copy.33
  191.1 23.1 %reduce-scatter.2.cloned.1.call-done = f32[54,128,256]{2,1,0:T(8,128)} async-done(((f32[54,128,1024]{2,1,0:T(8,128)}), f32[54,128,256]{2,1,0:T(8,128)}) %reduce-scatter.2.cloned.1.call-update) | async-done | bytes 7077904 | tf_op jit(solution)/shard_map/reduce_scatter | solution.py:45
  214.3 11.8 %multiply_reduce_fusion.1 = (f32[54]{0:T(128)S(1)}, f32[54,128,256]{2,1,0:T(8,128)}, bf16[54,128,256]{2,1,0:T(8,128)(2,1)S(1)}) fusion(f32[54,128,256]{2,1,0:T(8,128)} %reduce-scatter.2.cloned.1.call-done, f32[54,128,256]{2,1,0:T(8,128)} %param.9), kind=kLoop, calls=%fused_computation.6 | loop fusion | flops 15925194 | bytes 24772824 | tf_op jit(solution)/shard_map/reduce_sum | solution.py:49
  226.7 87.2 %all_to_all.30 = bf16[8,7,128,256]{3,2,1,0:T(8,128)(2,1)S(1)} all-to-all(bf16[8,7,128,256]{3,2,1,0:T(8,128)(2,1)S(1)} %bitcast.47), channel_id=1, replica_groups=mesh['dp'=8,'group'=4] {'dp'}, dimensions={0} | all-to-all | bytes 7340032 | tf_op jit(solution)/shard_map/all_to_all | solution.py:33
  313.9 2.3 copy.34
  316.2 39.3 %all-reduce.4 = (f32[54]{0:T(128)S(1)}, f32[2,2048]{1,0:T(2,128)S(1)}) all-reduce(f32[54]{0:T(128)S(1)} %get-tuple-element.16, f32[2,2048]{1,0:T(2,128)S(1)} %bitcast.57), channel_id=1, replica_groups=mesh['dp'=8,'group'=4] {'dp','group'}, use_global_device_ids=true, to_apply=%region_2.3 | all-reduce | flops 4150 | bytes 33200 | tf_op jit(solution)/shard_map/psum | solution.py:50
  355.6 55.9 %all-gather.3.cloned.1.call-done = bf16[7,1024,1024]{2,1,0:T(8,128)(2,1)} async-done(((bf16[7,1024,256]{2,1,0:T(8,128)(2,1)}), bf16[7,1024,1024]{2,1,0:T(8,128)(2,1)}) %all-gather.3.cloned.1.call-update) | async-done | bytes 14680080 | tf_op jit(solution)/shard_map/all_gather | solution.py:54
  411.5 17.6 %multiply_reduce_fusion = (f32[7]{0:T(128)S(1)}, f32[7,256,8,128]{3,1,2,0:T(8,128)}) fusion(bf16[7,8,128,1024]{3,2,1,0:T(8,128)(2,1)} %bitcast.59, bf16[7,1024,1024]{2,1,0:T(8,128)(2,1)} %all-gather.3.cloned.1.call-done, bf16[7,1024,256]{2,1,0:T(8,128)(2,1)} %bitcast.55), kind=kOutput, calls=%fused_computation.2 | convolution fusion | flops 7521697792 | bytes 40370204 | tf_op jit(solution)/shard_map/cdim,cmj->dcij/dot_general | solution.py:67
  429.1 5.9 psum.22
  435.0 4.1 fusion.1
  439.1 2.3 copy.36
  441.4 5.7 all-to-all-start.3
  447.1 8.5 %convert_bitcast_fusion = bf16[8,7,128,256]{2,3,0,1:T(8,128)(2,1)S(1)} fusion(bf16[7,8,128,1024]{3,2,1,0:T(8,128)(2,1)} %bitcast.58, bf16[7,1024,1024]{2,1,0:T(8,128)(2,1)} %all-gather.3.cloned.1.call-done, s32[]{:T(128)S(6)} %select_n.7), kind=kOutput, calls=%fused_computation.13 | convolution fusion | flops 3759931392 | bytes 22020100 | tf_op jit(solution)/shard_map/cdim,cjm->dcij/dot_general | solution.py:57
  455.5 2.1 copy.38
  457.6 71.1 %all-to-all-done.3 = bf16[8,7,128,256]{2,3,1,0:T(8,128)(2,1)} async-done(((bf16[8,7,128,256]{2,3,1,0:T(8,128)(2,1)}), bf16[8,7,128,256]{2,3,1,0:T(8,128)(2,1)}, u32[]{:S(2)}, u32[]{:S(2)}) %all-to-all-start.3) | async-done | bytes 3670048 | tf_op jit(solution)/shard_map/all_to_all | solution.py:37
  528.7 4.7 all-to-all-start.4
  533.4 9.0 %convolution_convert_fusion = bf16[7,1024,256]{2,1,0:T(8,128)(2,1)S(1)} fusion(bf16[7,1024,1024]{2,1,0:T(8,128)(2,1)} %all-gather.3.cloned.1.call-done, bf16[7,1024,256]{2,1,0:T(8,128)(2,1)} %bitcast.49), kind=kOutput, calls=%fused_computation.17 | convolution fusion | flops 3759931392 | bytes 22020096 | tf_op jit(solution)/shard_map/cim,cij->cmj/dot_general | solution.py:58
  544.5 70.2 %all-to-all-done.4 = bf16[8,7,128,256]{2,3,1,0:T(8,128)(2,1)} async-done(((bf16[8,7,128,256]{2,3,1,0:T(8,128)(2,1)}), bf16[8,7,128,256]{2,3,1,0:T(8,128)(2,1)}, u32[]{:S(2)}, u32[]{:S(2)}) %all-to-all-start.4) | async-done | bytes 3670048 | tf_op jit(solution)/shard_map/all_to_all | solution.py:37
  614.7 4.5 all-to-all-start.5
  619.9 6.2 copy.37
  626.1 4.2 slice.12
  630.3 6.2 copy.39
  636.4 8.6 %multiply_add_fusion.1 = f32[54,128,256]{2,1,0:T(8,128)} fusion(f32[54,128,256]{2,1,0:T(8,128)} %param.10, bf16[56,128,256]{2,1,0:T(8,128)(2,1)} %bitcast.54), kind=kLoop, calls=%fused_computation.5 | loop fusion | flops 7077888 | bytes 17694720 | tf_op jit(solution)/shard_map/add | solution.py:75
  645.1 55.4 %all-to-all-done.5 = bf16[8,7,128,256]{3,2,1,0:T(8,128)(2,1)} async-done(((bf16[8,7,128,256]{3,2,1,0:T(8,128)(2,1)}), bf16[8,7,128,256]{3,2,1,0:T(8,128)(2,1)}, u32[]{:S(2)}, u32[]{:S(2)}) %all-to-all-start.5) | async-done | bytes 3670048 | tf_op jit(solution)/shard_map/all_to_all | solution.py:37
  700.5 8.6 %multiply_add_fusion = f32[54,128,256]{2,1,0:T(8,128)} fusion(f32[54,128,256]{2,1,0:T(8,128)} %param.11, bf16[56,128,256]{2,1,0:T(8,128)(2,1)} %bitcast.21), kind=kLoop, calls=%fused_computation.4 | loop fusion | flops 7077888 | bytes 17694720 | tf_op jit(solution)/shard_map/add | solution.py:76
  (19 shorter events, 5.4 us)
Async XLA Ops:
  7.2 207.1 %reduce-scatter.2.cloned.1.call-start = ((), (), s32[]{:S(2)}) async-start(), calls=%async_computation.7 | async-start | bytes 35389440 | tf_op jit(solution)/shard_map/reduce_scatter | solution.py:45
  7.2 2.0 copy-start
  11.4 7.5 %copy-start.1 = (bf16[54,128,256]{2,1,0:T(8,128)(2,1)S(1)}, bf16[54,128,256]{2,1,0:T(8,128)(2,1)}, u32[]{:S(2)}) copy-start(bf16[54,128,256]{2,1,0:T(8,128)(2,1)} %param.13) | copy-start | bytes 10616836
  11.4 89.6 %all-to-all-start = ((bf16[8,7,128,256]{3,2,1,0:T(8,128)(2,1)}), bf16[8,7,128,256]{3,2,1,0:T(8,128)(2,1)}, u32[]{:S(2)}, u32[]{:S(2)}) async-start(bf16[8,7,128,256]{3,2,1,0:T(8,128)(2,1)} %bitcast.46), calls=%async_computation.1 | async-start | bytes 7340032 | tf_op jit(solution)/shard_map/all_to_all | solution.py:33
  101.0 85.9 %all-to-all-start.1 = ((bf16[8,7,128,256]{3,2,1,0:T(8,128)(2,1)}), bf16[8,7,128,256]{3,2,1,0:T(8,128)(2,1)}, u32[]{:S(2)}, u32[]{:S(2)}) async-start(bf16[8,7,128,256]{3,2,1,0:T(8,128)(2,1)} %bitcast.45), calls=%async_computation.2 | async-start | bytes 7340032 | tf_op jit(solution)/shard_map/all_to_all | solution.py:33
  105.5 250.1 %all-gather.5.cloned.1.call-start = ((), (), s32[]{:S(2)}) async-start(), calls=%async_computation.9 | async-start | bytes 18350080 | tf_op jit(solution)/shard_map/all_gather | solution.py:65
  214.3 197.2 %all-gather.3.cloned.1.call-start = ((), (), s32[]{:S(2)}) async-start(), calls=%async_computation.8 | async-start | bytes 18350080 | tf_op jit(solution)/shard_map/all_gather | solution.py:54
  313.9 2.3 copy-start.2
  441.4 87.3 %all-to-all-start.3 = ((bf16[8,7,128,256]{2,3,1,0:T(8,128)(2,1)}), bf16[8,7,128,256]{2,3,1,0:T(8,128)(2,1)}, u32[]{:S(2)}, u32[]{:S(2)}) async-start(bf16[8,7,128,256]{2,3,1,0:T(8,128)(2,1)} %copy.36), calls=%async_computation.4 | async-start | bytes 7340032 | tf_op jit(solution)/shard_map/all_to_all | solution.py:37
  528.7 86.0 %all-to-all-start.4 = ((bf16[8,7,128,256]{2,3,1,0:T(8,128)(2,1)}), bf16[8,7,128,256]{2,3,1,0:T(8,128)(2,1)}, u32[]{:S(2)}, u32[]{:S(2)}) async-start(bf16[8,7,128,256]{2,3,1,0:T(8,128)(2,1)} %copy.38), calls=%async_computation.5 | async-start | bytes 7340032 | tf_op jit(solution)/shard_map/all_to_all | solution.py:37
  542.4 76.8 %copy-start.3 = (f32[2,2048]{1,0:T(2,128)S(1)}, f32[2,2048]{1,0:T(2,128)}, u32[]{:S(2)}) copy-start(f32[2,2048]{1,0:T(2,128)} %param.15) | copy-start | bytes 49156
  614.7 85.8 %all-to-all-start.5 = ((bf16[8,7,128,256]{3,2,1,0:T(8,128)(2,1)}), bf16[8,7,128,256]{3,2,1,0:T(8,128)(2,1)}, u32[]{:S(2)}, u32[]{:S(2)}) async-start(bf16[8,7,128,256]{3,2,1,0:T(8,128)(2,1)} %bitcast.51), calls=%async_computation.6 | async-start | bytes 7340032 | tf_op jit(solution)/shard_map/all_to_all | solution.py:37
Sparse Core Ops, SparseCore 0:
  10.6 203.6 reduce-scatter.1
  216.5 95.9 all-gather.4
  316.3 95.1 all-gather.2

commit v4 on v1

v4 whole, which is shorter than its diff:
```python
import jax
import jax.numpy as jnp
from jax import lax
from jax.sharding import PartitionSpec as P

EPS_ADAM = 1e-08
EPS_GRAFT = 1e-06


def on_device(
    partials,
    second_moment,
    left_stats,
    right_stats,
    left_roots,
    right_roots,
    norm_partials,
    norm_moment,
):
    n_dp = lax.axis_size("dp")
    me_dp = lax.axis_index("dp")
    me_group = lax.axis_index("group")
    count = second_moment.shape[0]
    rows = partials.shape[2]
    quarter = second_moment.shape[2]
    width = rows * n_dp
    cap = -(-count // n_dp)
    slots = cap * n_dp
    lower = me_group * quarter
    split = (cap + 1) // 2
    bounds = [(0, split), (split, cap)] if cap > 1 else [(0, cap)]

    def to_owners(blocks, n_slots):
        padded = jnp.pad(blocks, ((0, n_slots * n_dp - blocks.shape[0]), (0, 0), (0, 0)))
        sent = lax.all_to_all(padded.reshape(n_slots, n_dp, rows, quarter), "dp", 1, 1, tiled=True)
        return sent.reshape(n_slots, width, quarter)

    def to_keepers(owned):
        n_slots = owned.shape[0]
        back = lax.all_to_all(owned.reshape(n_slots, n_dp, rows, quarter), "dp", 1, 1, tiled=True)
        return back.reshape(n_slots * n_dp, rows, quarter)

    left_root = to_owners(left_roots, cap)
    right_root = to_owners(right_roots, cap)
    local_norm = norm_partials[0, 0]

    moments, adam_parts, left_terms, right_terms, pieces = [], [], [], [], []
    for index, (s0, s1) in enumerate(bounds):
        b0, b1 = s0 * n_dp, min(s1 * n_dp, count)
        grad = lax.psum_scatter(partials[0, b0:b1], "group", scatter_dimension=2, tiled=True)
        if index == 0:
            grad, left_root, right_root = lax.optimization_barrier((grad, left_root, right_root))
        new_moment = 0.99 * second_moment[b0:b1] + 0.01 * grad * grad
        adam = grad / (jnp.sqrt(new_moment) + EPS_ADAM)
        adam_parts.append(jnp.sum(adam * adam, axis=(1, 2)))
        moments.append(new_moment)
        mine = to_owners(grad.astype(jnp.bfloat16), s1 - s0)
        piece = lax.all_gather(mine, "group", axis=2, tiled=True)
        own_rows = lax.dynamic_slice_in_dim(piece, lower, quarter, 1)
        gram_left = jnp.einsum("cim,cjm->cij", piece, own_rows, preferred_element_type=jnp.float32)
        gram_right = jnp.einsum("cim,cij->cmj", piece, mine, preferred_element_type=jnp.float32)
        left_terms.append(to_keepers(gram_left.astype(jnp.bfloat16))[: b1 - b0])
        right_terms.append(to_keepers(gram_right.astype(jnp.bfloat16))[: b1 - b0])
        pieces.append(piece)

    norm_grad, adam_sq = lax.psum((local_norm, jnp.concatenate(adam_parts)), ("dp", "group"))
    piece = jnp.concatenate(pieces) if len(pieces) > 1 else pieces[0]
    half = jnp.einsum("cim,cmj->cij", piece, right_root, preferred_element_type=jnp.float32)
    half = half.astype(jnp.bfloat16)
    full_left = lax.all_gather(left_root, "group", axis=2, tiled=True)
    direction = jnp.einsum("cim,cmj->cij", full_left, half, preferred_element_type=jnp.float32)
    direction_sq = lax.psum(jnp.sum(direction * direction, axis=(1, 2)), "group")
    adam_pad = jnp.pad(adam_sq, (0, slots - count)).reshape(cap, n_dp)
    adam_owned = lax.dynamic_slice_in_dim(adam_pad, me_dp, 1, 1)[:, 0]
    ratio = jnp.sqrt(adam_owned / (direction_sq + EPS_GRAFT))
    scaled = (ratio[:, None, None] * direction).astype(jnp.bfloat16)
    block_step = to_keepers(scaled)[:count]

    new_moment = jnp.concatenate(moments)
    left_term = jnp.concatenate(left_terms).astype(jnp.float32)
    right_term = jnp.concatenate(right_terms).astype(jnp.float32)
    new_left = 0.95 * left_stats + 0.05 * left_term
    new_right = 0.95 * right_stats + 0.05 * right_term
    new_norm_moment = 0.99 * norm_moment + 0.01 * norm_grad * norm_grad
    norm_step = norm_grad / (jnp.sqrt(new_norm_moment) + EPS_ADAM)
    return (block_step, new_moment, new_left, new_right, norm_step, new_norm_moment)


def solution(mesh):
    return jax.shard_map(
        on_device,
        mesh=mesh,
        in_specs=(
            P("group", None, "dp", None),
            P(None, "dp", "group"),
            P(None, "dp", "group"),
            P(None, "dp", "group"),
            P(None, "dp", "group"),
            P(None, "dp", "group"),
            P("dp", "group", None, None),
            P(),
        ),
        out_specs=(
            P(None, "dp", "group"),
            P(None, "dp", "group"),
            P(None, "dp", "group"),
            P(None, "dp", "group"),
            P(),
            P(),
        ),
        check_vma=False,
    )
```

time: 753 us -> 662 us (0.88)
  blocking collectives: 220 us -> 127 us
  waiting for transfers between devices: 392 us -> 338 us
  local copies, waits for them, and re-layouts: 37.2 us -> 71.5 us
  starting transfers between devices: 19.8 us -> 38.5 us
    all_to_all x2 -> x1, blocking collectives: 176 us -> 52.2 us  [to_owners(): lax.all_to_all(padded.reshape(n_slots, n_dp, rows, quarter), 'dp', 1, 1,...]
    reduce_scatter x1 -> x2, waiting for transfers between devices: 113 us -> 68.5 us  [on_device(): lax.psum_scatter(partials[0, b0:b1], 'group', scatter_dimension=2, tiled=...]
    psum x2, blocking collectives: 43.7 us -> 74.5 us  [the longest x1 68 us: on_device(): lax.psum((local_norm, jnp.concatenate(adam_parts)), ('dp', 'group'))]
    squeeze x0 -> x2, local copies, waits for them, and re-layouts: none -> 24.6 us  [on_device(): partials[0, b0:b1]]
    all_to_all x4 -> x8, starting transfers between devices: 19.6 us -> 38.3 us  [the longest x5 22.4 us: to_keepers(): lax.all_to_all(owned.reshape(n_slots, n_dp, rows, quarter), 'dp', 1, 1, t...]
    all_to_all x4 -> x8, waiting for transfers between devices: 278 us -> 261 us  [the longest x5 150 us: to_keepers(): lax.all_to_all(owned.reshape(n_slots, n_dp, rows, quarter), 'dp', 1, 1, t...]
    reshape x0 -> x10, local copies, waits for them, and re-layouts: none -> 14.7 us  [the longest x5 7.85 us: to_keepers(): owned.reshape(n_slots, n_dp, rows, quarter)]
    add x0 -> x2, other arithmetic: none -> 13 us  [on_device(): new_moment = 0.99 * second_moment[b0:b1] + 0.01 * grad * grad]
  transfers between devices with their start and end apart: 7 -> 13, of which waited for: 5 -> 9; matrix products, arithmetic and copies ran while one was open for 9% -> 19% of each run, Pallas kernels for 0% -> 0%
where the time goes in v4:
time: 662 us; the launch traced here: 661 us
  waiting for transfers between devices  338 us (51%)
  blocking collectives  127 us (19%)
  local copies, waits for them, and re-layouts  71.5 us (11%)
  matrix products  41.7 us (6%)
  starting transfers between devices  38.5 us (6%)
  other arithmetic  30.5 us (5%)
  between operations  14.1 us (2%)
    all_to_all x5, waiting for transfers between devices, to_keepers(): lax.all_to_all(owned.reshape(n_slots, n_dp, rows, quarter), 'dp', 1, 1, t...  150 us
    all_to_all x3, waiting for transfers between devices, to_owners(): lax.all_to_all(padded.reshape(n_slots, n_dp, rows, quarter), 'dp', 1, 1,...  111 us
    reduce_scatter x2, waiting for transfers between devices, on_device(): lax.psum_scatter(partials[0, b0:b1], 'group', scatter_dimension=2, tiled=...  68.5 us
    psum x1, blocking collectives, on_device(): lax.psum((local_norm, jnp.concatenate(adam_parts)), ('dp', 'group'))  68 us
    all_to_all x1, blocking collectives, to_owners(): lax.all_to_all(padded.reshape(n_slots, n_dp, rows, quarter), 'dp', 1, 1,...  52.2 us
    squeeze x2, local copies, waits for them, and re-layouts, on_device(): partials[0, b0:b1]  24.6 us
    all_to_all x5, starting transfers between devices, to_keepers(): lax.all_to_all(owned.reshape(n_slots, n_dp, rows, quarter), 'dp', 1, 1, t...  22.4 us
    dot_general x1, matrix products, on_device(): jnp.einsum('cim,cmj->cij', full_left, half, preferred_element_type=jnp.fl...  17.7 us
  transfers between devices with their start and end apart: 13, of which 9 were waited for; matrix products, arithmetic and copies ran while one was open for 19% of the time, Pallas kernels for 0%

profile of v4, /device:TPU:0, one launch (start us, length us, event | category | flops | bytes accessed | tf_op | source)
XLA Modules:
  0.0 660.7 jit_solution(12238571513643996081)
XLA Ops:
  7.2 10.9 %slice_bitcast_fusion.1 = f32[22,128,1024]{2,1,0:T(8,128)} fusion(f32[1,54,128,1024]{3,2,1,0:T(8,128)} %param.8), kind=kLoop, calls=%fused_computation.5 | loop fusion | bytes 23068672 | tf_op jit(solution)/shard_map/squeeze | solution.py:50
  18.2 13.7 %slice_bitcast_fusion = f32[32,128,1024]{2,1,0:T(8,128)} fusion(f32[1,54,128,1024]{3,2,1,0:T(8,128)} %param.8), kind=kLoop, calls=%fused_computation | loop fusion | bytes 33554432 | tf_op jit(solution)/shard_map/squeeze | solution.py:50
  37.7 7.0 %all-to-all-start = ((bf16[7,8,128,256]{3,2,0,1:T(8,128)(2,1)}), bf16[7,8,128,256]{3,2,0,1:T(8,128)(2,1)}, u32[]{:S(2)}, u32[]{:S(2)}) async-start(bf16[7,8,128,256]{3,2,0,1:T(8,128)(2,1)} %copy.28), calls=%async_computation.1 | async-start | bytes 7340032 | tf_op jit(solution)/shard_map/all_to_all | solution.py:35
  44.7 68.5 %reduce-scatter.5.cloned.1.call-done = f32[22,128,256]{2,1,0:T(8,128)} async-done(((f32[22,128,1024]{2,1,0:T(8,128)}), f32[22,128,256]{2,1,0:T(8,128)}) %reduce-scatter.5.cloned.1.call-update) | async-done | bytes 2883600 | tf_op jit(solution)/shard_map/reduce_scatter | solution.py:50
  113.2 5.3 fusion.11
  120.0 6.6 all-to-all-done
  126.5 4.3 all-to-all-start.3
  136.8 30.7 %all-to-all-done.3 = bf16[3,8,128,256]{3,2,0,1:T(8,128)(2,1)} async-done(((bf16[3,8,128,256]{3,2,0,1:T(8,128)(2,1)}), bf16[3,8,128,256]{3,2,0,1:T(8,128)(2,1)}, u32[]{:S(2)}, u32[]{:S(2)}) %all-to-all-start.3) | async-done | bytes 1572896 | tf_op jit(solution)/shard_map/all_to_all | solution.py:35
  167.5 4.5 all-to-all-start.1
  174.9 4.3 copy.29
  179.2 74.2 %all-to-all-done.1 = bf16[7,8,128,256]{3,2,0,1:T(8,128)(2,1)} async-done(((bf16[7,8,128,256]{3,2,0,1:T(8,128)(2,1)}), bf16[7,8,128,256]{3,2,0,1:T(8,128)(2,1)}, u32[]{:S(2)}, u32[]{:S(2)}) %all-to-all-start.1) | async-done | bytes 3670048 | tf_op jit(solution)/shard_map/all_to_all | solution.py:35
  253.4 4.5 copy.31
  257.8 7.6 %fusion.4 = (f32[32,128,256]{2,1,0:T(8,128)}, f32[32]{0:T(128)S(1)}, bf16[32,128,256]{2,1,0:T(8,128)(2,1)S(1)}) fusion(f32[32,128,256]{2,1,0:T(8,128)} %reduce-scatter.3.cloned.1.call-done, f32[54,128,256]{2,1,0:T(8,128)} %param.9), kind=kLoop, calls=%fused_computation.13 | loop fusion | flops 9437152 | bytes 14680192 | tf_op jit(solution)/shard_map/add | solution.py:53
  265.7 52.2 %all_to_all.45 = bf16[4,8,128,256]{3,2,0,1:T(8,128)(2,1)S(1)} all-to-all(bf16[4,8,128,256]{3,2,0,1:T(8,128)(2,1)S(1)} %copy.32), channel_id=1, replica_groups=mesh['dp'=8,'group'=4] {'dp'}, dimensions={1} | all-to-all | bytes 4194304 | tf_op jit(solution)/shard_map/all_to_all | solution.py:35
  320.0 5.1 convolution_convert_fusion.2
  326.3 4.5 all-to-all-start.6
  330.8 5.7 convolution_convert_fusion.1
  337.8 28.9 %all-to-all-done.6 = bf16[3,8,128,256]{3,2,0,1:T(8,128)(2,1)} async-done(((bf16[3,8,128,256]{3,2,0,1:T(8,128)(2,1)}), bf16[3,8,128,256]{3,2,0,1:T(8,128)(2,1)}, u32[]{:S(2)}, u32[]{:S(2)}) %all-to-all-start.6) | async-done | bytes 1572896 | tf_op jit(solution)/shard_map/all_to_all | solution.py:40
  366.7 4.3 all-to-all-start.8
  371.0 7.1 %all-gather.6.cloned.1.call-done = bf16[4,1024,1024]{2,1,0:T(8,128)(2,1)} async-done(((bf16[4,1024,256]{2,1,0:T(8,128)(2,1)}), bf16[4,1024,1024]{2,1,0:T(8,128)(2,1)}) %all-gather.6.cloned.1.call-update) | async-done | bytes 8388624 | tf_op jit(solution)/shard_map/all_gather | solution.py:58
  378.1 6.3 fusion.14
  385.9 21.5 %all-to-all-done.8 = bf16[3,8,128,256]{3,2,0,1:T(8,128)(2,1)} async-done(((bf16[3,8,128,256]{3,2,0,1:T(8,128)(2,1)}), bf16[3,8,128,256]{3,2,0,1:T(8,128)(2,1)}, u32[]{:S(2)}, u32[]{:S(2)}) %all-to-all-start.8) | async-done | bytes 1572896 | tf_op jit(solution)/shard_map/all_to_all | solution.py:40
  407.5 4.3 all-to-all-start.5
  411.8 6.9 %convolution_convert_fusion = bf16[4,1024,256]{2,1,0:T(8,128)(2,1)S(1)} fusion(bf16[4,1024,1024]{2,1,0:T(8,128)(2,1)} %all-gather.6.cloned.1.call-done, bf16[4,1024,256]{2,1,0:T(8,128)(2,1)} %bitcast.39), kind=kOutput, calls=%fused_computation.22 | convolution fusion | flops 2148532224 | bytes 12582912 | tf_op jit(solution)/shard_map/cim,cij->cmj/dot_general | solution.py:61
  420.2 39.4 %all-to-all-done.5 = bf16[4,8,128,256]{3,2,0,1:T(8,128)(2,1)} async-done(((bf16[4,8,128,256]{3,2,0,1:T(8,128)(2,1)}), bf16[4,8,128,256]{3,2,0,1:T(8,128)(2,1)}, u32[]{:S(2)}, u32[]{:S(2)}) %all-to-all-start.5) | async-done | bytes 2097184 | tf_op jit(solution)/shard_map/all_to_all | solution.py:40
  459.6 4.4 all-to-all-start.7
  464.1 68.0 %all-reduce.4 = (f32[54]{0:T(128)S(1)}, f32[2,2048]{1,0:T(2,128)S(1)}) all-reduce(f32[54]{0:T(128)S(1)} %pad_maximum_fusion.1, f32[2,2048]{1,0:T(2,128)S(1)} %bitcast.55), channel_id=1, replica_groups=mesh['dp'=8,'group'=4] {'dp','group'}, use_global_device_ids=true, to_apply=%region_4.5 | all-reduce | flops 4150 | bytes 33200 | tf_op jit(solution)/shard_map/psum | solution.py:66
  532.4 17.7 %multiply_reduce_fusion = (f32[7]{0:T(128)S(1)}, f32[7,1024,256]{2,1,0:T(8,128)}) fusion(bf16[7,1024,1024]{2,1,0:T(8,128)(2,1)} %all-gather.4.cloned.1.call-done, bf16[7,1024,256]{2,1,0:T(8,128)(2,1)} %bitcast.50, bf16[3,1024,1024]{2,1,0:T(8,128)(2,1)} %all-gather.8.cloned.1.call-done, bf16[4,1024,1024]{2,1,0:T(8,128)(2,1)} %all-gather.6.cloned.1.call-done), kind=kOutput, calls=%fused_computation.7 | convolution fusion | flops 7529037824 | bytes 40370204 | tf_op jit(solution)/shard_map/cim,cmj->cij/dot_general | solution.py:71
  550.1 6.6 psum.22
  562.8 4.9 all-to-all-start.4
  567.7 5.8 pad_maximum_fusion
  589.3 60.2 %all-to-all-done.4 = bf16[7,8,128,256]{3,2,0,1:T(8,128)(2,1)} async-done(((bf16[7,8,128,256]{3,2,0,1:T(8,128)(2,1)}), bf16[7,8,128,256]{3,2,0,1:T(8,128)(2,1)}, u32[]{:S(2)}, u32[]{:S(2)}) %all-to-all-start.4) | async-done | bytes 3670048 | tf_op jit(solution)/shard_map/all_to_all | solution.py:40
  (61 shorter events, 50.7 us)
Async XLA Ops:
  7.2 106.0 %reduce-scatter.5.cloned.1.call-start = ((), (), s32[]{:S(2)}) async-start(), calls=%async_computation.12 | async-start | bytes 14417920 | tf_op jit(solution)/shard_map/reduce_scatter | solution.py:50
  18.2 239.7 %reduce-scatter.3.cloned.1.call-start = ((), (), s32[]{:S(2)}) async-start(), calls=%async_computation.11 | async-start | bytes 20971520 | tf_op jit(solution)/shard_map/reduce_scatter | solution.py:50
  31.9 2.8 copy-start
  37.7 88.8 %all-to-all-start = ((bf16[7,8,128,256]{3,2,0,1:T(8,128)(2,1)}), bf16[7,8,128,256]{3,2,0,1:T(8,128)(2,1)}, u32[]{:S(2)}, u32[]{:S(2)}) async-start(bf16[7,8,128,256]{3,2,0,1:T(8,128)(2,1)} %copy.28), calls=%async_computation.1 | async-start | bytes 7340032 | tf_op jit(solution)/shard_map/all_to_all | solution.py:35
  126.5 40.9 %all-to-all-start.3 = ((bf16[3,8,128,256]{3,2,0,1:T(8,128)(2,1)}), bf16[3,8,128,256]{3,2,0,1:T(8,128)(2,1)}, u32[]{:S(2)}, u32[]{:S(2)}) async-start(bf16[3,8,128,256]{3,2,0,1:T(8,128)(2,1)} %copy.34), calls=%async_computation.5 | async-start | bytes 3145728 | tf_op jit(solution)/shard_map/all_to_all | solution.py:35
  167.5 85.9 %all-to-all-start.1 = ((bf16[7,8,128,256]{3,2,0,1:T(8,128)(2,1)}), bf16[7,8,128,256]{3,2,0,1:T(8,128)(2,1)}, u32[]{:S(2)}, u32[]{:S(2)}) async-start(bf16[7,8,128,256]{3,2,0,1:T(8,128)(2,1)} %copy.30), calls=%async_computation.2 | async-start | bytes 7340032 | tf_op jit(solution)/shard_map/all_to_all | solution.py:35
  172.0 147.9 %all-gather.8.cloned.1.call-start = ((), (), s32[]{:S(2)}) async-start(), calls=%async_computation.15 | async-start | bytes 7864320 | tf_op jit(solution)/shard_map/all_gather | solution.py:58
  174.8 203.2 %all-gather.6.cloned.1.call-start = ((), (), s32[]{:S(2)}) async-start(), calls=%async_computation.14 | async-start | bytes 10485760 | tf_op jit(solution)/shard_map/all_gather | solution.py:58
  319.4 213.0 %all-gather.4.cloned.1.call-start = ((), (), s32[]{:S(2)}) async-start(), calls=%async_computation.13 | async-start | bytes 18350080 | tf_op jit(solution)/shard_map/all_gather | solution.py:70
  326.3 40.4 %all-to-all-start.6 = ((bf16[3,8,128,256]{3,2,0,1:T(8,128)(2,1)}), bf16[3,8,128,256]{3,2,0,1:T(8,128)(2,1)}, u32[]{:S(2)}, u32[]{:S(2)}) async-start(bf16[3,8,128,256]{3,2,0,1:T(8,128)(2,1)} %copy.40), calls=%async_computation.8 | async-start | bytes 3145728 | tf_op jit(solution)/shard_map/all_to_all | solution.py:40
  366.7 40.8 %all-to-all-start.8 = ((bf16[3,8,128,256]{3,2,0,1:T(8,128)(2,1)}), bf16[3,8,128,256]{3,2,0,1:T(8,128)(2,1)}, u32[]{:S(2)}, u32[]{:S(2)}) async-start(bf16[3,8,128,256]{3,2,0,1:T(8,128)(2,1)} %copy.46), calls=%async_computation.10 | async-start | bytes 3145728 | tf_op jit(solution)/shard_map/all_to_all | solution.py:40
  407.5 52.2 %all-to-all-start.5 = ((bf16[4,8,128,256]{3,2,0,1:T(8,128)(2,1)}), bf16[4,8,128,256]{3,2,0,1:T(8,128)(2,1)}, u32[]{:S(2)}, u32[]{:S(2)}) async-start(bf16[4,8,128,256]{3,2,0,1:T(8,128)(2,1)} %copy.38), calls=%async_computation.7 | async-start | bytes 4194304 | tf_op jit(solution)/shard_map/all_to_all | solution.py:40
  418.8 45.3 %copy-start.1 = (f32[1,1,2,2048]{3,2,1,0:T(2,128)S(1)}, f32[1,1,2,2048]{3,2,1,0:T(2,128)}, u32[]{:S(2)}) copy-start(f32[1,1,2,2048]{3,2,1,0:T(2,128)} %param.14) | copy-start | bytes 49156
  459.6 103.1 %all-to-all-start.7 = ((bf16[4,8,128,256]{3,2,0,1:T(8,128)(2,1)}), bf16[4,8,128,256]{3,2,0,1:T(8,128)(2,1)}, u32[]{:S(2)}, u32[]{:S(2)}) async-start(bf16[4,8,128,256]{3,2,0,1:T(8,128)(2,1)} %copy.43), calls=%async_computation.9 | async-start | bytes 4194304 | tf_op jit(solution)/shard_map/all_to_all | solution.py:40
  562.8 86.7 %all-to-all-start.4 = ((bf16[7,8,128,256]{3,2,0,1:T(8,128)(2,1)}), bf16[7,8,128,256]{3,2,0,1:T(8,128)(2,1)}, u32[]{:S(2)}, u32[]{:S(2)}) async-start(bf16[7,8,128,256]{3,2,0,1:T(8,128)(2,1)} %copy.36), calls=%async_computation.6 | async-start | bytes 7340032 | tf_op jit(solution)/shard_map/all_to_all | solution.py:40
  567.7 5.8 copy-start.2
  575.8 6.2 slice-start
  577.6 4.4 slice-start.1
  577.6 8.0 %slice-start.2 = ((s8[7077888]{0:T(1024)(128)(4,1)}), s8[4194304]{0:T(1024)(128)(4,1)S(1)}, s32[]{:S(2)}) async-start(s8[7077888]{0:T(1024)(128)(4,1)} %bitcast.43), calls=%async_computation.18 | async-start | bytes 8388608
  582.0 3.7 slice-start.3
Sparse Core Ops, SparseCore 0:
  18.3 94.8 reduce-scatter.4
  115.8 126.1 reduce-scatter.2
  243.6 47.2 all-gather.7
  319.5 58.5 all-gather.5
  380.1 96.1 all-gather.3

commit v5 on v4

--- a/solution.py
+++ b/solution.py
@@ -63,13 +63,20 @@
         right_terms.append(to_keepers(gram_right.astype(jnp.bfloat16))[: b1 - b0])
         pieces.append(piece)
 
-    norm_grad, adam_sq = lax.psum((local_norm, jnp.concatenate(adam_parts)), ("dp", "group"))
     piece = jnp.concatenate(pieces) if len(pieces) > 1 else pieces[0]
     half = jnp.einsum("cim,cmj->cij", piece, right_root, preferred_element_type=jnp.float32)
     half = half.astype(jnp.bfloat16)
     full_left = lax.all_gather(left_root, "group", axis=2, tiled=True)
     direction = jnp.einsum("cim,cmj->cij", full_left, half, preferred_element_type=jnp.float32)
-    direction_sq = lax.psum(jnp.sum(direction * direction, axis=(1, 2)), "group")
+    direction_part = jnp.sum(direction * direction, axis=(1, 2))
+    direction_rows = lax.dynamic_update_slice_in_dim(
+        jnp.zeros((n_dp, cap), jnp.float32), direction_part[None], me_dp, 0
+    )
+    sums, left_terms, right_terms = lax.optimization_barrier(
+        ((local_norm, jnp.concatenate(adam_parts), direction_rows), left_terms, right_terms)
+    )
+    norm_grad, adam_sq, direction_all = lax.psum(sums, ("dp", "group"))
+    direction_sq = lax.dynamic_slice_in_dim(direction_all, me_dp, 1, 0)[0]
     adam_pad = jnp.pad(adam_sq, (0, slots - count)).reshape(cap, n_dp)
     adam_owned = lax.dynamic_slice_in_dim(adam_pad, me_dp, 1, 1)[:, 0]
     ratio = jnp.sqrt(adam_owned / (direction_sq + EPS_GRAFT))

time: 662 us -> 677 us (1.023)
  waiting for transfers between devices: 338 us -> 381 us
  blocking collectives: 127 us -> 90.3 us
    all_to_all x5, waiting for transfers between devices: 150 us -> 193 us  [to_keepers(): lax.all_to_all(owned.reshape(n_slots, n_dp, rows, quarter), 'dp', 1, 1, t...]
    psum x2 -> x1, blocking collectives: 74.5 us -> 38.1 us  [on_device(): norm_grad, adam_sq, direction_all = lax.psum(sums, ('dp', 'group'))]
  transfers between devices with their start and end apart: 13 -> 13, of which waited for: 9 -> 10; matrix products, arithmetic and copies ran while one was open for 19% -> 16% of each run, Pallas kernels for 0% -> 0%
where the time goes in v5:
time: 677 us; the launch traced here: 676 us
  waiting for transfers between devices  381 us (56%)
  blocking collectives  90.3 us (13%)
  local copies, waits for them, and re-layouts  75.8 us (11%)
  matrix products  41.8 us (6%)
  starting transfers between devices  39.5 us (6%)
  other arithmetic  33.6 us (5%)
  between operations  14 us (2%)
    all_to_all x5, waiting for transfers between devices, to_keepers(): lax.all_to_all(owned.reshape(n_slots, n_dp, rows, quarter), 'dp', 1, 1, t...  193 us
    all_to_all x3, waiting for transfers between devices, to_owners(): lax.all_to_all(padded.reshape(n_slots, n_dp, rows, quarter), 'dp', 1, 1,...  111 us
    reduce_scatter x2, waiting for transfers between devices, on_device(): lax.psum_scatter(partials[0, b0:b1], 'group', scatter_dimension=2, tiled=...  68.5 us
    all_to_all x1, blocking collectives, to_owners(): lax.all_to_all(padded.reshape(n_slots, n_dp, rows, quarter), 'dp', 1, 1,...  52.2 us
    psum x1, blocking collectives, on_device(): norm_grad, adam_sq, direction_all = lax.psum(sums, ('dp', 'group'))  38.1 us
    squeeze x2, local copies, waits for them, and re-layouts, on_device(): partials[0, b0:b1]  24.7 us
    all_to_all x5, starting transfers between devices, to_keepers(): lax.all_to_all(owned.reshape(n_slots, n_dp, rows, quarter), 'dp', 1, 1, t...  23.4 us
    dot_general x1, matrix products, on_device(): jnp.einsum('cim,cmj->cij', full_left, half, preferred_element_type=jnp.fl...  17.8 us
  transfers between devices with their start and end apart: 13, of which 10 were waited for; matrix products, arithmetic and copies ran while one was open for 16% of the time, Pallas kernels for 0%

profile of v5, /device:TPU:0, one launch (start us, length us, event | category | flops | bytes accessed | tf_op | source)
XLA Modules:
  0.0 675.7 jit_solution(9381388113911871350)
XLA Ops:
  7.2 11.1 %slice_bitcast_fusion.1 = f32[22,128,1024]{2,1,0:T(8,128)} fusion(f32[1,54,128,1024]{3,2,1,0:T(8,128)} %param.8), kind=kLoop, calls=%fused_computation.5 | loop fusion | bytes 23068672 | tf_op jit(solution)/shard_map/squeeze | solution.py:50
  18.4 13.7 %slice_bitcast_fusion = f32[32,128,1024]{2,1,0:T(8,128)} fusion(f32[1,54,128,1024]{3,2,1,0:T(8,128)} %param.8), kind=kLoop, calls=%fused_computation | loop fusion | bytes 33554432 | tf_op jit(solution)/shard_map/squeeze | solution.py:50
  37.8 7.0 %all-to-all-start = ((bf16[7,8,128,256]{3,2,0,1:T(8,128)(2,1)}), bf16[7,8,128,256]{3,2,0,1:T(8,128)(2,1)}, u32[]{:S(2)}, u32[]{:S(2)}) async-start(bf16[7,8,128,256]{3,2,0,1:T(8,128)(2,1)} %copy.28), calls=%async_computation.1 | async-start | bytes 7340032 | tf_op jit(solution)/shard_map/all_to_all | solution.py:35
  44.8 68.5 %reduce-scatter.5.cloned.1.call-done = f32[22,128,256]{2,1,0:T(8,128)} async-done(((f32[22,128,1024]{2,1,0:T(8,128)}), f32[22,128,256]{2,1,0:T(8,128)}) %reduce-scatter.5.cloned.1.call-update) | async-done | bytes 2883600 | tf_op jit(solution)/shard_map/reduce_scatter | solution.py:50
  113.3 5.4 fusion.11
  120.1 6.6 all-to-all-done
  126.7 4.3 all-to-all-start.3
  136.9 30.7 %all-to-all-done.3 = bf16[3,8,128,256]{3,2,0,1:T(8,128)(2,1)} async-done(((bf16[3,8,128,256]{3,2,0,1:T(8,128)(2,1)}), bf16[3,8,128,256]{3,2,0,1:T(8,128)(2,1)}, u32[]{:S(2)}, u32[]{:S(2)}) %all-to-all-start.3) | async-done | bytes 1572896 | tf_op jit(solution)/shard_map/all_to_all | solution.py:35
  167.6 4.5 all-to-all-start.1
  175.0 4.3 copy.29
  179.3 74.2 %all-to-all-done.1 = bf16[7,8,128,256]{3,2,0,1:T(8,128)(2,1)} async-done(((bf16[7,8,128,256]{3,2,0,1:T(8,128)(2,1)}), bf16[7,8,128,256]{3,2,0,1:T(8,128)(2,1)}, u32[]{:S(2)}, u32[]{:S(2)}) %all-to-all-start.1) | async-done | bytes 3670048 | tf_op jit(solution)/shard_map/all_to_all | solution.py:35
  253.5 4.5 copy.31
  258.0 7.6 %fusion.4 = (f32[32,128,256]{2,1,0:T(8,128)}, f32[32]{0:T(128)S(1)}, bf16[32,128,256]{2,1,0:T(8,128)(2,1)S(1)}) fusion(f32[32,128,256]{2,1,0:T(8,128)} %reduce-scatter.3.cloned.1.call-done, f32[54,128,256]{2,1,0:T(8,128)} %param.9), kind=kLoop, calls=%fused_computation.13 | loop fusion | flops 9437152 | bytes 14680192 | tf_op jit(solution)/shard_map/add | solution.py:53
  265.8 52.2 %all_to_all.45 = bf16[4,8,128,256]{3,2,0,1:T(8,128)(2,1)S(1)} all-to-all(bf16[4,8,128,256]{3,2,0,1:T(8,128)(2,1)S(1)} %copy.32), channel_id=1, replica_groups=mesh['dp'=8,'group'=4] {'dp'}, dimensions={1} | all-to-all | bytes 4194304 | tf_op jit(solution)/shard_map/all_to_all | solution.py:35
  320.1 5.1 convolution_convert_fusion.2
  326.5 4.5 all-to-all-start.5
  331.0 5.7 convolution_convert_fusion.1
  337.9 28.9 %all-to-all-done.5 = bf16[3,8,128,256]{3,2,0,1:T(8,128)(2,1)} async-done(((bf16[3,8,128,256]{3,2,0,1:T(8,128)(2,1)}), bf16[3,8,128,256]{3,2,0,1:T(8,128)(2,1)}, u32[]{:S(2)}, u32[]{:S(2)}) %all-to-all-start.5) | async-done | bytes 1572896 | tf_op jit(solution)/shard_map/all_to_all | solution.py:40
  371.2 7.0 %all-gather.6.cloned.1.call-done = bf16[4,1024,1024]{2,1,0:T(8,128)(2,1)} async-done(((bf16[4,1024,256]{2,1,0:T(8,128)(2,1)}), bf16[4,1024,1024]{2,1,0:T(8,128)(2,1)}) %all-gather.6.cloned.1.call-update) | async-done | bytes 8388624 | tf_op jit(solution)/shard_map/all_gather | solution.py:58
  378.2 6.3 fusion.14
  386.0 21.6 %all-to-all-done.7 = bf16[3,8,128,256]{3,2,0,1:T(8,128)(2,1)} async-done(((bf16[3,8,128,256]{3,2,0,1:T(8,128)(2,1)}), bf16[3,8,128,256]{3,2,0,1:T(8,128)(2,1)}, u32[]{:S(2)}, u32[]{:S(2)}) %all-to-all-start.7) | async-done | bytes 1572896 | tf_op jit(solution)/shard_map/all_to_all | solution.py:40
  407.7 4.4 all-to-all-start.4
  412.0 6.9 %convolution_convert_fusion = bf16[4,1024,256]{2,1,0:T(8,128)(2,1)S(1)} fusion(bf16[4,1024,1024]{2,1,0:T(8,128)(2,1)} %all-gather.6.cloned.1.call-done, bf16[4,1024,256]{2,1,0:T(8,128)(2,1)} %bitcast.46), kind=kOutput, calls=%fused_computation.22 | convolution fusion | flops 2148532224 | bytes 12582912 | tf_op jit(solution)/shard_map/cim,cij->cmj/dot_general | solution.py:61
  420.4 39.4 %all-to-all-done.4 = bf16[4,8,128,256]{3,2,0,1:T(8,128)(2,1)} async-done(((bf16[4,8,128,256]{3,2,0,1:T(8,128)(2,1)}), bf16[4,8,128,256]{3,2,0,1:T(8,128)(2,1)}, u32[]{:S(2)}, u32[]{:S(2)}) %all-to-all-start.4) | async-done | bytes 2097184 | tf_op jit(solution)/shard_map/all_to_all | solution.py:40
  459.8 4.4 all-to-all-start.6
  472.9 39.1 %all-to-all-done.6 = bf16[4,8,128,256]{3,2,0,1:T(8,128)(2,1)} async-done(((bf16[4,8,128,256]{3,2,0,1:T(8,128)(2,1)}), bf16[4,8,128,256]{3,2,0,1:T(8,128)(2,1)}, u32[]{:S(2)}, u32[]{:S(2)}) %all-to-all-start.6) | async-done | bytes 2097184 | tf_op jit(solution)/shard_map/all_to_all | solution.py:40
  515.1 17.8 %multiply_reduce_fusion = (f32[7]{0:T(128)S(1)}, f32[7,1024,256]{2,1,0:T(8,128)}) fusion(bf16[7,1024,1024]{2,1,0:T(8,128)(2,1)} %all-gather.4.cloned.1.call-done, bf16[7,1024,256]{2,1,0:T(8,128)(2,1)} %bitcast.53, bf16[3,1024,1024]{2,1,0:T(8,128)(2,1)} %all-gather.8.cloned.1.call-done, bf16[4,1024,1024]{2,1,0:T(8,128)(2,1)} %all-gather.6.cloned.1.call-done), kind=kOutput, calls=%fused_computation.7 | convolution fusion | flops 7529037824 | bytes 40370204 | tf_op jit(solution)/shard_map/cim,cmj->cij/dot_general | solution.py:70
  533.2 38.1 %all-reduce.4 = (f32[54]{0:T(128)S(1)}, f32[8,7]{1,0:T(8,128)S(1)}, f32[2,2048]{1,0:T(2,128)S(1)}) all-reduce(f32[54]{0:T(128)S(1)} %pad_maximum_fusion.1, f32[8,7]{1,0:T(8,128)S(1)} %dynamic_update_slice.3, f32[2,2048]{1,0:T(2,128)S(1)} %bitcast.58), channel_id=1, replica_groups=mesh['dp'=8,'group'=4] {'dp','group'}, use_global_device_ids=true, to_apply=%region_5.6 | all-reduce | flops 4206 | bytes 33648 | tf_op jit(solution)/shard_map/psum | solution.py:78
  577.6 5.9 all-to-all-start.8
  583.6 6.0 pad_maximum_fusion
  590.2 10.1 %multiply_add_fusion = (f32[54,128,256]{2,1,0:T(8,128)}, f32[54,128,256]{2,1,0:T(8,128)}) fusion(f32[54,128,256]{2,1,0:T(8,128)} %param.11, bf16[22,128,256]{2,1,0:T(8,128)(2,1)S(1)} %copy-done.3, bf16[32,128,256]{2,1,0:T(8,128)(2,1)S(1)} %bitcast.44, bf16[22,128,256]{2,1,0:T(8,128)(2,1)S(1)} %copy-done.2, bf16[32,128,256]{2,1,0:T(8,128)(2,1)S(1)} %bitcast.43, ...), kind=kLoop, calls=%fused_computation.9 | loop fusion | flops 17694720 | bytes 35389440 | tf_op jit(solution)/shard_map/add | solution.py:90
  600.4 64.1 %all-to-all-done.8 = bf16[7,8,128,256]{3,2,0,1:T(8,128)(2,1)} async-done(((bf16[7,8,128,256]{3,2,0,1:T(8,128)(2,1)}), bf16[7,8,128,256]{3,2,0,1:T(8,128)(2,1)}, u32[]{:S(2)}, u32[]{:S(2)}) %all-to-all-start.8) | async-done | bytes 3670048 | tf_op jit(solution)/shard_map/all_to_all | solution.py:40
  (59 shorter events, 51.9 us)
Async XLA Ops:
  7.2 106.2 %reduce-scatter.5.cloned.1.call-start = ((), (), s32[]{:S(2)}) async-start(), calls=%async_computation.12 | async-start | bytes 14417920 | tf_op jit(solution)/shard_map/reduce_scatter | solution.py:50
  18.3 239.7 %reduce-scatter.3.cloned.1.call-start = ((), (), s32[]{:S(2)}) async-start(), calls=%async_computation.11 | async-start | bytes 20971520 | tf_op jit(solution)/shard_map/reduce_scatter | solution.py:50
  32.0 2.8 copy-start.4
  37.8 88.8 %all-to-all-start = ((bf16[7,8,128,256]{3,2,0,1:T(8,128)(2,1)}), bf16[7,8,128,256]{3,2,0,1:T(8,128)(2,1)}, u32[]{:S(2)}, u32[]{:S(2)}) async-start(bf16[7,8,128,256]{3,2,0,1:T(8,128)(2,1)} %copy.28), calls=%async_computation.1 | async-start | bytes 7340032 | tf_op jit(solution)/shard_map/all_to_all | solution.py:35
  126.7 40.9 %all-to-all-start.3 = ((bf16[3,8,128,256]{3,2,0,1:T(8,128)(2,1)}), bf16[3,8,128,256]{3,2,0,1:T(8,128)(2,1)}, u32[]{:S(2)}, u32[]{:S(2)}) async-start(bf16[3,8,128,256]{3,2,0,1:T(8,128)(2,1)} %copy.34), calls=%async_computation.5 | async-start | bytes 3145728 | tf_op jit(solution)/shard_map/all_to_all | solution.py:35
  167.6 85.9 %all-to-all-start.1 = ((bf16[7,8,128,256]{3,2,0,1:T(8,128)(2,1)}), bf16[7,8,128,256]{3,2,0,1:T(8,128)(2,1)}, u32[]{:S(2)}, u32[]{:S(2)}) async-start(bf16[7,8,128,256]{3,2,0,1:T(8,128)(2,1)} %copy.30), calls=%async_computation.2 | async-start | bytes 7340032 | tf_op jit(solution)/shard_map/all_to_all | solution.py:35
  172.1 147.9 %all-gather.8.cloned.1.call-start = ((), (), s32[]{:S(2)}) async-start(), calls=%async_computation.15 | async-start | bytes 7864320 | tf_op jit(solution)/shard_map/all_gather | solution.py:58
  174.9 203.2 %all-gather.6.cloned.1.call-start = ((), (), s32[]{:S(2)}) async-start(), calls=%async_computation.14 | async-start | bytes 10485760 | tf_op jit(solution)/shard_map/all_gather | solution.py:58
  319.5 195.7 %all-gather.4.cloned.1.call-start = ((), (), s32[]{:S(2)}) async-start(), calls=%async_computation.13 | async-start | bytes 18350080 | tf_op jit(solution)/shard_map/all_gather | solution.py:69
  326.5 40.4 %all-to-all-start.5 = ((bf16[3,8,128,256]{3,2,0,1:T(8,128)(2,1)}), bf16[3,8,128,256]{3,2,0,1:T(8,128)(2,1)}, u32[]{:S(2)}, u32[]{:S(2)}) async-start(bf16[3,8,128,256]{3,2,0,1:T(8,128)(2,1)} %copy.38), calls=%async_computation.7 | async-start | bytes 3145728 | tf_op jit(solution)/shard_map/all_to_all | solution.py:40
  366.9 40.8 %all-to-all-start.7 = ((bf16[3,8,128,256]{3,2,0,1:T(8,128)(2,1)}), bf16[3,8,128,256]{3,2,0,1:T(8,128)(2,1)}, u32[]{:S(2)}, u32[]{:S(2)}) async-start(bf16[3,8,128,256]{3,2,0,1:T(8,128)(2,1)} %copy.44), calls=%async_computation.9 | async-start | bytes 3145728 | tf_op jit(solution)/shard_map/all_to_all | solution.py:40
  407.7 52.2 %all-to-all-start.4 = ((bf16[4,8,128,256]{3,2,0,1:T(8,128)(2,1)}), bf16[4,8,128,256]{3,2,0,1:T(8,128)(2,1)}, u32[]{:S(2)}, u32[]{:S(2)}) async-start(bf16[4,8,128,256]{3,2,0,1:T(8,128)(2,1)} %copy.36), calls=%async_computation.6 | async-start | bytes 4194304 | tf_op jit(solution)/shard_map/all_to_all | solution.py:40
  459.8 52.2 %all-to-all-start.6 = ((bf16[4,8,128,256]{3,2,0,1:T(8,128)(2,1)}), bf16[4,8,128,256]{3,2,0,1:T(8,128)(2,1)}, u32[]{:S(2)}, u32[]{:S(2)}) async-start(bf16[4,8,128,256]{3,2,0,1:T(8,128)(2,1)} %copy.41), calls=%async_computation.8 | async-start | bytes 4194304 | tf_op jit(solution)/shard_map/all_to_all | solution.py:40
  515.1 18.0 %copy-start.5 = (f32[1,1,2,2048]{3,2,1,0:T(2,128)S(1)}, f32[1,1,2,2048]{3,2,1,0:T(2,128)}, u32[]{:S(2)}) copy-start(f32[1,1,2,2048]{3,2,1,0:T(2,128)} %param.14) | copy-start | bytes 49156
  577.6 86.9 %all-to-all-start.8 = ((bf16[7,8,128,256]{3,2,0,1:T(8,128)(2,1)}), bf16[7,8,128,256]{3,2,0,1:T(8,128)(2,1)}, u32[]{:S(2)}, u32[]{:S(2)}) async-start(bf16[7,8,128,256]{3,2,0,1:T(8,128)(2,1)} %copy.46), calls=%async_computation.10 | async-start | bytes 7340032 | tf_op jit(solution)/shard_map/all_to_all | solution.py:40
  583.6 6.0 copy-start.6
  583.6 6.7 copy-start
  583.6 6.6 copy-start.1
  583.6 6.6 copy-start.2
  583.6 6.6 copy-start.3
Sparse Core Ops, SparseCore 0:
  18.4 94.8 reduce-scatter.4
  115.9 126.1 reduce-scatter.2
  243.7 47.2 all-gather.7
  319.6 58.5 all-gather.5
  380.2 95.9 all-gather.3

commit v6 on v4

--- a/solution.py
+++ b/solution.py
@@ -63,7 +63,10 @@
         right_terms.append(to_keepers(gram_right.astype(jnp.bfloat16))[: b1 - b0])
         pieces.append(piece)
 
-    norm_grad, adam_sq = lax.psum((local_norm, jnp.concatenate(adam_parts)), ("dp", "group"))
+    flat = jnp.concatenate([local_norm.reshape(-1)] + adam_parts)
+    total = lax.psum(jnp.pad(flat, (0, max(16384 - flat.shape[0], 0))), ("dp", "group"))
+    norm_grad = total[: local_norm.size].reshape(local_norm.shape)
+    adam_sq = total[local_norm.size : local_norm.size + count]
     piece = jnp.concatenate(pieces) if len(pieces) > 1 else pieces[0]
     half = jnp.einsum("cim,cmj->cij", piece, right_root, preferred_element_type=jnp.float32)
     half = half.astype(jnp.bfloat16)

time: 662 us -> 765 us (1.16)
  waiting for transfers between devices: 338 us -> 507 us
  blocking collectives: 127 us -> 58.3 us
    all_gather x1, waiting for transfers between devices: 0.02 us -> 97.9 us  [on_device(): full_left = lax.all_gather(left_root, 'group', axis=2, tiled=True)]
    psum x0 -> x1, waiting for transfers between devices: none -> 70.3 us  [on_device(): lax.psum(jnp.pad(flat, (0, max(16384 - flat.shape[0], 0))), ('dp', 'group'))]
    psum x1 -> x0, blocking collectives: 68 us -> none  [on_device(): lax.psum((local_norm, jnp.concatenate(adam_parts)), ('dp', 'group'))]
  transfers between devices with their start and end apart: 13 -> 14, of which waited for: 9 -> 11; matrix products, arithmetic and copies ran while one was open for 19% -> 17% of each run, Pallas kernels for 0% -> 0%
where the time goes in v6:
time: 765 us; the launch traced here: 764 us
  waiting for transfers between devices  507 us (66%)
  local copies, waits for them, and re-layouts  72.8 us (10%)
  blocking collectives  58.3 us (8%)
  matrix products  41.7 us (5%)
  starting transfers between devices  39.3 us (5%)
  other arithmetic  30.9 us (4%)
  between operations  14.4 us (2%)
    all_to_all x5, waiting for transfers between devices, to_keepers(): lax.all_to_all(owned.reshape(n_slots, n_dp, rows, quarter), 'dp', 1, 1, t...  152 us
    all_to_all x3, waiting for transfers between devices, to_owners(): lax.all_to_all(padded.reshape(n_slots, n_dp, rows, quarter), 'dp', 1, 1,...  111 us
    all_gather x1, waiting for transfers between devices, on_device(): full_left = lax.all_gather(left_root, 'group', axis=2, tiled=True)  97.9 us
    psum x1, waiting for transfers between devices, on_device(): lax.psum(jnp.pad(flat, (0, max(16384 - flat.shape[0], 0))), ('dp', 'group'))  70.3 us
    reduce_scatter x2, waiting for transfers between devices, on_device(): lax.psum_scatter(partials[0, b0:b1], 'group', scatter_dimension=2, tiled=...  68.5 us
    all_to_all x1, blocking collectives, to_owners(): lax.all_to_all(padded.reshape(n_slots, n_dp, rows, quarter), 'dp', 1, 1,...  52.2 us
    squeeze x2, local copies, waits for them, and re-layouts, on_device(): partials[0, b0:b1]  24.6 us
    all_to_all x5, starting transfers between devices, to_keepers(): lax.all_to_all(owned.reshape(n_slots, n_dp, rows, quarter), 'dp', 1, 1, t...  23.2 us
  transfers between devices with their start and end apart: 14, of which 11 were waited for; matrix products, arithmetic and copies ran while one was open for 17% of the time, Pallas kernels for 0%

profile of v6, /device:TPU:0, one launch (start us, length us, event | category | flops | bytes accessed | tf_op | source)
XLA Modules:
  0.0 763.9 jit_solution(17270704169734318350)
XLA Ops:
  7.2 10.9 %slice_bitcast_fusion.1 = f32[22,128,1024]{2,1,0:T(8,128)} fusion(f32[1,54,128,1024]{3,2,1,0:T(8,128)} %param.8), kind=kLoop, calls=%fused_computation.5 | loop fusion | bytes 23068672 | tf_op jit(solution)/shard_map/squeeze | solution.py:50
  18.2 13.7 %slice_bitcast_fusion = f32[32,128,1024]{2,1,0:T(8,128)} fusion(f32[1,54,128,1024]{3,2,1,0:T(8,128)} %param.8), kind=kLoop, calls=%fused_computation | loop fusion | bytes 33554432 | tf_op jit(solution)/shard_map/squeeze | solution.py:50
  37.7 7.0 all-to-all-start
  44.7 68.5 %reduce-scatter.5.cloned.1.call-done = f32[22,128,256]{2,1,0:T(8,128)} async-done(((f32[22,128,1024]{2,1,0:T(8,128)}), f32[22,128,256]{2,1,0:T(8,128)}) %reduce-scatter.5.cloned.1.call-update) | async-done | bytes 2883600 | tf_op jit(solution)/shard_map/reduce_scatter | solution.py:50
  113.2 5.3 fusion.11
  120.0 6.6 all-to-all-done
  126.5 4.3 all-to-all-start.3
  136.8 30.7 %all-to-all-done.3 = bf16[3,8,128,256]{3,2,0,1:T(8,128)(2,1)} async-done(((bf16[3,8,128,256]{3,2,0,1:T(8,128)(2,1)}), bf16[3,8,128,256]{3,2,0,1:T(8,128)(2,1)}, u32[]{:S(2)}, u32[]{:S(2)}) %all-to-all-start.3) | async-done | bytes 1572896 | tf_op jit(solution)/shard_map/all_to_all | solution.py:35
  167.5 4.5 all-to-all-start.1
  174.9 4.3 copy.29
  179.2 74.2 %all-to-all-done.1 = bf16[7,8,128,256]{3,2,0,1:T(8,128)(2,1)} async-done(((bf16[7,8,128,256]{3,2,0,1:T(8,128)(2,1)}), bf16[7,8,128,256]{3,2,0,1:T(8,128)(2,1)}, u32[]{:S(2)}, u32[]{:S(2)}) %all-to-all-start.1) | async-done | bytes 3670048 | tf_op jit(solution)/shard_map/all_to_all | solution.py:35
  253.4 4.5 copy.31
  257.8 8.0 %fusion.4 = (f32[32,128,256]{2,1,0:T(8,128)}, f32[32]{0:T(128)S(1)}, bf16[32,128,256]{2,1,0:T(8,128)(2,1)S(1)}) fusion(f32[32,128,256]{2,1,0:T(8,128)} %reduce-scatter.3.cloned.1.call-done, f32[54,128,256]{2,1,0:T(8,128)} %param.9), kind=kLoop, calls=%fused_computation.13 | loop fusion | flops 9437152 | bytes 14680192 | tf_op jit(solution)/shard_map/add | solution.py:53
  266.1 52.2 %all_to_all.45 = bf16[4,8,128,256]{3,2,0,1:T(8,128)(2,1)S(1)} all-to-all(bf16[4,8,128,256]{3,2,0,1:T(8,128)(2,1)S(1)} %copy.32), channel_id=1, replica_groups=mesh['dp'=8,'group'=4] {'dp'}, dimensions={1} | all-to-all | bytes 4194304 | tf_op jit(solution)/shard_map/all_to_all | solution.py:35
  321.2 5.1 convolution_convert_fusion.2
  327.5 4.5 all-to-all-start.6
  332.0 5.7 convolution_convert_fusion.1
  339.0 28.9 %all-to-all-done.6 = bf16[3,8,128,256]{3,2,0,1:T(8,128)(2,1)} async-done(((bf16[3,8,128,256]{3,2,0,1:T(8,128)(2,1)}), bf16[3,8,128,256]{3,2,0,1:T(8,128)(2,1)}, u32[]{:S(2)}, u32[]{:S(2)}) %all-to-all-start.6) | async-done | bytes 1572896 | tf_op jit(solution)/shard_map/all_to_all | solution.py:40
  372.2 6.2 all-gather.6.cloned.1.call-done
  378.4 6.3 fusion.14
  386.3 22.8 %all-to-all-done.8 = bf16[3,8,128,256]{3,2,0,1:T(8,128)(2,1)} async-done(((bf16[3,8,128,256]{3,2,0,1:T(8,128)(2,1)}), bf16[3,8,128,256]{3,2,0,1:T(8,128)(2,1)}, u32[]{:S(2)}, u32[]{:S(2)}) %all-to-all-start.8) | async-done | bytes 1572896 | tf_op jit(solution)/shard_map/all_to_all | solution.py:40
  409.1 4.4 all-to-all-start.5
  413.4 7.0 convolution_convert_fusion
  421.9 39.9 %all-to-all-done.5 = bf16[4,8,128,256]{3,2,0,1:T(8,128)(2,1)} async-done(((bf16[4,8,128,256]{3,2,0,1:T(8,128)(2,1)}), bf16[4,8,128,256]{3,2,0,1:T(8,128)(2,1)}, u32[]{:S(2)}, u32[]{:S(2)}) %all-to-all-start.5) | async-done | bytes 2097184 | tf_op jit(solution)/shard_map/all_to_all | solution.py:40
  461.7 4.3 all-to-all-start.7
  466.1 70.3 %all-reduce.7.cloned.1.call-done = f32[16384]{0:T(1024)} async-done(((f32[16384]{0:T(1024)}), f32[16384]{0:T(1024)}) %all-reduce.7.cloned.1.call-update) | async-done | bytes 65552 | tf_op jit(solution)/shard_map/psum | solution.py:67
  537.3 97.9 %all-gather.4.cloned.1.call-done = bf16[7,1024,1024]{2,1,0:T(8,128)(2,1)} async-done(((bf16[7,1024,256]{2,1,0:T(8,128)(2,1)}), bf16[7,1024,1024]{2,1,0:T(8,128)(2,1)}) %all-gather.4.cloned.1.call-update) | async-done | bytes 14680080 | tf_op jit(solution)/shard_map/all_gather | solution.py:73
  635.2 17.6 %multiply_reduce_fusion = (f32[7]{0:T(128)S(1)}, f32[7,1024,256]{2,1,0:T(8,128)}) fusion(bf16[7,1024,1024]{2,1,0:T(8,128)(2,1)} %all-gather.4.cloned.1.call-done, bf16[7,1024,256]{2,1,0:T(8,128)(2,1)} %bitcast.51, bf16[3,1024,1024]{2,1,0:T(8,128)(2,1)} %all-gather.8.cloned.1.call-done, bf16[4,1024,1024]{2,1,0:T(8,128)(2,1)} %all-gather.6.cloned.1.call-done), kind=kOutput, calls=%fused_computation.7 | convolution fusion | flops 7529037824 | bytes 40370204 | tf_op jit(solution)/shard_map/cim,cmj->cij/dot_general | solution.py:74
  652.9 6.1 psum.15
  665.0 5.7 all-to-all-start.4
  670.7 5.8 pad_maximum_fusion
  692.4 60.0 %all-to-all-done.4 = bf16[7,8,128,256]{3,2,0,1:T(8,128)(2,1)} async-done(((bf16[7,8,128,256]{3,2,0,1:T(8,128)(2,1)}), bf16[7,8,128,256]{3,2,0,1:T(8,128)(2,1)}, u32[]{:S(2)}, u32[]{:S(2)}) %all-to-all-start.4) | async-done | bytes 3670048 | tf_op jit(solution)/shard_map/all_to_all | solution.py:40
  (69 shorter events, 56.3 us)
Async XLA Ops:
  7.2 106.0 %reduce-scatter.5.cloned.1.call-start = ((), (), s32[]{:S(2)}) async-start(), calls=%async_computation.12 | async-start | bytes 14417920 | tf_op jit(solution)/shard_map/reduce_scatter | solution.py:50
  18.2 239.7 %reduce-scatter.3.cloned.1.call-start = ((), (), s32[]{:S(2)}) async-start(), calls=%async_computation.11 | async-start | bytes 20971520 | tf_op jit(solution)/shard_map/reduce_scatter | solution.py:50
  31.9 2.8 copy-start
  37.7 88.8 %all-to-all-start = ((bf16[7,8,128,256]{3,2,0,1:T(8,128)(2,1)}), bf16[7,8,128,256]{3,2,0,1:T(8,128)(2,1)}, u32[]{:S(2)}, u32[]{:S(2)}) async-start(bf16[7,8,128,256]{3,2,0,1:T(8,128)(2,1)} %copy.28), calls=%async_computation.1 | async-start | bytes 7340032 | tf_op jit(solution)/shard_map/all_to_all | solution.py:35
  126.5 40.9 %all-to-all-start.3 = ((bf16[3,8,128,256]{3,2,0,1:T(8,128)(2,1)}), bf16[3,8,128,256]{3,2,0,1:T(8,128)(2,1)}, u32[]{:S(2)}, u32[]{:S(2)}) async-start(bf16[3,8,128,256]{3,2,0,1:T(8,128)(2,1)} %copy.34), calls=%async_computation.5 | async-start | bytes 3145728 | tf_op jit(solution)/shard_map/all_to_all | solution.py:35
  167.5 85.9 %all-to-all-start.1 = ((bf16[7,8,128,256]{3,2,0,1:T(8,128)(2,1)}), bf16[7,8,128,256]{3,2,0,1:T(8,128)(2,1)}, u32[]{:S(2)}, u32[]{:S(2)}) async-start(bf16[7,8,128,256]{3,2,0,1:T(8,128)(2,1)} %copy.30), calls=%async_computation.2 | async-start | bytes 7340032 | tf_op jit(solution)/shard_map/all_to_all | solution.py:35
  172.0 149.1 %all-gather.8.cloned.1.call-start = ((), (), s32[]{:S(2)}) async-start(), calls=%async_computation.16 | async-start | bytes 7864320 | tf_op jit(solution)/shard_map/all_gather | solution.py:58
  174.8 203.6 %all-gather.6.cloned.1.call-start = ((), (), s32[]{:S(2)}) async-start(), calls=%async_computation.15 | async-start | bytes 10485760 | tf_op jit(solution)/shard_map/all_gather | solution.py:58
  318.3 1.5 copy-start.1
  319.8 216.6 %all-reduce.7.cloned.1.call-start = ((), (), s32[]{:S(2)}) async-start(), calls=%async_computation.13 | async-start | bytes 131072 | tf_op jit(solution)/shard_map/psum | solution.py:67
  320.5 314.7 %all-gather.4.cloned.1.call-start = ((), (), s32[]{:S(2)}) async-start(), calls=%async_computation.14 | async-start | bytes 18350080 | tf_op jit(solution)/shard_map/all_gather | solution.py:73
  327.5 40.4 %all-to-all-start.6 = ((bf16[3,8,128,256]{3,2,0,1:T(8,128)(2,1)}), bf16[3,8,128,256]{3,2,0,1:T(8,128)(2,1)}, u32[]{:S(2)}, u32[]{:S(2)}) async-start(bf16[3,8,128,256]{3,2,0,1:T(8,128)(2,1)} %copy.40), calls=%async_computation.8 | async-start | bytes 3145728 | tf_op jit(solution)/shard_map/all_to_all | solution.py:40
  367.9 41.2 %all-to-all-start.8 = ((bf16[3,8,128,256]{3,2,0,1:T(8,128)(2,1)}), bf16[3,8,128,256]{3,2,0,1:T(8,128)(2,1)}, u32[]{:S(2)}, u32[]{:S(2)}) async-start(bf16[3,8,128,256]{3,2,0,1:T(8,128)(2,1)} %copy.46), calls=%async_computation.10 | async-start | bytes 3145728 | tf_op jit(solution)/shard_map/all_to_all | solution.py:40
  409.1 52.7 %all-to-all-start.5 = ((bf16[4,8,128,256]{3,2,0,1:T(8,128)(2,1)}), bf16[4,8,128,256]{3,2,0,1:T(8,128)(2,1)}, u32[]{:S(2)}, u32[]{:S(2)}) async-start(bf16[4,8,128,256]{3,2,0,1:T(8,128)(2,1)} %copy.38), calls=%async_computation.7 | async-start | bytes 4194304 | tf_op jit(solution)/shard_map/all_to_all | solution.py:40
  461.7 203.3 %all-to-all-start.7 = ((bf16[4,8,128,256]{3,2,0,1:T(8,128)(2,1)}), bf16[4,8,128,256]{3,2,0,1:T(8,128)(2,1)}, u32[]{:S(2)}, u32[]{:S(2)}) async-start(bf16[4,8,128,256]{3,2,0,1:T(8,128)(2,1)} %copy.43), calls=%async_computation.9 | async-start | bytes 4194304 | tf_op jit(solution)/shard_map/all_to_all | solution.py:40
  665.0 87.3 %all-to-all-start.4 = ((bf16[7,8,128,256]{3,2,0,1:T(8,128)(2,1)}), bf16[7,8,128,256]{3,2,0,1:T(8,128)(2,1)}, u32[]{:S(2)}, u32[]{:S(2)}) async-start(bf16[7,8,128,256]{3,2,0,1:T(8,128)(2,1)} %copy.36), calls=%async_computation.6 | async-start | bytes 7340032 | tf_op jit(solution)/shard_map/all_to_all | solution.py:40
  670.7 5.8 slice-start.4
  670.7 5.8 copy-start.2
  678.9 6.2 slice-start
  680.7 4.4 slice-start.1
  680.7 8.0 %slice-start.2 = ((s8[7077888]{0:T(1024)(128)(4,1)}), s8[4194304]{0:T(1024)(128)(4,1)S(1)}, s32[]{:S(2)}) async-start(s8[7077888]{0:T(1024)(128)(4,1)} %bitcast.44), calls=%async_computation.19 | async-start | bytes 8388608
  685.1 3.7 slice-start.3
Sparse Core Ops, SparseCore 0:
  18.3 94.8 reduce-scatter.4
  115.8 126.1 reduce-scatter.2
  243.6 47.2 all-gather.7
  319.9 58.5 all-gather.5
  384.8 151.4 all-reduce.6
  538.4 96.7 all-gather.3

commit v7 on v4

--- a/solution.py
+++ b/solution.py
@@ -44,7 +44,7 @@
     right_root = to_owners(right_roots, cap)
     local_norm = norm_partials[0, 0]
 
-    moments, adam_parts, left_terms, right_terms, pieces = [], [], [], [], []
+    grads, moments, adam_parts = [], [], []
     for index, (s0, s1) in enumerate(bounds):
         b0, b1 = s0 * n_dp, min(s1 * n_dp, count)
         grad = lax.psum_scatter(partials[0, b0:b1], "group", scatter_dimension=2, tiled=True)
@@ -54,7 +54,15 @@
         adam = grad / (jnp.sqrt(new_moment) + EPS_ADAM)
         adam_parts.append(jnp.sum(adam * adam, axis=(1, 2)))
         moments.append(new_moment)
-        mine = to_owners(grad.astype(jnp.bfloat16), s1 - s0)
+        grads.append(grad.astype(jnp.bfloat16))
+
+    norm_grad, adam_sq = lax.psum((local_norm, jnp.concatenate(adam_parts)), ("dp", "group"))
+    norm_grad, adam_sq, grads[0] = lax.optimization_barrier((norm_grad, adam_sq, grads[0]))
+
+    left_terms, right_terms, pieces = [], [], []
+    for (s0, s1), grad_low in zip(bounds, grads):
+        b0, b1 = s0 * n_dp, min(s1 * n_dp, count)
+        mine = to_owners(grad_low, s1 - s0)
         piece = lax.all_gather(mine, "group", axis=2, tiled=True)
         own_rows = lax.dynamic_slice_in_dim(piece, lower, quarter, 1)
         gram_left = jnp.einsum("cim,cjm->cij", piece, own_rows, preferred_element_type=jnp.float32)
@@ -63,7 +71,6 @@
         right_terms.append(to_keepers(gram_right.astype(jnp.bfloat16))[: b1 - b0])
         pieces.append(piece)
 
-    norm_grad, adam_sq = lax.psum((local_norm, jnp.concatenate(adam_parts)), ("dp", "group"))
     piece = jnp.concatenate(pieces) if len(pieces) > 1 else pieces[0]
     half = jnp.einsum("cim,cmj->cij", piece, right_root, preferred_element_type=jnp.float32)
     half = half.astype(jnp.bfloat16)

time: 662 us -> 652 us (0.985)
  blocking collectives: 127 us -> 98.1 us
  waiting for transfers between devices: 338 us -> 355 us
    psum x1, blocking collectives: 68 us -> 38.6 us  [on_device(): lax.psum((local_norm, jnp.concatenate(adam_parts)), ('dp', 'group'))]
    all_gather x1, waiting for transfers between devices: 0.02 us -> 10.2 us  [on_device(): full_left = lax.all_gather(left_root, 'group', axis=2, tiled=True)]
    all_to_all x5, waiting for transfers between devices: 150 us -> 159 us  [to_keepers(): lax.all_to_all(owned.reshape(n_slots, n_dp, rows, quarter), 'dp', 1, 1, t...]
  transfers between devices with their start and end apart: 13 -> 13, of which waited for: 9 -> 11; matrix products, arithmetic and copies ran while one was open for 19% -> 20% of each run, Pallas kernels for 0% -> 0%
where the time goes in v7:
time: 652 us; the launch traced here: 651 us
  waiting for transfers between devices  355 us (54%)
  blocking collectives  98.1 us (15%)
  local copies, waits for them, and re-layouts  72.9 us (11%)
  matrix products  41.7 us (6%)
  starting transfers between devices  38.2 us (6%)
  other arithmetic  30.9 us (5%)
  between operations  14.1 us (2%)
    all_to_all x5, waiting for transfers between devices, to_keepers(): lax.all_to_all(owned.reshape(n_slots, n_dp, rows, quarter), 'dp', 1, 1, t...  159 us
    all_to_all x3, waiting for transfers between devices, to_owners(): lax.all_to_all(padded.reshape(n_slots, n_dp, rows, quarter), 'dp', 1, 1,...  111 us
    reduce_scatter x2, waiting for transfers between devices, on_device(): lax.psum_scatter(partials[0, b0:b1], 'group', scatter_dimension=2, tiled=...  68.5 us
    all_to_all x1, blocking collectives, to_owners(): lax.all_to_all(padded.reshape(n_slots, n_dp, rows, quarter), 'dp', 1, 1,...  53.2 us
    psum x1, blocking collectives, on_device(): lax.psum((local_norm, jnp.concatenate(adam_parts)), ('dp', 'group'))  38.6 us
    squeeze x2, local copies, waits for them, and re-layouts, on_device(): partials[0, b0:b1]  24.6 us
    all_to_all x5, starting transfers between devices, to_keepers(): lax.all_to_all(owned.reshape(n_slots, n_dp, rows, quarter), 'dp', 1, 1, t...  22.2 us
    dot_general x1, matrix products, on_device(): jnp.einsum('cim,cmj->cij', full_left, half, preferred_element_type=jnp.fl...  17.7 us
  transfers between devices with their start and end apart: 13, of which 11 were waited for; matrix products, arithmetic and copies ran while one was open for 20% of the time, Pallas kernels for 0%

profile of v7, /device:TPU:0, one launch (start us, length us, event | category | flops | bytes accessed | tf_op | source)
XLA Modules:
  0.0 651.0 jit_solution(5039232775791451112)
XLA Ops:
  7.2 10.9 %slice_bitcast_fusion.1 = f32[22,128,1024]{2,1,0:T(8,128)} fusion(f32[1,54,128,1024]{3,2,1,0:T(8,128)} %param.8), kind=kLoop, calls=%fused_computation.5 | loop fusion | bytes 23068672 | tf_op jit(solution)/shard_map/squeeze | solution.py:50
  18.2 13.7 %slice_bitcast_fusion = f32[32,128,1024]{2,1,0:T(8,128)} fusion(f32[1,54,128,1024]{3,2,1,0:T(8,128)} %param.8), kind=kLoop, calls=%fused_computation | loop fusion | bytes 33554432 | tf_op jit(solution)/shard_map/squeeze | solution.py:50
  37.7 7.0 %all-to-all-start = ((bf16[7,8,128,256]{3,2,0,1:T(8,128)(2,1)}), bf16[7,8,128,256]{3,2,0,1:T(8,128)(2,1)}, u32[]{:S(2)}, u32[]{:S(2)}) async-start(bf16[7,8,128,256]{3,2,0,1:T(8,128)(2,1)} %copy.28), calls=%async_computation.1 | async-start | bytes 7340032 | tf_op jit(solution)/shard_map/all_to_all | solution.py:35
  44.7 68.5 %reduce-scatter.5.cloned.1.call-done = f32[22,128,256]{2,1,0:T(8,128)} async-done(((f32[22,128,1024]{2,1,0:T(8,128)}), f32[22,128,256]{2,1,0:T(8,128)}) %reduce-scatter.5.cloned.1.call-update) | async-done | bytes 2883600 | tf_op jit(solution)/shard_map/reduce_scatter | solution.py:50
  113.2 5.3 fusion.11
  120.0 6.6 %all-to-all-done = bf16[7,8,128,256]{3,2,0,1:T(8,128)(2,1)} async-done(((bf16[7,8,128,256]{3,2,0,1:T(8,128)(2,1)}), bf16[7,8,128,256]{3,2,0,1:T(8,128)(2,1)}, u32[]{:S(2)}, u32[]{:S(2)}) %all-to-all-start) | async-done | bytes 3670048 | tf_op jit(solution)/shard_map/all_to_all | solution.py:35
  126.5 4.3 all-to-all-start.3
  136.8 30.7 %all-to-all-done.3 = bf16[3,8,128,256]{3,2,0,1:T(8,128)(2,1)} async-done(((bf16[3,8,128,256]{3,2,0,1:T(8,128)(2,1)}), bf16[3,8,128,256]{3,2,0,1:T(8,128)(2,1)}, u32[]{:S(2)}, u32[]{:S(2)}) %all-to-all-start.3) | async-done | bytes 1572896 | tf_op jit(solution)/shard_map/all_to_all | solution.py:35
  167.5 4.5 all-to-all-start.1
  179.2 74.2 %all-to-all-done.1 = bf16[7,8,128,256]{3,2,0,1:T(8,128)(2,1)} async-done(((bf16[7,8,128,256]{3,2,0,1:T(8,128)(2,1)}), bf16[7,8,128,256]{3,2,0,1:T(8,128)(2,1)}, u32[]{:S(2)}, u32[]{:S(2)}) %all-to-all-start.1) | async-done | bytes 3670048 | tf_op jit(solution)/shard_map/all_to_all | solution.py:35
  253.4 4.5 copy.31
  257.8 8.0 %fusion.4 = (f32[32,128,256]{2,1,0:T(8,128)}, f32[32]{0:T(128)S(1)}, bf16[32,128,256]{2,1,0:T(8,128)(2,1)}) fusion(f32[32,128,256]{2,1,0:T(8,128)} %reduce-scatter.3.cloned.1.call-done, f32[54,128,256]{2,1,0:T(8,128)} %param.9), kind=kLoop, calls=%fused_computation.13 | loop fusion | flops 9437152 | bytes 14680192 | tf_op jit(solution)/shard_map/add | solution.py:53
  265.9 38.6 %all-reduce.4 = (f32[2,2048]{1,0:T(2,128)S(1)}, f32[54]{0:T(128)S(1)}) all-reduce(f32[2,2048]{1,0:T(2,128)S(1)} %bitcast.55, f32[54]{0:T(128)S(1)} %pad_maximum_fusion.1), channel_id=1, replica_groups=mesh['dp'=8,'group'=4] {'dp','group'}, use_global_device_ids=true, to_apply=%region_0.1 | all-reduce | flops 4150 | bytes 33200 | tf_op jit(solution)/shard_map/psum | solution.py:59
  306.2 53.2 %all_to_all.45 = bf16[4,8,128,256]{3,2,0,1:T(8,128)(2,1)S(1)} all-to-all(bf16[4,8,128,256]{3,2,0,1:T(8,128)(2,1)S(1)} %copy.32), channel_id=1, replica_groups=mesh['dp'=8,'group'=4] {'dp'}, dimensions={1} | all-to-all | bytes 4194304 | tf_op jit(solution)/shard_map/all_to_all | solution.py:35
  361.5 5.5 convolution_convert_fusion.1
  368.4 4.5 all-to-all-start.8
  372.9 5.2 convolution_convert_fusion.2
  379.4 29.3 %all-to-all-done.8 = bf16[3,8,128,256]{3,2,0,1:T(8,128)(2,1)} async-done(((bf16[3,8,128,256]{3,2,0,1:T(8,128)(2,1)}), bf16[3,8,128,256]{3,2,0,1:T(8,128)(2,1)}, u32[]{:S(2)}, u32[]{:S(2)}) %all-to-all-start.8) | async-done | bytes 1572896 | tf_op jit(solution)/shard_map/all_to_all | solution.py:40
  413.0 5.5 all-gather.6.cloned.1.call-done
  418.5 6.9 %convolution_convert_fusion = bf16[4,1024,256]{2,1,0:T(8,128)(2,1)S(1)} fusion(bf16[4,1024,1024]{2,1,0:T(8,128)(2,1)} %all-gather.6.cloned.1.call-done, bf16[4,1024,256]{2,1,0:T(8,128)(2,1)} %bitcast.39), kind=kOutput, calls=%fused_computation.22 | convolution fusion | flops 2148532224 | bytes 12582912 | tf_op jit(solution)/shard_map/cim,cij->cmj/dot_general | solution.py:69
  426.9 22.7 %all-to-all-done.6 = bf16[3,8,128,256]{3,2,0,1:T(8,128)(2,1)} async-done(((bf16[3,8,128,256]{3,2,0,1:T(8,128)(2,1)}), bf16[3,8,128,256]{3,2,0,1:T(8,128)(2,1)}, u32[]{:S(2)}, u32[]{:S(2)}) %all-to-all-start.6) | async-done | bytes 1572896 | tf_op jit(solution)/shard_map/all_to_all | solution.py:40
  449.6 4.3 all-to-all-start.7
  453.9 6.4 fusion.14
  461.7 40.0 %all-to-all-done.7 = bf16[4,8,128,256]{3,2,0,1:T(8,128)(2,1)} async-done(((bf16[4,8,128,256]{3,2,0,1:T(8,128)(2,1)}), bf16[4,8,128,256]{3,2,0,1:T(8,128)(2,1)}, u32[]{:S(2)}, u32[]{:S(2)}) %all-to-all-start.7) | async-done | bytes 2097184 | tf_op jit(solution)/shard_map/all_to_all | solution.py:40
  501.7 4.4 all-to-all-start.5
  506.4 10.2 %all-gather.4.cloned.1.call-done = bf16[7,1024,1024]{2,1,0:T(8,128)(2,1)} async-done(((bf16[7,1024,256]{2,1,0:T(8,128)(2,1)}), bf16[7,1024,1024]{2,1,0:T(8,128)(2,1)}) %all-gather.4.cloned.1.call-update) | async-done | bytes 14680080 | tf_op jit(solution)/shard_map/all_gather | solution.py:77
  516.6 17.7 %multiply_reduce_fusion = (f32[7]{0:T(128)S(1)}, f32[7,1024,256]{2,1,0:T(8,128)}) fusion(bf16[7,1024,1024]{2,1,0:T(8,128)(2,1)} %all-gather.4.cloned.1.call-done, bf16[7,1024,256]{2,1,0:T(8,128)(2,1)} %bitcast.50, bf16[3,1024,1024]{2,1,0:T(8,128)(2,1)} %all-gather.8.cloned.1.call-done, bf16[4,1024,1024]{2,1,0:T(8,128)(2,1)} %all-gather.6.cloned.1.call-done), kind=kOutput, calls=%fused_computation.7 | convolution fusion | flops 7529037824 | bytes 40370204 | tf_op jit(solution)/shard_map/cim,cmj->cij/dot_general | solution.py:78
  534.3 6.3 psum.23
  546.7 7.2 %all-to-all-done.5 = bf16[4,8,128,256]{3,2,0,1:T(8,128)(2,1)} async-done(((bf16[4,8,128,256]{3,2,0,1:T(8,128)(2,1)}), bf16[4,8,128,256]{3,2,0,1:T(8,128)(2,1)}, u32[]{:S(2)}, u32[]{:S(2)}) %all-to-all-start.5) | async-done | bytes 2097184 | tf_op jit(solution)/shard_map/all_to_all | solution.py:40
  553.9 4.7 all-to-all-start.4
  558.6 5.8 pad_maximum_fusion
  580.2 59.6 %all-to-all-done.4 = bf16[7,8,128,256]{3,2,0,1:T(8,128)(2,1)} async-done(((bf16[7,8,128,256]{3,2,0,1:T(8,128)(2,1)}), bf16[7,8,128,256]{3,2,0,1:T(8,128)(2,1)}, u32[]{:S(2)}, u32[]{:S(2)}) %all-to-all-start.4) | async-done | bytes 3670048 | tf_op jit(solution)/shard_map/all_to_all | solution.py:40
  (61 shorter events, 60.7 us)
Async XLA Ops:
  7.2 106.0 %reduce-scatter.5.cloned.1.call-start = ((), (), s32[]{:S(2)}) async-start(), calls=%async_computation.12 | async-start | bytes 14417920 | tf_op jit(solution)/shard_map/reduce_scatter | solution.py:50
  18.2 239.7 %reduce-scatter.3.cloned.1.call-start = ((), (), s32[]{:S(2)}) async-start(), calls=%async_computation.11 | async-start | bytes 20971520 | tf_op jit(solution)/shard_map/reduce_scatter | solution.py:50
  31.9 2.8 copy-start
  37.7 88.8 %all-to-all-start = ((bf16[7,8,128,256]{3,2,0,1:T(8,128)(2,1)}), bf16[7,8,128,256]{3,2,0,1:T(8,128)(2,1)}, u32[]{:S(2)}, u32[]{:S(2)}) async-start(bf16[7,8,128,256]{3,2,0,1:T(8,128)(2,1)} %copy.28), calls=%async_computation.1 | async-start | bytes 7340032 | tf_op jit(solution)/shard_map/all_to_all | solution.py:35
  126.5 40.9 %all-to-all-start.3 = ((bf16[3,8,128,256]{3,2,0,1:T(8,128)(2,1)}), bf16[3,8,128,256]{3,2,0,1:T(8,128)(2,1)}, u32[]{:S(2)}, u32[]{:S(2)}) async-start(bf16[3,8,128,256]{3,2,0,1:T(8,128)(2,1)} %copy.34), calls=%async_computation.5 | async-start | bytes 3145728 | tf_op jit(solution)/shard_map/all_to_all | solution.py:35
  167.5 85.9 %all-to-all-start.1 = ((bf16[7,8,128,256]{3,2,0,1:T(8,128)(2,1)}), bf16[7,8,128,256]{3,2,0,1:T(8,128)(2,1)}, u32[]{:S(2)}, u32[]{:S(2)}) async-start(bf16[7,8,128,256]{3,2,0,1:T(8,128)(2,1)} %copy.30), calls=%async_computation.2 | async-start | bytes 7340032 | tf_op jit(solution)/shard_map/all_to_all | solution.py:35
  172.0 189.5 %all-gather.8.cloned.1.call-start = ((), (), s32[]{:S(2)}) async-start(), calls=%async_computation.15 | async-start | bytes 7864320 | tf_op jit(solution)/shard_map/all_gather | solution.py:66
  174.8 243.7 %all-gather.6.cloned.1.call-start = ((), (), s32[]{:S(2)}) async-start(), calls=%async_computation.14 | async-start | bytes 10485760 | tf_op jit(solution)/shard_map/all_gather | solution.py:66
  257.8 8.1 %copy-start.1 = (f32[1,1,2,2048]{3,2,1,0:T(2,128)S(1)}, f32[1,1,2,2048]{3,2,1,0:T(2,128)}, u32[]{:S(2)}) copy-start(f32[1,1,2,2048]{3,2,1,0:T(2,128)} %param.14) | copy-start | bytes 49156
  360.9 155.6 %all-gather.4.cloned.1.call-start = ((), (), s32[]{:S(2)}) async-start(), calls=%async_computation.13 | async-start | bytes 18350080 | tf_op jit(solution)/shard_map/all_gather | solution.py:77
  368.4 40.3 %all-to-all-start.8 = ((bf16[3,8,128,256]{3,2,0,1:T(8,128)(2,1)}), bf16[3,8,128,256]{3,2,0,1:T(8,128)(2,1)}, u32[]{:S(2)}, u32[]{:S(2)}) async-start(bf16[3,8,128,256]{3,2,0,1:T(8,128)(2,1)} %copy.46), calls=%async_computation.10 | async-start | bytes 3145728 | tf_op jit(solution)/shard_map/all_to_all | solution.py:40
  408.7 40.9 %all-to-all-start.6 = ((bf16[3,8,128,256]{3,2,0,1:T(8,128)(2,1)}), bf16[3,8,128,256]{3,2,0,1:T(8,128)(2,1)}, u32[]{:S(2)}, u32[]{:S(2)}) async-start(bf16[3,8,128,256]{3,2,0,1:T(8,128)(2,1)} %copy.40), calls=%async_computation.8 | async-start | bytes 3145728 | tf_op jit(solution)/shard_map/all_to_all | solution.py:40
  449.6 52.2 %all-to-all-start.7 = ((bf16[4,8,128,256]{3,2,0,1:T(8,128)(2,1)}), bf16[4,8,128,256]{3,2,0,1:T(8,128)(2,1)}, u32[]{:S(2)}, u32[]{:S(2)}) async-start(bf16[4,8,128,256]{3,2,0,1:T(8,128)(2,1)} %copy.43), calls=%async_computation.9 | async-start | bytes 4194304 | tf_op jit(solution)/shard_map/all_to_all | solution.py:40
  501.7 52.2 %all-to-all-start.5 = ((bf16[4,8,128,256]{3,2,0,1:T(8,128)(2,1)}), bf16[4,8,128,256]{3,2,0,1:T(8,128)(2,1)}, u32[]{:S(2)}, u32[]{:S(2)}) async-start(bf16[4,8,128,256]{3,2,0,1:T(8,128)(2,1)} %copy.38), calls=%async_computation.7 | async-start | bytes 4194304 | tf_op jit(solution)/shard_map/all_to_all | solution.py:40
  553.9 86.0 %all-to-all-start.4 = ((bf16[7,8,128,256]{3,2,0,1:T(8,128)(2,1)}), bf16[7,8,128,256]{3,2,0,1:T(8,128)(2,1)}, u32[]{:S(2)}, u32[]{:S(2)}) async-start(bf16[7,8,128,256]{3,2,0,1:T(8,128)(2,1)} %copy.36), calls=%async_computation.6 | async-start | bytes 7340032 | tf_op jit(solution)/shard_map/all_to_all | solution.py:40
  558.6 5.8 copy-start.2
  566.7 6.2 slice-start
  568.5 4.4 slice-start.1
  568.6 8.0 %slice-start.2 = ((s8[7077888]{0:T(1024)(128)(4,1)}), s8[4194304]{0:T(1024)(128)(4,1)S(1)}, s32[]{:S(2)}) async-start(s8[7077888]{0:T(1024)(128)(4,1)} %bitcast.43), calls=%async_computation.18 | async-start | bytes 8388608
  573.0 3.7 slice-start.3
Sparse Core Ops, SparseCore 0:
  18.3 94.8 reduce-scatter.4
  115.8 126.1 reduce-scatter.2
  243.6 47.9 all-gather.7
  361.0 57.4 all-gather.5
  420.5 95.9 all-gather.3

commit v8 on v7

--- a/solution.py
+++ b/solution.py
@@ -56,8 +56,12 @@
         moments.append(new_moment)
         grads.append(grad.astype(jnp.bfloat16))
 
-    norm_grad, adam_sq = lax.psum((local_norm, jnp.concatenate(adam_parts)), ("dp", "group"))
-    norm_grad, adam_sq, grads[0] = lax.optimization_barrier((norm_grad, adam_sq, grads[0]))
+    adam_cat = jnp.pad(jnp.concatenate(adam_parts), (0, slots - count))
+    adam_rows = adam_cat.reshape(cap, n_dp).T
+    norm_rows = jnp.broadcast_to(local_norm.reshape(1, -1), (n_dp, local_norm.size))
+    sent = lax.all_to_all(jnp.concatenate([adam_rows, norm_rows], axis=1), "dp", 0, 0, tiled=True)
+    dp_sums = jnp.sum(sent, axis=0)
+    dp_sums, grads[0] = lax.optimization_barrier((dp_sums, grads[0]))
 
     left_terms, right_terms, pieces = [], [], []
     for (s0, s1), grad_low in zip(bounds, grads):
@@ -76,9 +80,10 @@
     half = half.astype(jnp.bfloat16)
     full_left = lax.all_gather(left_root, "group", axis=2, tiled=True)
     direction = jnp.einsum("cim,cmj->cij", full_left, half, preferred_element_type=jnp.float32)
-    direction_sq = lax.psum(jnp.sum(direction * direction, axis=(1, 2)), "group")
-    adam_pad = jnp.pad(adam_sq, (0, slots - count)).reshape(cap, n_dp)
-    adam_owned = lax.dynamic_slice_in_dim(adam_pad, me_dp, 1, 1)[:, 0]
+    totals = lax.psum(jnp.concatenate([jnp.sum(direction * direction, axis=(1, 2)), dp_sums]), "group")
+    direction_sq = totals[:cap]
+    adam_owned = totals[cap : 2 * cap]
+    norm_grad = totals[2 * cap :].reshape(local_norm.shape)
     ratio = jnp.sqrt(adam_owned / (direction_sq + EPS_GRAFT))
     scaled = (ratio[:, None, None] * direction).astype(jnp.bfloat16)
     block_step = to_keepers(scaled)[:count]

time: 652 us -> 623 us (0.956)
  blocking collectives: 98.1 us -> 72.2 us
    psum x2 -> x1, blocking collectives: 44.9 us -> 10.7 us  [on_device(): lax.psum(jnp.concatenate([jnp.sum(direction * direction, axis=(1, 2)), dp...]
    all_to_all x0 -> x1, blocking collectives: none -> 11.2 us  [on_device(): lax.all_to_all(jnp.concatenate([adam_rows, norm_rows], axis=1), 'dp', 0,...]
    all_to_all x5, waiting for transfers between devices: 159 us -> 152 us  [to_keepers(): lax.all_to_all(owned.reshape(n_slots, n_dp, rows, quarter), 'dp', 1, 1, t...]
where the time goes in v8:
time: 623 us; the launch traced here: 621 us
  waiting for transfers between devices  351 us (56%)
  local copies, waits for them, and re-layouts  73.1 us (12%)
  blocking collectives  72.2 us (12%)
  matrix products  41.7 us (7%)
  starting transfers between devices  38.3 us (6%)
  other arithmetic  31.1 us (5%)
  between operations  14.1 us (2%)
    all_to_all x5, waiting for transfers between devices, to_keepers(): lax.all_to_all(owned.reshape(n_slots, n_dp, rows, quarter), 'dp', 1, 1, t...  152 us
    all_to_all x3, waiting for transfers between devices, to_owners(): lax.all_to_all(padded.reshape(n_slots, n_dp, rows, quarter), 'dp', 1, 1,...  111 us
    reduce_scatter x2, waiting for transfers between devices, on_device(): lax.psum_scatter(partials[0, b0:b1], 'group', scatter_dimension=2, tiled=...  68.5 us
    all_to_all x1, blocking collectives, to_owners(): lax.all_to_all(padded.reshape(n_slots, n_dp, rows, quarter), 'dp', 1, 1,...  50.2 us
    squeeze x2, local copies, waits for them, and re-layouts, on_device(): partials[0, b0:b1]  24.6 us
    all_to_all x5, starting transfers between devices, to_keepers(): lax.all_to_all(owned.reshape(n_slots, n_dp, rows, quarter), 'dp', 1, 1, t...  22.3 us
    dot_general x1, matrix products, on_device(): jnp.einsum('cim,cmj->cij', full_left, half, preferred_element_type=jnp.fl...  17.7 us
    all_to_all x3, starting transfers between devices, to_owners(): lax.all_to_all(padded.reshape(n_slots, n_dp, rows, quarter), 'dp', 1, 1,...  15.8 us
  transfers between devices with their start and end apart: 13, of which 11 were waited for; matrix products, arithmetic and copies ran while one was open for 20% of the time, Pallas kernels for 0%

profile of v8, /device:TPU:0, one launch (start us, length us, event | category | flops | bytes accessed | tf_op | source)
XLA Modules:
  0.0 621.4 jit_solution(1482784461278332018)
XLA Ops:
  7.2 11.0 %slice_bitcast_fusion.1 = f32[22,128,1024]{2,1,0:T(8,128)} fusion(f32[1,54,128,1024]{3,2,1,0:T(8,128)} %param.8), kind=kLoop, calls=%fused_computation.5 | loop fusion | bytes 23068672 | tf_op jit(solution)/shard_map/squeeze | solution.py:50
  18.2 13.7 %slice_bitcast_fusion = f32[32,128,1024]{2,1,0:T(8,128)} fusion(f32[1,54,128,1024]{3,2,1,0:T(8,128)} %param.8), kind=kLoop, calls=%fused_computation | loop fusion | bytes 33554432 | tf_op jit(solution)/shard_map/squeeze | solution.py:50
  37.7 7.0 %all-to-all-start = ((bf16[7,8,128,256]{3,2,0,1:T(8,128)(2,1)}), bf16[7,8,128,256]{3,2,0,1:T(8,128)(2,1)}, u32[]{:S(2)}, u32[]{:S(2)}) async-start(bf16[7,8,128,256]{3,2,0,1:T(8,128)(2,1)} %copy.28), calls=%async_computation.1 | async-start | bytes 7340032 | tf_op jit(solution)/shard_map/all_to_all | solution.py:35
  44.7 68.5 %reduce-scatter.5.cloned.1.call-done = f32[22,128,256]{2,1,0:T(8,128)} async-done(((f32[22,128,1024]{2,1,0:T(8,128)}), f32[22,128,256]{2,1,0:T(8,128)}) %reduce-scatter.5.cloned.1.call-update) | async-done | bytes 2883600 | tf_op jit(solution)/shard_map/reduce_scatter | solution.py:50
  113.2 5.3 fusion.11
  120.0 6.6 %all-to-all-done = bf16[7,8,128,256]{3,2,0,1:T(8,128)(2,1)} async-done(((bf16[7,8,128,256]{3,2,0,1:T(8,128)(2,1)}), bf16[7,8,128,256]{3,2,0,1:T(8,128)(2,1)}, u32[]{:S(2)}, u32[]{:S(2)}) %all-to-all-start) | async-done | bytes 3670048 | tf_op jit(solution)/shard_map/all_to_all | solution.py:35
  126.6 4.4 all-to-all-start.4
  136.8 30.7 %all-to-all-done.4 = bf16[3,8,128,256]{3,2,0,1:T(8,128)(2,1)} async-done(((bf16[3,8,128,256]{3,2,0,1:T(8,128)(2,1)}), bf16[3,8,128,256]{3,2,0,1:T(8,128)(2,1)}, u32[]{:S(2)}, u32[]{:S(2)}) %all-to-all-start.4) | async-done | bytes 1572896 | tf_op jit(solution)/shard_map/all_to_all | solution.py:35
  167.5 4.5 all-to-all-start.1
  175.0 4.3 copy.29
  179.3 74.1 %all-to-all-done.1 = bf16[7,8,128,256]{3,2,0,1:T(8,128)(2,1)} async-done(((bf16[7,8,128,256]{3,2,0,1:T(8,128)(2,1)}), bf16[7,8,128,256]{3,2,0,1:T(8,128)(2,1)}, u32[]{:S(2)}, u32[]{:S(2)}) %all-to-all-start.1) | async-done | bytes 3670048 | tf_op jit(solution)/shard_map/all_to_all | solution.py:35
  253.4 4.5 copy.31
  257.8 7.9 %fusion.4 = (f32[32,128,256]{2,1,0:T(8,128)}, f32[32]{0:T(128)S(1)}, bf16[32,128,256]{2,1,0:T(8,128)(2,1)}) fusion(f32[32,128,256]{2,1,0:T(8,128)} %reduce-scatter.3.cloned.1.call-done, f32[54,128,256]{2,1,0:T(8,128)} %param.9), kind=kLoop, calls=%fused_computation.13 | loop fusion | flops 9437152 | bytes 14680192 | tf_op jit(solution)/shard_map/add | solution.py:53
  266.1 11.2 %all_to_all.54 = f32[8,1,4103]{2,1,0:T(1,128)S(1)} all-to-all(f32[8,1,4103]{2,1,0:T(1,128)S(1)} %all_to_all.35), channel_id=1, replica_groups=mesh['dp'=8,'group'=4] {'dp'}, dimensions={0} | all-to-all | bytes 262592 | tf_op jit(solution)/shard_map/all_to_all | solution.py:62
  279.2 50.2 %all_to_all.55 = bf16[4,8,128,256]{3,2,0,1:T(8,128)(2,1)S(1)} all-to-all(bf16[4,8,128,256]{3,2,0,1:T(8,128)(2,1)S(1)} %copy.33), channel_id=1, replica_groups=mesh['dp'=8,'group'=4] {'dp'}, dimensions={1} | all-to-all | bytes 4194304 | tf_op jit(solution)/shard_map/all_to_all | solution.py:35
  331.5 5.5 convolution_convert_fusion.1
  338.4 4.6 all-to-all-start.9
  342.9 5.2 convolution_convert_fusion.2
  349.4 29.3 %all-to-all-done.9 = bf16[3,8,128,256]{3,2,0,1:T(8,128)(2,1)} async-done(((bf16[3,8,128,256]{3,2,0,1:T(8,128)(2,1)}), bf16[3,8,128,256]{3,2,0,1:T(8,128)(2,1)}, u32[]{:S(2)}, u32[]{:S(2)}) %all-to-all-start.9) | async-done | bytes 1572896 | tf_op jit(solution)/shard_map/all_to_all | solution.py:40
  383.0 6.7 %all-gather.6.cloned.1.call-done = bf16[4,1024,1024]{2,1,0:T(8,128)(2,1)} async-done(((bf16[4,1024,256]{2,1,0:T(8,128)(2,1)}), bf16[4,1024,1024]{2,1,0:T(8,128)(2,1)}) %all-gather.6.cloned.1.call-update) | async-done | bytes 8388624 | tf_op jit(solution)/shard_map/all_gather | solution.py:70
  389.7 6.9 %convolution_convert_fusion = bf16[4,1024,256]{2,1,0:T(8,128)(2,1)S(1)} fusion(bf16[4,1024,1024]{2,1,0:T(8,128)(2,1)} %all-gather.6.cloned.1.call-done, bf16[4,1024,256]{2,1,0:T(8,128)(2,1)} %bitcast.41), kind=kOutput, calls=%fused_computation.22 | convolution fusion | flops 2148532224 | bytes 12582912 | tf_op jit(solution)/shard_map/cim,cij->cmj/dot_general | solution.py:73
  398.0 21.4 %all-to-all-done.7 = bf16[3,8,128,256]{3,2,0,1:T(8,128)(2,1)} async-done(((bf16[3,8,128,256]{3,2,0,1:T(8,128)(2,1)}), bf16[3,8,128,256]{3,2,0,1:T(8,128)(2,1)}, u32[]{:S(2)}, u32[]{:S(2)}) %all-to-all-start.7) | async-done | bytes 1572896 | tf_op jit(solution)/shard_map/all_to_all | solution.py:40
  419.5 4.3 all-to-all-start.8
  423.9 6.4 %fusion.14 = bf16[4,1024,256]{2,1,0:T(8,128)(2,1)S(1)} fusion(bf16[4,1024,1024]{2,1,0:T(8,128)(2,1)} %all-gather.6.cloned.1.call-done, s32[]{:T(128)S(6)} %select_n.4), kind=kOutput, calls=%fused_computation.21 | convolution fusion | flops 2148532224 | bytes 12582916 | tf_op jit(solution)/shard_map/cim,cjm->cij/dot_general | solution.py:72
  431.7 40.0 %all-to-all-done.8 = bf16[4,8,128,256]{3,2,0,1:T(8,128)(2,1)} async-done(((bf16[4,8,128,256]{3,2,0,1:T(8,128)(2,1)}), bf16[4,8,128,256]{3,2,0,1:T(8,128)(2,1)}, u32[]{:S(2)}, u32[]{:S(2)}) %all-to-all-start.8) | async-done | bytes 2097184 | tf_op jit(solution)/shard_map/all_to_all | solution.py:40
  471.7 4.3 all-to-all-start.6
  476.0 11.7 %all-gather.4.cloned.1.call-done = bf16[7,1024,1024]{2,1,0:T(8,128)(2,1)} async-done(((bf16[7,1024,256]{2,1,0:T(8,128)(2,1)}), bf16[7,1024,1024]{2,1,0:T(8,128)(2,1)}) %all-gather.4.cloned.1.call-update) | async-done | bytes 14680080 | tf_op jit(solution)/shard_map/all_gather | solution.py:81
  487.7 17.7 %multiply_reduce_fusion = (f32[7]{0:T(128)S(1)}, f32[7,1024,256]{2,1,0:T(8,128)}) fusion(bf16[7,1024,1024]{2,1,0:T(8,128)(2,1)} %all-gather.4.cloned.1.call-done, bf16[7,1024,256]{2,1,0:T(8,128)(2,1)} %bitcast.52, bf16[3,1024,1024]{2,1,0:T(8,128)(2,1)} %all-gather.8.cloned.1.call-done, bf16[4,1024,1024]{2,1,0:T(8,128)(2,1)} %all-gather.6.cloned.1.call-done), kind=kOutput, calls=%fused_computation.7 | convolution fusion | flops 7529037824 | bytes 40370204 | tf_op jit(solution)/shard_map/cim,cmj->cij/dot_general | solution.py:82
  505.5 10.7 %psum.7 = f32[4110]{0:T(1024)S(1)} all-reduce(f32[4110]{0:T(1024)S(1)} %pad_maximum_fusion.2), channel_id=1, replica_groups=mesh['dp'=8,'group'=4] {'group'}, use_global_device_ids=true, to_apply=%region_6.7 | all-reduce | flops 4110 | bytes 32880 | tf_op jit(solution)/shard_map/psum | solution.py:83
  523.8 4.7 all-to-all-start.5
  528.6 5.8 pad_maximum_fusion
  550.3 59.9 %all-to-all-done.5 = bf16[7,8,128,256]{3,2,0,1:T(8,128)(2,1)} async-done(((bf16[7,8,128,256]{3,2,0,1:T(8,128)(2,1)}), bf16[7,8,128,256]{3,2,0,1:T(8,128)(2,1)}, u32[]{:S(2)}, u32[]{:S(2)}) %all-to-all-start.5) | async-done | bytes 3670048 | tf_op jit(solution)/shard_map/all_to_all | solution.py:40
  (68 shorter events, 58.3 us)
Async XLA Ops:
  7.2 106.1 %reduce-scatter.5.cloned.1.call-start = ((), (), s32[]{:S(2)}) async-start(), calls=%async_computation.14 | async-start | bytes 14417920 | tf_op jit(solution)/shard_map/reduce_scatter | solution.py:50
  18.2 239.7 %reduce-scatter.3.cloned.1.call-start = ((), (), s32[]{:S(2)}) async-start(), calls=%async_computation.12 | async-start | bytes 20971520 | tf_op jit(solution)/shard_map/reduce_scatter | solution.py:50
  31.9 2.8 copy-start
  37.7 88.8 %all-to-all-start = ((bf16[7,8,128,256]{3,2,0,1:T(8,128)(2,1)}), bf16[7,8,128,256]{3,2,0,1:T(8,128)(2,1)}, u32[]{:S(2)}, u32[]{:S(2)}) async-start(bf16[7,8,128,256]{3,2,0,1:T(8,128)(2,1)} %copy.28), calls=%async_computation.1 | async-start | bytes 7340032 | tf_op jit(solution)/shard_map/all_to_all | solution.py:35
  126.6 40.9 %all-to-all-start.4 = ((bf16[3,8,128,256]{3,2,0,1:T(8,128)(2,1)}), bf16[3,8,128,256]{3,2,0,1:T(8,128)(2,1)}, u32[]{:S(2)}, u32[]{:S(2)}) async-start(bf16[3,8,128,256]{3,2,0,1:T(8,128)(2,1)} %copy.35), calls=%async_computation.6 | async-start | bytes 3145728 | tf_op jit(solution)/shard_map/all_to_all | solution.py:35
  167.5 85.9 %all-to-all-start.1 = ((bf16[7,8,128,256]{3,2,0,1:T(8,128)(2,1)}), bf16[7,8,128,256]{3,2,0,1:T(8,128)(2,1)}, u32[]{:S(2)}, u32[]{:S(2)}) async-start(bf16[7,8,128,256]{3,2,0,1:T(8,128)(2,1)} %copy.30), calls=%async_computation.2 | async-start | bytes 7340032 | tf_op jit(solution)/shard_map/all_to_all | solution.py:35
  172.0 2.9 copy-start.1
  172.0 159.5 %all-gather.8.cloned.1.call-start = ((), (), s32[]{:S(2)}) async-start(), calls=%async_computation.16 | async-start | bytes 7864320 | tf_op jit(solution)/shard_map/all_gather | solution.py:70
  174.8 214.9 %all-gather.6.cloned.1.call-start = ((), (), s32[]{:S(2)}) async-start(), calls=%async_computation.15 | async-start | bytes 10485760 | tf_op jit(solution)/shard_map/all_gather | solution.py:70
  330.9 156.8 %all-gather.4.cloned.1.call-start = ((), (), s32[]{:S(2)}) async-start(), calls=%async_computation.13 | async-start | bytes 18350080 | tf_op jit(solution)/shard_map/all_gather | solution.py:81
  338.4 40.3 %all-to-all-start.9 = ((bf16[3,8,128,256]{3,2,0,1:T(8,128)(2,1)}), bf16[3,8,128,256]{3,2,0,1:T(8,128)(2,1)}, u32[]{:S(2)}, u32[]{:S(2)}) async-start(bf16[3,8,128,256]{3,2,0,1:T(8,128)(2,1)} %copy.47), calls=%async_computation.11 | async-start | bytes 3145728 | tf_op jit(solution)/shard_map/all_to_all | solution.py:40
  378.7 40.8 %all-to-all-start.7 = ((bf16[3,8,128,256]{3,2,0,1:T(8,128)(2,1)}), bf16[3,8,128,256]{3,2,0,1:T(8,128)(2,1)}, u32[]{:S(2)}, u32[]{:S(2)}) async-start(bf16[3,8,128,256]{3,2,0,1:T(8,128)(2,1)} %copy.41), calls=%async_computation.9 | async-start | bytes 3145728 | tf_op jit(solution)/shard_map/all_to_all | solution.py:40
  419.5 52.2 %all-to-all-start.8 = ((bf16[4,8,128,256]{3,2,0,1:T(8,128)(2,1)}), bf16[4,8,128,256]{3,2,0,1:T(8,128)(2,1)}, u32[]{:S(2)}, u32[]{:S(2)}) async-start(bf16[4,8,128,256]{3,2,0,1:T(8,128)(2,1)} %copy.44), calls=%async_computation.10 | async-start | bytes 4194304 | tf_op jit(solution)/shard_map/all_to_all | solution.py:40
  471.7 52.2 %all-to-all-start.6 = ((bf16[4,8,128,256]{3,2,0,1:T(8,128)(2,1)}), bf16[4,8,128,256]{3,2,0,1:T(8,128)(2,1)}, u32[]{:S(2)}, u32[]{:S(2)}) async-start(bf16[4,8,128,256]{3,2,0,1:T(8,128)(2,1)} %copy.39), calls=%async_computation.8 | async-start | bytes 4194304 | tf_op jit(solution)/shard_map/all_to_all | solution.py:40
  523.8 86.3 %all-to-all-start.5 = ((bf16[7,8,128,256]{3,2,0,1:T(8,128)(2,1)}), bf16[7,8,128,256]{3,2,0,1:T(8,128)(2,1)}, u32[]{:S(2)}, u32[]{:S(2)}) async-start(bf16[7,8,128,256]{3,2,0,1:T(8,128)(2,1)} %copy.37), calls=%async_computation.7 | async-start | bytes 7340032 | tf_op jit(solution)/shard_map/all_to_all | solution.py:40
  536.0 6.2 slice-start
  537.8 4.4 slice-start.1
  537.8 8.0 %slice-start.2 = ((s8[7077888]{0:T(1024)(128)(4,1)}), s8[4194304]{0:T(1024)(128)(4,1)S(1)}, s32[]{:S(2)}) async-start(s8[7077888]{0:T(1024)(128)(4,1)} %bitcast.45), calls=%async_computation.19 | async-start | bytes 8388608
  542.2 3.7 slice-start.3
  545.9 3.7 copy-start.2
Sparse Core Ops, SparseCore 0:
  18.3 94.8 reduce-scatter.4
  115.8 126.1 reduce-scatter.2
  243.6 47.2 all-gather.7
  331.0 58.5 all-gather.5
  391.7 95.9 all-gather.3

commit v9 on v4

--- a/solution.py
+++ b/solution.py
@@ -30,10 +30,19 @@
     split = (cap + 1) // 2
     bounds = [(0, split), (split, cap)] if cap > 1 else [(0, cap)]
 
+    def pad_slots(blocks, n_slots):
+        return jnp.pad(blocks, ((0, n_slots * n_dp - blocks.shape[0]), (0, 0), (0, 0)))
+
     def to_owners(blocks, n_slots):
-        padded = jnp.pad(blocks, ((0, n_slots * n_dp - blocks.shape[0]), (0, 0), (0, 0)))
+        padded = pad_slots(blocks, n_slots)
         sent = lax.all_to_all(padded.reshape(n_slots, n_dp, rows, quarter), "dp", 1, 1, tiled=True)
         return sent.reshape(n_slots, width, quarter)
+
+    def gather_columns(mine):
+        n_group = lax.axis_size("group")
+        spread = jnp.broadcast_to(mine[None], (n_group,) + mine.shape)
+        got = lax.all_to_all(spread, "group", 0, 0, tiled=True)
+        return got.transpose(1, 2, 0, 3).reshape(mine.shape[0], width, n_group * quarter)
 
     def to_keepers(owned):
         n_slots = owned.shape[0]
@@ -44,37 +53,72 @@
     right_root = to_owners(right_roots, cap)
     local_norm = norm_partials[0, 0]
 
-    moments, adam_parts, left_terms, right_terms, pieces = [], [], [], [], []
-    for index, (s0, s1) in enumerate(bounds):
+    def chunk_grad(s0, s1):
         b0, b1 = s0 * n_dp, min(s1 * n_dp, count)
-        grad = lax.psum_scatter(partials[0, b0:b1], "group", scatter_dimension=2, tiled=True)
-        if index == 0:
-            grad, left_root, right_root = lax.optimization_barrier((grad, left_root, right_root))
+        return lax.psum_scatter(partials[0, b0:b1], "group", scatter_dimension=2, tiled=True)
+
+    def chunk_terms(grad, s0, s1):
+        b0, b1 = s0 * n_dp, min(s1 * n_dp, count)
         new_moment = 0.99 * second_moment[b0:b1] + 0.01 * grad * grad
         adam = grad / (jnp.sqrt(new_moment) + EPS_ADAM)
-        adam_parts.append(jnp.sum(adam * adam, axis=(1, 2)))
-        moments.append(new_moment)
-        mine = to_owners(grad.astype(jnp.bfloat16), s1 - s0)
-        piece = lax.all_gather(mine, "group", axis=2, tiled=True)
+        return new_moment, jnp.sum(adam * adam, axis=(1, 2)), grad.astype(jnp.bfloat16)
+
+    def chunk_grams(piece, mine, s0, s1):
+        b0, b1 = s0 * n_dp, min(s1 * n_dp, count)
         own_rows = lax.dynamic_slice_in_dim(piece, lower, quarter, 1)
         gram_left = jnp.einsum("cim,cjm->cij", piece, own_rows, preferred_element_type=jnp.float32)
         gram_right = jnp.einsum("cim,cij->cmj", piece, mine, preferred_element_type=jnp.float32)
-        left_terms.append(to_keepers(gram_left.astype(jnp.bfloat16))[: b1 - b0])
-        right_terms.append(to_keepers(gram_right.astype(jnp.bfloat16))[: b1 - b0])
-        pieces.append(piece)
+        left = to_keepers(gram_left.astype(jnp.bfloat16))[: b1 - b0]
+        right = to_keepers(gram_right.astype(jnp.bfloat16))[: b1 - b0]
+        return left, right
 
-    norm_grad, adam_sq = lax.psum((local_norm, jnp.concatenate(adam_parts)), ("dp", "group"))
+    (a0, a1) = bounds[0]
+    if len(bounds) > 1:
+        (c0, c1) = bounds[1]
+        moment_b, adam_b, low_b = chunk_terms(chunk_grad(c0, c1), c0, c1)
+        mine_b = to_owners(low_b, c1 - c0)
+        piece_b = gather_columns(mine_b)
+        grad_a = chunk_grad(a0, a1)
+        grad_a, left_root, right_root, piece_b = lax.optimization_barrier((grad_a, left_root, right_root, piece_b))
+    else:
+        grad_a = chunk_grad(a0, a1)
+        grad_a, left_root, right_root = lax.optimization_barrier((grad_a, left_root, right_root))
+    moment_a, adam_a, low_a = chunk_terms(grad_a, a0, a1)
+    moments, adam_parts = [moment_a], [adam_a]
+    if len(bounds) > 1:
+        moments.append(moment_b)
+        adam_parts.append(adam_b)
+
+    adam_cat = jnp.pad(jnp.concatenate(adam_parts), (0, slots - count))
+    adam_rows = adam_cat.reshape(cap, n_dp).T
+    norm_rows = jnp.broadcast_to(local_norm.reshape(1, -1), (n_dp, local_norm.size))
+    sent = lax.all_to_all(jnp.concatenate([adam_rows, norm_rows], axis=1), "dp", 0, 0, tiled=True)
+    dp_sums = jnp.sum(sent, axis=0)
+    dp_sums, low_a = lax.optimization_barrier((dp_sums, low_a))
+
+    mine_a = to_owners(low_a, a1 - a0)
+    piece_a = lax.all_gather(mine_a, "group", axis=2, tiled=True)
+    left_a, right_a = chunk_grams(piece_a, mine_a, a0, a1)
+    pieces, left_terms, right_terms = [piece_a], [left_a], [right_a]
+    if len(bounds) > 1:
+        left_b, right_b = chunk_grams(piece_b, mine_b, c0, c1)
+        pieces.append(piece_b)
+        left_terms.append(left_b)
+        right_terms.append(right_b)
+
     piece = jnp.concatenate(pieces) if len(pieces) > 1 else pieces[0]
     half = jnp.einsum("cim,cmj->cij", piece, right_root, preferred_element_type=jnp.float32)
     half = half.astype(jnp.bfloat16)
     full_left = lax.all_gather(left_root, "group", axis=2, tiled=True)
     direction = jnp.einsum("cim,cmj->cij", full_left, half, preferred_element_type=jnp.float32)
-    direction_sq = lax.psum(jnp.sum(direction * direction, axis=(1, 2)), "group")
-    adam_pad = jnp.pad(adam_sq, (0, slots - count)).reshape(cap, n_dp)
-    adam_owned = lax.dynamic_slice_in_dim(adam_pad, me_dp, 1, 1)[:, 0]
+    totals = lax.psum(jnp.concatenate([jnp.sum(direction * direction, axis=(1, 2)), dp_sums[:cap]]), "group")
+    direction_sq = totals[:cap]
+    adam_owned = totals[cap:]
     ratio = jnp.sqrt(adam_owned / (direction_sq + EPS_GRAFT))
     scaled = (ratio[:, None, None] * direction).astype(jnp.bfloat16)
+    scaled, norm_dp = lax.optimization_barrier((scaled, dp_sums[cap:]))
     block_step = to_keepers(scaled)[:count]
+    norm_grad = lax.psum(norm_dp, "group").reshape(local_norm.shape)
 
     new_moment = jnp.concatenate(moments)
     left_term = jnp.concatenate(left_terms).astype(jnp.float32)

time: 662 us -> 704 us (1.063)
  waiting for transfers between devices: 338 us -> 410 us
  blocking collectives: 127 us -> 77.4 us
  local copies, waits for them, and re-layouts: 71.5 us -> 84 us
    all_to_all x0 -> x1, waiting for transfers between devices: none -> 62 us  [gather_columns(): got = lax.all_to_all(spread, 'group', 0, 0, tiled=True)]
    psum x2, blocking collectives: 74.5 us -> 17.2 us  [the longest x1 10.9 us: on_device(): norm_grad = lax.psum(norm_dp, 'group').reshape(local_norm.shape)]
    all_to_all x0 -> x1, blocking collectives: none -> 10.8 us  [on_device(): lax.all_to_all(jnp.concatenate([adam_rows, norm_rows], axis=1), 'dp', 0,...]
    all_gather x1, waiting for transfers between devices: 0.02 us -> 10.3 us  [on_device(): full_left = lax.all_gather(left_root, 'group', axis=2, tiled=True)]
  transfers between devices with their start and end apart: 13 -> 13, of which waited for: 9 -> 12; matrix products, arithmetic and copies ran while one was open for 19% -> 18% of each run, Pallas kernels for 0% -> 0%
where the time goes in v9:
time: 704 us; the launch traced here: 703 us
  waiting for transfers between devices  410 us (58%)
  local copies, waits for them, and re-layouts  84 us (12%)
  blocking collectives  77.4 us (11%)
  starting transfers between devices  43.6 us (6%)
  matrix products  41.7 us (6%)
  other arithmetic  31.5 us (4%)
  between operations  14.1 us (2%)
    all_to_all x5, waiting for transfers between devices, to_keepers(): lax.all_to_all(owned.reshape(n_slots, n_dp, rows, quarter), 'dp', 1, 1, t...  148 us
    all_to_all x3, waiting for transfers between devices, to_owners(): lax.all_to_all(padded.reshape(n_slots, n_dp, rows, quarter), 'dp', 1, 1,...  116 us
    reduce_scatter x2, waiting for transfers between devices, chunk_grad(): lax.psum_scatter(partials[0, b0:b1], 'group', scatter_dimension=2, tiled=...  68.5 us
    all_to_all x1, waiting for transfers between devices, gather_columns(): got = lax.all_to_all(spread, 'group', 0, 0, tiled=True)  62 us
    all_to_all x1, blocking collectives, to_owners(): lax.all_to_all(padded.reshape(n_slots, n_dp, rows, quarter), 'dp', 1, 1,...  49.4 us
    squeeze x2, local copies, waits for them, and re-layouts, chunk_grad(): partials[0, b0:b1]  24.7 us
    all_to_all x5, starting transfers between devices, to_keepers(): lax.all_to_all(owned.reshape(n_slots, n_dp, rows, quarter), 'dp', 1, 1, t...  22 us
    dot_general x1, matrix products, on_device(): jnp.einsum('cim,cmj->cij', full_left, half, preferred_element_type=jnp.fl...  17.7 us
  transfers between devices with their start and end apart: 13, of which 12 were waited for; matrix products, arithmetic and copies ran while one was open for 18% of the time, Pallas kernels for 0%

profile of v9, /device:TPU:0, one launch (start us, length us, event | category | flops | bytes accessed | tf_op | source)
XLA Modules:
  0.0 702.8 jit_solution(2795005093535610791)
XLA Ops:
  7.2 11.1 %slice_bitcast_fusion.1 = f32[22,128,1024]{2,1,0:T(8,128)} fusion(f32[1,54,128,1024]{3,2,1,0:T(8,128)} %param.8), kind=kLoop, calls=%fused_computation.5 | loop fusion | bytes 23068672 | tf_op jit(solution)/shard_map/squeeze | solution.py:58
  18.4 13.7 %slice_bitcast_fusion = f32[32,128,1024]{2,1,0:T(8,128)} fusion(f32[1,54,128,1024]{3,2,1,0:T(8,128)} %param.8), kind=kLoop, calls=%fused_computation | loop fusion | bytes 33554432 | tf_op jit(solution)/shard_map/squeeze | solution.py:58
  37.8 7.0 all-to-all-start
  44.8 68.5 %reduce-scatter.5.cloned.1.call-done = f32[22,128,256]{2,1,0:T(8,128)} async-done(((f32[22,128,1024]{2,1,0:T(8,128)}), f32[22,128,256]{2,1,0:T(8,128)}) %reduce-scatter.5.cloned.1.call-update) | async-done | bytes 2883600 | tf_op jit(solution)/shard_map/reduce_scatter | solution.py:58
  113.3 5.3 fusion.11
  120.1 6.6 all-to-all-done
  137.0 30.7 %all-to-all-done.2 = bf16[3,8,128,256]{3,2,0,1:T(8,128)(2,1)} async-done(((bf16[3,8,128,256]{3,2,0,1:T(8,128)(2,1)}), bf16[3,8,128,256]{3,2,0,1:T(8,128)(2,1)}, u32[]{:S(2)}, u32[]{:S(2)}) %all-to-all-start.2) | async-done | bytes 1572896 | tf_op jit(solution)/shard_map/all_to_all | solution.py:38
  167.6 4.5 all-to-all-start.1
  174.8 78.6 %all-to-all-done.1 = bf16[7,8,128,256]{3,2,0,1:T(8,128)(2,1)} async-done(((bf16[7,8,128,256]{3,2,0,1:T(8,128)(2,1)}), bf16[7,8,128,256]{3,2,0,1:T(8,128)(2,1)}, u32[]{:S(2)}, u32[]{:S(2)}) %all-to-all-start.1) | async-done | bytes 3670048 | tf_op jit(solution)/shard_map/all_to_all | solution.py:38
  253.5 4.7 broadcast_in_dim.16
  258.1 5.4 all-to-all-start.3
  272.2 62.0 %all-to-all-done.3 = bf16[4,3,1024,256]{3,2,1,0:T(8,128)(2,1)} async-done(((bf16[4,3,1024,256]{3,2,1,0:T(8,128)(2,1)}), bf16[4,3,1024,256]{3,2,1,0:T(8,128)(2,1)}, u32[]{:S(2)}, u32[]{:S(2)}) %all-to-all-start.3) | async-done | bytes 6291488 | tf_op jit(solution)/shard_map/all_to_all | solution.py:44
  334.2 6.4 copy.53
  340.6 8.3 %fusion.4 = (f32[32,128,256]{2,1,0:T(8,128)}, f32[32]{0:T(128)S(1)}, bf16[32,128,256]{2,1,0:T(8,128)(2,1)}) fusion(f32[32,128,256]{2,1,0:T(8,128)} %reduce-scatter.3.cloned.1.call-done, f32[54,128,256]{2,1,0:T(8,128)} %param.9), kind=kLoop, calls=%fused_computation.13 | loop fusion | flops 9437152 | bytes 14680192 | tf_op jit(solution)/shard_map/add | solution.py:62
  349.3 10.8 %all_to_all.59 = f32[8,1,4103]{2,1,0:T(1,128)S(1)} all-to-all(f32[8,1,4103]{2,1,0:T(1,128)S(1)} %all_to_all.40), channel_id=1, replica_groups=mesh['dp'=8,'group'=4] {'dp'}, dimensions={0} | all-to-all | bytes 262592 | tf_op jit(solution)/shard_map/all_to_all | solution.py:95
  362.0 49.4 %all_to_all.60 = bf16[4,8,128,256]{3,2,0,1:T(8,128)(2,1)S(1)} all-to-all(bf16[4,8,128,256]{3,2,0,1:T(8,128)(2,1)S(1)} %copy.37), channel_id=1, replica_groups=mesh['dp'=8,'group'=4] {'dp'}, dimensions={1} | all-to-all | bytes 4194304 | tf_op jit(solution)/shard_map/all_to_all | solution.py:38
  413.5 5.5 convolution_convert_fusion.1
  424.6 5.2 convolution_convert_fusion.2
  431.1 29.6 %all-to-all-done.10 = bf16[3,8,128,256]{3,2,0,1:T(8,128)(2,1)} async-done(((bf16[3,8,128,256]{3,2,0,1:T(8,128)(2,1)}), bf16[3,8,128,256]{3,2,0,1:T(8,128)(2,1)}, u32[]{:S(2)}, u32[]{:S(2)}) %all-to-all-start.10) | async-done | bytes 1572896 | tf_op jit(solution)/shard_map/all_to_all | solution.py:49
  465.0 5.5 all-gather.5.cloned.1.call-done
  470.5 6.9 convolution_convert_fusion
  479.0 22.5 %all-to-all-done.8 = bf16[3,8,128,256]{3,2,0,1:T(8,128)(2,1)} async-done(((bf16[3,8,128,256]{3,2,0,1:T(8,128)(2,1)}), bf16[3,8,128,256]{3,2,0,1:T(8,128)(2,1)}, u32[]{:S(2)}, u32[]{:S(2)}) %all-to-all-start.8) | async-done | bytes 1572896 | tf_op jit(solution)/shard_map/all_to_all | solution.py:49
  505.8 6.4 fusion.14
  513.6 40.0 %all-to-all-done.9 = bf16[4,8,128,256]{3,2,0,1:T(8,128)(2,1)} async-done(((bf16[4,8,128,256]{3,2,0,1:T(8,128)(2,1)}), bf16[4,8,128,256]{3,2,0,1:T(8,128)(2,1)}, u32[]{:S(2)}, u32[]{:S(2)}) %all-to-all-start.9) | async-done | bytes 2097184 | tf_op jit(solution)/shard_map/all_to_all | solution.py:49
  553.6 4.6 all-to-all-start.7
  558.3 10.3 %all-gather.3.cloned.1.call-done = bf16[7,1024,1024]{2,1,0:T(8,128)(2,1)} async-done(((bf16[7,1024,256]{2,1,0:T(8,128)(2,1)}), bf16[7,1024,1024]{2,1,0:T(8,128)(2,1)}) %all-gather.3.cloned.1.call-update) | async-done | bytes 14680080 | tf_op jit(solution)/shard_map/all_gather | solution.py:112
  568.6 17.7 %multiply_reduce_fusion = (f32[7]{0:T(128)S(1)}, f32[7,1024,256]{2,1,0:T(8,128)}) fusion(bf16[7,1024,1024]{2,1,0:T(8,128)(2,1)} %all-gather.3.cloned.1.call-done, bf16[7,1024,256]{2,1,0:T(8,128)(2,1)} %bitcast.58, bf16[3,1024,1024]{2,1,0:T(8,128)(2,1)} %bitcast.52, bf16[4,1024,1024]{2,1,0:T(8,128)(2,1)} %all-gather.5.cloned.1.call-done), kind=kOutput, calls=%fused_computation.7 | convolution fusion | flops 7529037824 | bytes 40370204 | tf_op jit(solution)/shard_map/cim,cmj->cij/dot_general | solution.py:113
  586.4 6.3 psum.14
  598.8 7.1 %all-to-all-done.7 = bf16[4,8,128,256]{3,2,0,1:T(8,128)(2,1)} async-done(((bf16[4,8,128,256]{3,2,0,1:T(8,128)(2,1)}), bf16[4,8,128,256]{3,2,0,1:T(8,128)(2,1)}, u32[]{:S(2)}, u32[]{:S(2)}) %all-to-all-start.7) | async-done | bytes 2097184 | tf_op jit(solution)/shard_map/all_to_all | solution.py:49
  610.4 5.8 pad_maximum_fusion
  631.4 10.9 %psum.15 = f32[2,2048]{1,0:T(2,128)S(1)} all-reduce(f32[2,2048]{1,0:T(2,128)S(1)} %reshape.97), channel_id=1, replica_groups=mesh['dp'=8,'group'=4] {'group'}, use_global_device_ids=true, to_apply=%region_7.8 | all-reduce | flops 4096 | bytes 32768 | tf_op jit(solution)/shard_map/psum | solution.py:121
  643.0 48.7 %all-to-all-done.6 = bf16[7,8,128,256]{3,2,0,1:T(8,128)(2,1)} async-done(((bf16[7,8,128,256]{3,2,0,1:T(8,128)(2,1)}), bf16[7,8,128,256]{3,2,0,1:T(8,128)(2,1)}, u32[]{:S(2)}, u32[]{:S(2)}) %all-to-all-start.6) | async-done | bytes 3670048 | tf_op jit(solution)/shard_map/all_to_all | solution.py:49
  (74 shorter events, 82.9 us)
Async XLA Ops:
  7.2 106.2 %reduce-scatter.5.cloned.1.call-start = ((), (), s32[]{:S(2)}) async-start(), calls=%async_computation.14 | async-start | bytes 14417920 | tf_op jit(solution)/shard_map/reduce_scatter | solution.py:58
  18.3 322.3 %reduce-scatter.3.cloned.1.call-start = ((), (), s32[]{:S(2)}) async-start(), calls=%async_computation.13 | async-start | bytes 20971520 | tf_op jit(solution)/shard_map/reduce_scatter | solution.py:58
  32.0 2.8 copy-start
  37.8 88.8 %all-to-all-start = ((bf16[7,8,128,256]{3,2,0,1:T(8,128)(2,1)}), bf16[7,8,128,256]{3,2,0,1:T(8,128)(2,1)}, u32[]{:S(2)}, u32[]{:S(2)}) async-start(bf16[7,8,128,256]{3,2,0,1:T(8,128)(2,1)} %copy.29), calls=%async_computation.1 | async-start | bytes 7340032 | tf_op jit(solution)/shard_map/all_to_all | solution.py:38
  126.7 40.9 %all-to-all-start.2 = ((bf16[3,8,128,256]{3,2,0,1:T(8,128)(2,1)}), bf16[3,8,128,256]{3,2,0,1:T(8,128)(2,1)}, u32[]{:S(2)}, u32[]{:S(2)}) async-start(bf16[3,8,128,256]{3,2,0,1:T(8,128)(2,1)} %copy.33), calls=%async_computation.4 | async-start | bytes 3145728 | tf_op jit(solution)/shard_map/all_to_all | solution.py:38
  167.6 85.9 %all-to-all-start.1 = ((bf16[7,8,128,256]{3,2,0,1:T(8,128)(2,1)}), bf16[7,8,128,256]{3,2,0,1:T(8,128)(2,1)}, u32[]{:S(2)}, u32[]{:S(2)}) async-start(bf16[7,8,128,256]{3,2,0,1:T(8,128)(2,1)} %copy.31), calls=%async_computation.2 | async-start | bytes 7340032 | tf_op jit(solution)/shard_map/all_to_all | solution.py:38
  258.1 5.4 copy-start.2
  258.1 76.1 %all-to-all-start.3 = ((bf16[4,3,1024,256]{3,2,1,0:T(8,128)(2,1)}), bf16[4,3,1024,256]{3,2,1,0:T(8,128)(2,1)}, u32[]{:S(2)}, u32[]{:S(2)}) async-start(bf16[4,3,1024,256]{3,2,1,0:T(8,128)(2,1)} %broadcast_in_dim.16), calls=%async_computation.5 | async-start | bytes 12582912 | tf_op jit(solution)/shard_map/all_to_all | solution.py:44
  263.5 207.0 %all-gather.5.cloned.1.call-start = ((), (), s32[]{:S(2)}) async-start(), calls=%async_computation.16 | async-start | bytes 10485760 | tf_op jit(solution)/shard_map/all_gather | solution.py:100
  360.2 198.0 %copy-start.1 = (f32[4103]{0:T(1024)}, f32[4103]{0:T(1024)S(1)}, u32[]{:S(2)}) copy-start(f32[4103]{0:T(1024)S(1)} %reduce_sum.38) | copy-start | bytes 49240
  412.9 155.7 %all-gather.3.cloned.1.call-start = ((), (), s32[]{:S(2)}) async-start(), calls=%async_computation.15 | async-start | bytes 18350080 | tf_op jit(solution)/shard_map/all_gather | solution.py:112
  420.3 40.4 %all-to-all-start.10 = ((bf16[3,8,128,256]{3,2,0,1:T(8,128)(2,1)}), bf16[3,8,128,256]{3,2,0,1:T(8,128)(2,1)}, u32[]{:S(2)}, u32[]{:S(2)}) async-start(bf16[3,8,128,256]{3,2,0,1:T(8,128)(2,1)} %copy.49), calls=%async_computation.12 | async-start | bytes 3145728 | tf_op jit(solution)/shard_map/all_to_all | solution.py:49
  460.7 40.8 %all-to-all-start.8 = ((bf16[3,8,128,256]{3,2,0,1:T(8,128)(2,1)}), bf16[3,8,128,256]{3,2,0,1:T(8,128)(2,1)}, u32[]{:S(2)}, u32[]{:S(2)}) async-start(bf16[3,8,128,256]{3,2,0,1:T(8,128)(2,1)} %copy.43), calls=%async_computation.10 | async-start | bytes 3145728 | tf_op jit(solution)/shard_map/all_to_all | solution.py:49
  501.5 52.2 %all-to-all-start.9 = ((bf16[4,8,128,256]{3,2,0,1:T(8,128)(2,1)}), bf16[4,8,128,256]{3,2,0,1:T(8,128)(2,1)}, u32[]{:S(2)}, u32[]{:S(2)}) async-start(bf16[4,8,128,256]{3,2,0,1:T(8,128)(2,1)} %copy.46), calls=%async_computation.11 | async-start | bytes 4194304 | tf_op jit(solution)/shard_map/all_to_all | solution.py:49
  553.6 52.3 %all-to-all-start.7 = ((bf16[4,8,128,256]{3,2,0,1:T(8,128)(2,1)}), bf16[4,8,128,256]{3,2,0,1:T(8,128)(2,1)}, u32[]{:S(2)}, u32[]{:S(2)}) async-start(bf16[4,8,128,256]{3,2,0,1:T(8,128)(2,1)} %copy.41), calls=%async_computation.9 | async-start | bytes 4194304 | tf_op jit(solution)/shard_map/all_to_all | solution.py:49
  558.3 28.1 %slice-start.4 = ((f32[4103]{0:T(1024)}), f32[7]{0:T(128)S(1)}, s32[]{:S(2)}) async-start(f32[4103]{0:T(1024)} %copy-done.1), calls=%async_computation.21 | async-start | bytes 1024 | tf_op jit(solution)/shard_map/slice | solution.py:114
  605.9 85.8 %all-to-all-start.6 = ((bf16[7,8,128,256]{3,2,0,1:T(8,128)(2,1)}), bf16[7,8,128,256]{3,2,0,1:T(8,128)(2,1)}, u32[]{:S(2)}, u32[]{:S(2)}) async-start(bf16[7,8,128,256]{3,2,0,1:T(8,128)(2,1)} %copy.39), calls=%async_computation.8 | async-start | bytes 7340032 | tf_op jit(solution)/shard_map/all_to_all | solution.py:49
  617.8 6.2 slice-start
  619.7 4.4 slice-start.1
  619.7 8.0 %slice-start.2 = ((s8[7077888]{0:T(1024)(128)(4,1)}), s8[4194304]{0:T(1024)(128)(4,1)S(1)}, s32[]{:S(2)}) async-start(s8[7077888]{0:T(1024)(128)(4,1)} %bitcast.48), calls=%async_computation.19 | async-start | bytes 8388608
  624.1 3.7 slice-start.3
  627.7 14.6 %copy-start.3 = (f32[2,2048]{1,0:T(2,128)S(1)}, f32[2,2048]{1,0:T(2,128)}, u32[]{:S(2)}) copy-start(f32[2,2048]{1,0:T(2,128)} %param.15) | copy-start | bytes 49156
Sparse Core Ops, SparseCore 0:
  18.4 94.8 reduce-scatter.4
  115.9 126.1 reduce-scatter.2
  413.0 57.4 all-gather.4
  472.6 95.9 all-gather.2

commit v10 on v8

--- a/solution.py
+++ b/solution.py
@@ -61,13 +61,14 @@
     norm_rows = jnp.broadcast_to(local_norm.reshape(1, -1), (n_dp, local_norm.size))
     sent = lax.all_to_all(jnp.concatenate([adam_rows, norm_rows], axis=1), "dp", 0, 0, tiled=True)
     dp_sums = jnp.sum(sent, axis=0)
-    dp_sums, grads[0] = lax.optimization_barrier((dp_sums, grads[0]))
 
     left_terms, right_terms, pieces = [], [], []
     for (s0, s1), grad_low in zip(bounds, grads):
         b0, b1 = s0 * n_dp, min(s1 * n_dp, count)
         mine = to_owners(grad_low, s1 - s0)
         piece = lax.all_gather(mine, "group", axis=2, tiled=True)
+        if s0 == 0:
+            dp_sums, piece = lax.optimization_barrier((dp_sums, piece))
         own_rows = lax.dynamic_slice_in_dim(piece, lower, quarter, 1)
         gram_left = jnp.einsum("cim,cjm->cij", piece, own_rows, preferred_element_type=jnp.float32)
         gram_right = jnp.einsum("cim,cij->cmj", piece, mine, preferred_element_type=jnp.float32)
@@ -80,13 +81,14 @@
     half = half.astype(jnp.bfloat16)
     full_left = lax.all_gather(left_root, "group", axis=2, tiled=True)
     direction = jnp.einsum("cim,cmj->cij", full_left, half, preferred_element_type=jnp.float32)
-    totals = lax.psum(jnp.concatenate([jnp.sum(direction * direction, axis=(1, 2)), dp_sums]), "group")
+    totals = lax.psum(jnp.concatenate([jnp.sum(direction * direction, axis=(1, 2)), dp_sums[:cap]]), "group")
     direction_sq = totals[:cap]
-    adam_owned = totals[cap : 2 * cap]
-    norm_grad = totals[2 * cap :].reshape(local_norm.shape)
+    adam_owned = totals[cap:]
     ratio = jnp.sqrt(adam_owned / (direction_sq + EPS_GRAFT))
     scaled = (ratio[:, None, None] * direction).astype(jnp.bfloat16)
+    scaled, norm_dp = lax.optimization_barrier((scaled, dp_sums[cap:]))
     block_step = to_keepers(scaled)[:count]
+    norm_grad = lax.psum(norm_dp, "group").reshape(local_norm.shape)
 
     new_moment = jnp.concatenate(moments)
     left_term = jnp.concatenate(left_terms).astype(jnp.float32)

time: 623 us -> 618 us (level)
  waiting for transfers between devices: 351 us -> 344 us
    all_to_all x1 -> x0, blocking collectives: 11.2 us -> none  [on_device(): lax.all_to_all(jnp.concatenate([adam_rows, norm_rows], axis=1), 'dp', 0,...]
    psum x0 -> x1, blocking collectives: none -> 10.9 us  [on_device(): norm_grad = lax.psum(norm_dp, 'group').reshape(local_norm.shape)]
    all_gather x1, waiting for transfers between devices: 11.7 us -> 4.3 us  [on_device(): full_left = lax.all_gather(left_root, 'group', axis=2, tiled=True)]
    all_to_all x5, waiting for transfers between devices: 152 us -> 159 us  [to_keepers(): lax.all_to_all(owned.reshape(n_slots, n_dp, rows, quarter), 'dp', 1, 1, t...]
    all_gather x2, waiting for transfers between devices: 6.72 us -> 0.03 us  [on_device(): piece = lax.all_gather(mine, 'group', axis=2, tiled=True)]
  transfers between devices with their start and end apart: 13 -> 14, of which waited for: 11 -> 10; matrix products, arithmetic and copies ran while one was open for 20% -> 21% of each run, Pallas kernels for 0% -> 0%
where the time goes in v10:
time: 618 us; the launch traced here: 617 us
  waiting for transfers between devices  344 us (56%)
  local copies, waits for them, and re-layouts  72.3 us (12%)
  blocking collectives  69.6 us (11%)
  starting transfers between devices  43.2 us (7%)
  matrix products  42.8 us (7%)
  other arithmetic  31.2 us (5%)
  between operations  14.1 us (2%)
    all_to_all x5, waiting for transfers between devices, to_keepers(): lax.all_to_all(owned.reshape(n_slots, n_dp, rows, quarter), 'dp', 1, 1, t...  159 us
    all_to_all x3, waiting for transfers between devices, to_owners(): lax.all_to_all(padded.reshape(n_slots, n_dp, rows, quarter), 'dp', 1, 1,...  111 us
    reduce_scatter x2, waiting for transfers between devices, on_device(): lax.psum_scatter(partials[0, b0:b1], 'group', scatter_dimension=2, tiled=...  68.5 us
    all_to_all x1, blocking collectives, to_owners(): lax.all_to_all(padded.reshape(n_slots, n_dp, rows, quarter), 'dp', 1, 1,...  52.2 us
    squeeze x2, local copies, waits for them, and re-layouts, on_device(): partials[0, b0:b1]  24.6 us
    all_to_all x5, starting transfers between devices, to_keepers(): lax.all_to_all(owned.reshape(n_slots, n_dp, rows, quarter), 'dp', 1, 1, t...  23.5 us
    dot_general x1, matrix products, on_device(): jnp.einsum('cim,cmj->cij', full_left, half, preferred_element_type=jnp.fl...  17.7 us
    all_to_all x3, starting transfers between devices, to_owners(): lax.all_to_all(padded.reshape(n_slots, n_dp, rows, quarter), 'dp', 1, 1,...  15.8 us
  transfers between devices with their start and end apart: 14, of which 10 were waited for; matrix products, arithmetic and copies ran while one was open for 21% of the time, Pallas kernels for 0%

profile of v10, /device:TPU:0, one launch (start us, length us, event | category | flops | bytes accessed | tf_op | source)
XLA Modules:
  0.0 617.0 jit_solution(13853001837249483373)
XLA Ops:
  7.2 10.9 %slice_bitcast_fusion.1 = f32[22,128,1024]{2,1,0:T(8,128)} fusion(f32[1,54,128,1024]{3,2,1,0:T(8,128)} %param.8), kind=kLoop, calls=%fused_computation.5 | loop fusion | bytes 23068672 | tf_op jit(solution)/shard_map/squeeze | solution.py:50
  18.2 13.7 %slice_bitcast_fusion = f32[32,128,1024]{2,1,0:T(8,128)} fusion(f32[1,54,128,1024]{3,2,1,0:T(8,128)} %param.8), kind=kLoop, calls=%fused_computation | loop fusion | bytes 33554432 | tf_op jit(solution)/shard_map/squeeze | solution.py:50
  37.7 7.0 %all-to-all-start = ((bf16[7,8,128,256]{3,2,0,1:T(8,128)(2,1)}), bf16[7,8,128,256]{3,2,0,1:T(8,128)(2,1)}, u32[]{:S(2)}, u32[]{:S(2)}) async-start(bf16[7,8,128,256]{3,2,0,1:T(8,128)(2,1)} %copy.28), calls=%async_computation.1 | async-start | bytes 7340032 | tf_op jit(solution)/shard_map/all_to_all | solution.py:35
  44.7 68.5 %reduce-scatter.5.cloned.1.call-done = f32[22,128,256]{2,1,0:T(8,128)} async-done(((f32[22,128,1024]{2,1,0:T(8,128)}), f32[22,128,256]{2,1,0:T(8,128)}) %reduce-scatter.5.cloned.1.call-update) | async-done | bytes 2883600 | tf_op jit(solution)/shard_map/reduce_scatter | solution.py:50
  113.2 5.3 fusion.11
  120.0 6.6 %all-to-all-done = bf16[7,8,128,256]{3,2,0,1:T(8,128)(2,1)} async-done(((bf16[7,8,128,256]{3,2,0,1:T(8,128)(2,1)}), bf16[7,8,128,256]{3,2,0,1:T(8,128)(2,1)}, u32[]{:S(2)}, u32[]{:S(2)}) %all-to-all-start) | async-done | bytes 3670048 | tf_op jit(solution)/shard_map/all_to_all | solution.py:35
  126.5 4.3 all-to-all-start.4
  136.8 30.7 %all-to-all-done.4 = bf16[3,8,128,256]{3,2,0,1:T(8,128)(2,1)} async-done(((bf16[3,8,128,256]{3,2,0,1:T(8,128)(2,1)}), bf16[3,8,128,256]{3,2,0,1:T(8,128)(2,1)}, u32[]{:S(2)}, u32[]{:S(2)}) %all-to-all-start.4) | async-done | bytes 1572896 | tf_op jit(solution)/shard_map/all_to_all | solution.py:35
  167.5 4.5 all-to-all-start.1
  174.9 4.3 copy.29
  179.2 74.1 %all-to-all-done.1 = bf16[7,8,128,256]{3,2,0,1:T(8,128)(2,1)} async-done(((bf16[7,8,128,256]{3,2,0,1:T(8,128)(2,1)}), bf16[7,8,128,256]{3,2,0,1:T(8,128)(2,1)}, u32[]{:S(2)}, u32[]{:S(2)}) %all-to-all-start.1) | async-done | bytes 3670048 | tf_op jit(solution)/shard_map/all_to_all | solution.py:35
  253.4 4.5 copy.31
  257.8 8.0 %fusion.4 = (f32[32,128,256]{2,1,0:T(8,128)}, f32[32]{0:T(128)S(1)}, bf16[32,128,256]{2,1,0:T(8,128)(2,1)S(1)}) fusion(f32[32,128,256]{2,1,0:T(8,128)} %reduce-scatter.3.cloned.1.call-done, f32[54,128,256]{2,1,0:T(8,128)} %param.9), kind=kLoop, calls=%fused_computation.13 | loop fusion | flops 9437152 | bytes 14680192 | tf_op jit(solution)/shard_map/add | solution.py:53
  266.1 52.2 %all_to_all.54 = bf16[4,8,128,256]{3,2,0,1:T(8,128)(2,1)S(1)} all-to-all(bf16[4,8,128,256]{3,2,0,1:T(8,128)(2,1)S(1)} %copy.33), channel_id=1, replica_groups=mesh['dp'=8,'group'=4] {'dp'}, dimensions={1} | all-to-all | bytes 4194304 | tf_op jit(solution)/shard_map/all_to_all | solution.py:35
  325.2 6.3 %convolution_convert_fusion.2 = bf16[3,1024,256]{2,1,0:T(8,128)(2,1)S(1)} fusion(bf16[3,1024,1024]{2,1,0:T(8,128)(2,1)} %all-gather.8.cloned.1.call-done, s32[]{:T(128)S(6)} %select_n.4), kind=kOutput, calls=%fused_computation.24 | convolution fusion | flops 1611399168 | bytes 9437188 | tf_op jit(solution)/shard_map/cim,cjm->cij/dot_general | solution.py:73
  332.7 6.0 all-to-all-start.7
  338.7 5.6 convolution_convert_fusion.1
  345.5 29.4 %all-to-all-done.7 = bf16[3,8,128,256]{3,2,0,1:T(8,128)(2,1)} async-done(((bf16[3,8,128,256]{3,2,0,1:T(8,128)(2,1)}), bf16[3,8,128,256]{3,2,0,1:T(8,128)(2,1)}, u32[]{:S(2)}, u32[]{:S(2)}) %all-to-all-start.7) | async-done | bytes 1572896 | tf_op jit(solution)/shard_map/all_to_all | solution.py:40
  374.9 4.3 all-to-all-start.9
  379.4 6.3 %fusion.14 = bf16[4,1024,256]{2,1,0:T(8,128)(2,1)S(1)} fusion(bf16[4,1024,1024]{2,1,0:T(8,128)(2,1)} %all-gather.6.cloned.1.call-done, s32[]{:T(128)S(6)} %select_n.4), kind=kOutput, calls=%fused_computation.21 | convolution fusion | flops 2148532224 | bytes 12582916 | tf_op jit(solution)/shard_map/cim,cjm->cij/dot_general | solution.py:73
  387.2 28.4 %all-to-all-done.9 = bf16[3,8,128,256]{3,2,0,1:T(8,128)(2,1)} async-done(((bf16[3,8,128,256]{3,2,0,1:T(8,128)(2,1)}), bf16[3,8,128,256]{3,2,0,1:T(8,128)(2,1)}, u32[]{:S(2)}, u32[]{:S(2)}) %all-to-all-start.9) | async-done | bytes 1572896 | tf_op jit(solution)/shard_map/all_to_all | solution.py:40
  415.6 4.4 all-to-all-start.6
  420.0 6.9 %convolution_convert_fusion = bf16[4,1024,256]{2,1,0:T(8,128)(2,1)S(1)} fusion(bf16[4,1024,1024]{2,1,0:T(8,128)(2,1)} %all-gather.6.cloned.1.call-done, bf16[4,1024,256]{2,1,0:T(8,128)(2,1)} %bitcast.41), kind=kOutput, calls=%fused_computation.22 | convolution fusion | flops 2148532224 | bytes 12582912 | tf_op jit(solution)/shard_map/cim,cij->cmj/dot_general | solution.py:74
  428.4 39.4 %all-to-all-done.6 = bf16[4,8,128,256]{3,2,0,1:T(8,128)(2,1)} async-done(((bf16[4,8,128,256]{3,2,0,1:T(8,128)(2,1)}), bf16[4,8,128,256]{3,2,0,1:T(8,128)(2,1)}, u32[]{:S(2)}, u32[]{:S(2)}) %all-to-all-start.6) | async-done | bytes 2097184 | tf_op jit(solution)/shard_map/all_to_all | solution.py:40
  467.8 4.4 all-to-all-start.8
  476.5 17.7 %multiply_reduce_fusion = (f32[7]{0:T(128)S(1)}, f32[7,1024,256]{2,1,0:T(8,128)}) fusion(bf16[7,1024,1024]{2,1,0:T(8,128)(2,1)} %all-gather.4.cloned.1.call-done, bf16[7,1024,256]{2,1,0:T(8,128)(2,1)} %bitcast.52, bf16[3,1024,1024]{2,1,0:T(8,128)(2,1)} %all-gather.8.cloned.1.call-done, bf16[4,1024,1024]{2,1,0:T(8,128)(2,1)} %all-gather.6.cloned.1.call-done), kind=kOutput, calls=%fused_computation.7 | convolution fusion | flops 7529037824 | bytes 40370204 | tf_op jit(solution)/shard_map/cim,cmj->cij/dot_general | solution.py:83
  494.2 6.5 %psum.14 = f32[14]{0:T(128)S(1)} all-reduce(f32[14]{0:T(128)S(1)} %pad_maximum_fusion.2), channel_id=1, replica_groups=mesh['dp'=8,'group'=4] {'group'}, use_global_device_ids=true, to_apply=%region_6.7 | all-reduce | flops 14 | bytes 112 | tf_op jit(solution)/shard_map/psum | solution.py:84
  506.9 13.0 %all-to-all-done.8 = bf16[4,8,128,256]{3,2,0,1:T(8,128)(2,1)} async-done(((bf16[4,8,128,256]{3,2,0,1:T(8,128)(2,1)}), bf16[4,8,128,256]{3,2,0,1:T(8,128)(2,1)}, u32[]{:S(2)}, u32[]{:S(2)}) %all-to-all-start.8) | async-done | bytes 2097184 | tf_op jit(solution)/shard_map/all_to_all | solution.py:40
  519.9 4.5 all-to-all-start.5
  524.5 5.8 pad_maximum_fusion
  545.4 10.9 %psum.15 = f32[2,2048]{1,0:T(2,128)S(1)} all-reduce(f32[2,2048]{1,0:T(2,128)S(1)} %reshape.95), channel_id=1, replica_groups=mesh['dp'=8,'group'=4] {'group'}, use_global_device_ids=true, to_apply=%region_7.8 | all-reduce | flops 4096 | bytes 32768 | tf_op jit(solution)/shard_map/psum | solution.py:91
  557.0 48.8 %all-to-all-done.5 = bf16[7,8,128,256]{3,2,0,1:T(8,128)(2,1)} async-done(((bf16[7,8,128,256]{3,2,0,1:T(8,128)(2,1)}), bf16[7,8,128,256]{3,2,0,1:T(8,128)(2,1)}, u32[]{:S(2)}, u32[]{:S(2)}) %all-to-all-start.5) | async-done | bytes 3670048 | tf_op jit(solution)/shard_map/all_to_all | solution.py:40
  (74 shorter events, 59.7 us)
Async XLA Ops:
  7.2 106.0 %reduce-scatter.5.cloned.1.call-start = ((), (), s32[]{:S(2)}) async-start(), calls=%async_computation.14 | async-start | bytes 14417920 | tf_op jit(solution)/shard_map/reduce_scatter | solution.py:50
  18.2 239.7 %reduce-scatter.3.cloned.1.call-start = ((), (), s32[]{:S(2)}) async-start(), calls=%async_computation.12 | async-start | bytes 20971520 | tf_op jit(solution)/shard_map/reduce_scatter | solution.py:50
  31.9 2.8 copy-start
  37.7 88.8 %all-to-all-start = ((bf16[7,8,128,256]{3,2,0,1:T(8,128)(2,1)}), bf16[7,8,128,256]{3,2,0,1:T(8,128)(2,1)}, u32[]{:S(2)}, u32[]{:S(2)}) async-start(bf16[7,8,128,256]{3,2,0,1:T(8,128)(2,1)} %copy.28), calls=%async_computation.1 | async-start | bytes 7340032 | tf_op jit(solution)/shard_map/all_to_all | solution.py:35
  126.5 40.9 %all-to-all-start.4 = ((bf16[3,8,128,256]{3,2,0,1:T(8,128)(2,1)}), bf16[3,8,128,256]{3,2,0,1:T(8,128)(2,1)}, u32[]{:S(2)}, u32[]{:S(2)}) async-start(bf16[3,8,128,256]{3,2,0,1:T(8,128)(2,1)} %copy.35), calls=%async_computation.6 | async-start | bytes 3145728 | tf_op jit(solution)/shard_map/all_to_all | solution.py:35
  167.5 85.9 %all-to-all-start.1 = ((bf16[7,8,128,256]{3,2,0,1:T(8,128)(2,1)}), bf16[7,8,128,256]{3,2,0,1:T(8,128)(2,1)}, u32[]{:S(2)}, u32[]{:S(2)}) async-start(bf16[7,8,128,256]{3,2,0,1:T(8,128)(2,1)} %copy.30), calls=%async_computation.2 | async-start | bytes 7340032 | tf_op jit(solution)/shard_map/all_to_all | solution.py:35
  172.0 153.2 %all-gather.8.cloned.1.call-start = ((), (), s32[]{:S(2)}) async-start(), calls=%async_computation.16 | async-start | bytes 7864320 | tf_op jit(solution)/shard_map/all_gather | solution.py:69
  174.8 204.5 %all-gather.6.cloned.1.call-start = ((), (), s32[]{:S(2)}) async-start(), calls=%async_computation.15 | async-start | bytes 10485760 | tf_op jit(solution)/shard_map/all_gather | solution.py:69
  319.7 0.7 copy-start.2
  319.8 156.8 %all-gather.4.cloned.1.call-start = ((), (), s32[]{:S(2)}) async-start(), calls=%async_computation.13 | async-start | bytes 18350080 | tf_op jit(solution)/shard_map/all_gather | solution.py:82
  321.5 11.2 %all-to-all-start.2 = ((f32[8,1,4103]{2,1,0:T(1,128)}), f32[8,1,4103]{2,1,0:T(1,128)S(1)}, u32[]{:S(2)}, u32[]{:S(2)}) async-start(f32[8,1,4103]{2,1,0:T(1,128)} %all_to_all.35), calls=%async_computation.4 | async-start | bytes 270336 | tf_op jit(solution)/shard_map/all_to_all | solution.py:62
  332.7 42.2 %all-to-all-start.7 = ((bf16[3,8,128,256]{3,2,0,1:T(8,128)(2,1)}), bf16[3,8,128,256]{3,2,0,1:T(8,128)(2,1)}, u32[]{:S(2)}, u32[]{:S(2)}) async-start(bf16[3,8,128,256]{3,2,0,1:T(8,128)(2,1)} %copy.41), calls=%async_computation.9 | async-start | bytes 3145728 | tf_op jit(solution)/shard_map/all_to_all | solution.py:40
  374.9 40.7 %all-to-all-start.9 = ((bf16[3,8,128,256]{3,2,0,1:T(8,128)(2,1)}), bf16[3,8,128,256]{3,2,0,1:T(8,128)(2,1)}, u32[]{:S(2)}, u32[]{:S(2)}) async-start(bf16[3,8,128,256]{3,2,0,1:T(8,128)(2,1)} %copy.47), calls=%async_computation.11 | async-start | bytes 3145728 | tf_op jit(solution)/shard_map/all_to_all | solution.py:40
  379.3 92.8 %copy-start.1 = (f32[4103]{0:T(1024)}, f32[4103]{0:T(1024)S(1)}, u32[]{:S(2)}) copy-start(f32[4103]{0:T(1024)S(1)} %reduce_sum.38) | copy-start | bytes 49240
  415.6 52.2 %all-to-all-start.6 = ((bf16[4,8,128,256]{3,2,0,1:T(8,128)(2,1)}), bf16[4,8,128,256]{3,2,0,1:T(8,128)(2,1)}, u32[]{:S(2)}, u32[]{:S(2)}) async-start(bf16[4,8,128,256]{3,2,0,1:T(8,128)(2,1)} %copy.39), calls=%async_computation.8 | async-start | bytes 4194304 | tf_op jit(solution)/shard_map/all_to_all | solution.py:40
  467.8 52.2 %all-to-all-start.8 = ((bf16[4,8,128,256]{3,2,0,1:T(8,128)(2,1)}), bf16[4,8,128,256]{3,2,0,1:T(8,128)(2,1)}, u32[]{:S(2)}, u32[]{:S(2)}) async-start(bf16[4,8,128,256]{3,2,0,1:T(8,128)(2,1)} %copy.44), calls=%async_computation.10 | async-start | bytes 4194304 | tf_op jit(solution)/shard_map/all_to_all | solution.py:40
  472.2 22.0 %slice-start.4 = ((f32[4103]{0:T(1024)}), f32[7]{0:T(128)S(1)}, s32[]{:S(2)}) async-start(f32[4103]{0:T(1024)} %copy-done.1), calls=%async_computation.21 | async-start | bytes 1024 | tf_op jit(solution)/shard_map/slice | solution.py:84
  519.9 85.9 %all-to-all-start.5 = ((bf16[7,8,128,256]{3,2,0,1:T(8,128)(2,1)}), bf16[7,8,128,256]{3,2,0,1:T(8,128)(2,1)}, u32[]{:S(2)}, u32[]{:S(2)}) async-start(bf16[7,8,128,256]{3,2,0,1:T(8,128)(2,1)} %copy.37), calls=%async_computation.7 | async-start | bytes 7340032 | tf_op jit(solution)/shard_map/all_to_all | solution.py:40
  531.9 6.2 %slice-start = ((s8[7077888]{0:T(1024)(128)(4,1)}), s8[4194304]{0:T(1024)(128)(4,1)S(1)}, s32[]{:S(2)}) async-start(s8[7077888]{0:T(1024)(128)(4,1)} %bitcast.43), calls=%async_computation.17 | async-start | bytes 8388608
  533.7 4.4 slice-start.1
  533.7 8.0 %slice-start.2 = ((s8[7077888]{0:T(1024)(128)(4,1)}), s8[4194304]{0:T(1024)(128)(4,1)S(1)}, s32[]{:S(2)}) async-start(s8[7077888]{0:T(1024)(128)(4,1)} %bitcast.45), calls=%async_computation.19 | async-start | bytes 8388608
  538.1 3.7 slice-start.3
  541.8 14.6 %copy-start.3 = (f32[2,2048]{1,0:T(2,128)S(1)}, f32[2,2048]{1,0:T(2,128)}, u32[]{:S(2)}) copy-start(f32[2,2048]{1,0:T(2,128)} %param.15) | copy-start | bytes 49156
Sparse Core Ops, SparseCore 0:
  18.3 94.8 reduce-scatter.4
  115.8 126.1 reduce-scatter.2
  243.6 47.2 all-gather.7
  319.9 58.5 all-gather.5
  380.5 95.9 all-gather.3

commit v11 on v10

--- a/solution.py
+++ b/solution.py
@@ -27,7 +27,7 @@
     cap = -(-count // n_dp)
     slots = cap * n_dp
     lower = me_group * quarter
-    split = (cap + 1) // 2
+    split = cap // 2
     bounds = [(0, split), (split, cap)] if cap > 1 else [(0, cap)]
 
     def to_owners(blocks, n_slots):

time: 618 us -> 634 us (1.026)
  blocking collectives: 69.6 us -> 109 us
  waiting for transfers between devices: 344 us -> 325 us
    reduce_scatter x2, waiting for transfers between devices: 68.5 us -> 0.02 us  [on_device(): lax.psum_scatter(partials[0, b0:b1], 'group', scatter_dimension=2, tiled=...]
    all_to_all x3 -> x2, waiting for transfers between devices: 111 us -> 155 us  [to_owners(): lax.all_to_all(padded.reshape(n_slots, n_dp, rows, quarter), 'dp', 1, 1,...]
    all_to_all x1 -> x2, blocking collectives: 52.2 us -> 92.2 us  [to_owners(): lax.all_to_all(padded.reshape(n_slots, n_dp, rows, quarter), 'dp', 1, 1,...]
    all_to_all x1, waiting for transfers between devices: 0.01 us -> 7.31 us  [on_device(): lax.all_to_all(jnp.concatenate([adam_rows, norm_rows], axis=1), 'dp', 0,...]
    all_to_all x3 -> x2, starting transfers between devices: 15.8 us -> 12.3 us  [to_owners(): lax.all_to_all(padded.reshape(n_slots, n_dp, rows, quarter), 'dp', 1, 1,...]
  transfers between devices with their start and end apart: 14 -> 13, of which waited for: 10 -> 8; matrix products, arithmetic and copies ran while one was open for 21% -> 20% of each run, Pallas kernels for 0% -> 0%
where the time goes in v11:
time: 634 us; the launch traced here: 632 us
  waiting for transfers between devices  325 us (51%)
  blocking collectives  109 us (17%)
  local copies, waits for them, and re-layouts  72.4 us (11%)
  matrix products  42.8 us (7%)
  starting transfers between devices  38.1 us (6%)
  other arithmetic  30.8 us (5%)
  between operations  14.1 us (2%)
    all_to_all x5, waiting for transfers between devices, to_keepers(): lax.all_to_all(owned.reshape(n_slots, n_dp, rows, quarter), 'dp', 1, 1, t...  162 us
    all_to_all x2, waiting for transfers between devices, to_owners(): lax.all_to_all(padded.reshape(n_slots, n_dp, rows, quarter), 'dp', 1, 1,...  155 us
    all_to_all x2, blocking collectives, to_owners(): lax.all_to_all(padded.reshape(n_slots, n_dp, rows, quarter), 'dp', 1, 1,...  92.2 us
    squeeze x2, local copies, waits for them, and re-layouts, on_device(): partials[0, b0:b1]  29.8 us
    all_to_all x5, starting transfers between devices, to_keepers(): lax.all_to_all(owned.reshape(n_slots, n_dp, rows, quarter), 'dp', 1, 1, t...  22.1 us
    dot_general x1, matrix products, on_device(): jnp.einsum('cim,cmj->cij', full_left, half, preferred_element_type=jnp.fl...  18.2 us
    add x2, other arithmetic, on_device(): new_moment = 0.99 * second_moment[b0:b1] + 0.01 * grad * grad  12.9 us
  transfers between devices with their start and end apart: 13, of which 8 were waited for; matrix products, arithmetic and copies ran while one was open for 20% of the time, Pallas kernels for 0%

profile of v11, /device:TPU:0, one launch (start us, length us, event | category | flops | bytes accessed | tf_op | source)
XLA Modules:
  0.0 632.5 jit_solution(7094261463739128783)
XLA Ops:
  7.2 11.9 %slice_bitcast_fusion.1 = f32[24,128,1024]{2,1,0:T(8,128)} fusion(f32[1,54,128,1024]{3,2,1,0:T(8,128)} %param.8), kind=kLoop, calls=%fused_computation.5 | loop fusion | bytes 25165824 | tf_op jit(solution)/shard_map/squeeze | solution.py:50
  19.2 17.9 %slice_bitcast_fusion = f32[30,128,1024]{2,1,0:T(8,128)} fusion(f32[1,54,128,1024]{3,2,1,0:T(8,128)} %param.8), kind=kLoop, calls=%fused_computation | loop fusion | bytes 31457280 | tf_op jit(solution)/shard_map/squeeze | solution.py:50
  42.6 7.7 %all-to-all-start = ((bf16[7,8,128,256]{3,2,0,1:T(8,128)(2,1)}), bf16[7,8,128,256]{3,2,0,1:T(8,128)(2,1)}, u32[]{:S(2)}, u32[]{:S(2)}) async-start(bf16[7,8,128,256]{3,2,0,1:T(8,128)(2,1)} %copy.28), calls=%async_computation.1 | async-start | bytes 7340032 | tf_op jit(solution)/shard_map/all_to_all | solution.py:35
  52.9 79.6 %all-to-all-done = bf16[7,8,128,256]{3,2,0,1:T(8,128)(2,1)} async-done(((bf16[7,8,128,256]{3,2,0,1:T(8,128)(2,1)}), bf16[7,8,128,256]{3,2,0,1:T(8,128)(2,1)}, u32[]{:S(2)}, u32[]{:S(2)}) %all-to-all-start) | async-done | bytes 3670048 | tf_op jit(solution)/shard_map/all_to_all | solution.py:35
  132.5 4.6 all-to-all-start.1
  137.2 5.5 copy.29
  142.6 75.7 %all-to-all-done.1 = bf16[7,8,128,256]{3,2,0,1:T(8,128)(2,1)} async-done(((bf16[7,8,128,256]{3,2,0,1:T(8,128)(2,1)}), bf16[7,8,128,256]{3,2,0,1:T(8,128)(2,1)}, u32[]{:S(2)}, u32[]{:S(2)}) %all-to-all-start.1) | async-done | bytes 3670048 | tf_op jit(solution)/shard_map/all_to_all | solution.py:35
  218.4 4.3 copy.31
  222.7 5.7 fusion.11
  228.5 40.7 %all_to_all.54 = bf16[3,8,128,256]{3,2,0,1:T(8,128)(2,1)S(1)} all-to-all(bf16[3,8,128,256]{3,2,0,1:T(8,128)(2,1)S(1)} %copy.33), channel_id=1, replica_groups=mesh['dp'=8,'group'=4] {'dp'}, dimensions={1} | all-to-all | bytes 3145728 | tf_op jit(solution)/shard_map/all_to_all | solution.py:35
  270.6 7.2 %fusion.4 = (f32[30,128,256]{2,1,0:T(8,128)}, f32[30]{0:T(128)S(1)}, bf16[30,128,256]{2,1,0:T(8,128)(2,1)S(1)}) fusion(f32[30,128,256]{2,1,0:T(8,128)} %reduce-scatter.5.cloned.1.call-done, f32[54,128,256]{2,1,0:T(8,128)} %param.9), kind=kLoop, calls=%fused_computation.13 | loop fusion | flops 8847330 | bytes 13762680 | tf_op jit(solution)/shard_map/add | solution.py:53
  278.3 51.4 %all_to_all.55 = bf16[4,8,128,256]{3,2,0,1:T(8,128)(2,1)S(1)} all-to-all(bf16[4,8,128,256]{3,2,0,1:T(8,128)(2,1)S(1)} %copy.35), channel_id=1, replica_groups=mesh['dp'=8,'group'=4] {'dp'}, dimensions={1} | all-to-all | bytes 4194304 | tf_op jit(solution)/shard_map/all_to_all | solution.py:35
  336.6 7.3 %all-to-all-done.2 = f32[8,1,4103]{2,1,0:T(1,128)S(1)} async-done(((f32[8,1,4103]{2,1,0:T(1,128)}), f32[8,1,4103]{2,1,0:T(1,128)S(1)}, u32[]{:S(2)}, u32[]{:S(2)}) %all-to-all-start.2) | async-done | bytes 131328 | tf_op jit(solution)/shard_map/all_to_all | solution.py:62
  344.0 5.2 convolution_convert_fusion.2
  350.5 4.3 all-to-all-start.6
  354.8 5.5 convolution_convert_fusion.1
  361.6 28.8 %all-to-all-done.6 = bf16[3,8,128,256]{3,2,0,1:T(8,128)(2,1)} async-done(((bf16[3,8,128,256]{3,2,0,1:T(8,128)(2,1)}), bf16[3,8,128,256]{3,2,0,1:T(8,128)(2,1)}, u32[]{:S(2)}, u32[]{:S(2)}) %all-to-all-start.6) | async-done | bytes 1572896 | tf_op jit(solution)/shard_map/all_to_all | solution.py:40
  390.4 4.3 all-to-all-start.8
  394.7 7.0 %fusion.14 = bf16[4,1024,256]{2,1,0:T(8,128)(2,1)S(1)} fusion(bf16[4,1024,1024]{2,1,0:T(8,128)(2,1)} %all-gather.8.cloned.1.call-done, s32[]{:T(128)S(6)} %select_n.4), kind=kOutput, calls=%fused_computation.21 | convolution fusion | flops 2148532224 | bytes 12582916 | tf_op jit(solution)/shard_map/cim,cjm->cij/dot_general | solution.py:73
  403.3 27.8 %all-to-all-done.8 = bf16[3,8,128,256]{3,2,0,1:T(8,128)(2,1)} async-done(((bf16[3,8,128,256]{3,2,0,1:T(8,128)(2,1)}), bf16[3,8,128,256]{3,2,0,1:T(8,128)(2,1)}, u32[]{:S(2)}, u32[]{:S(2)}) %all-to-all-start.8) | async-done | bytes 1572896 | tf_op jit(solution)/shard_map/all_to_all | solution.py:40
  431.1 4.4 all-to-all-start.7
  435.5 6.9 %convolution_convert_fusion = bf16[4,1024,256]{2,1,0:T(8,128)(2,1)S(1)} fusion(bf16[4,1024,1024]{2,1,0:T(8,128)(2,1)} %all-gather.8.cloned.1.call-done, bf16[4,1024,256]{2,1,0:T(8,128)(2,1)} %bitcast.39), kind=kOutput, calls=%fused_computation.22 | convolution fusion | flops 2148532224 | bytes 12582912 | tf_op jit(solution)/shard_map/cim,cij->cmj/dot_general | solution.py:74
  443.8 39.4 %all-to-all-done.7 = bf16[4,8,128,256]{3,2,0,1:T(8,128)(2,1)} async-done(((bf16[4,8,128,256]{3,2,0,1:T(8,128)(2,1)}), bf16[4,8,128,256]{3,2,0,1:T(8,128)(2,1)}, u32[]{:S(2)}, u32[]{:S(2)}) %all-to-all-start.7) | async-done | bytes 2097184 | tf_op jit(solution)/shard_map/all_to_all | solution.py:40
  483.3 4.6 all-to-all-start.9
  488.0 18.2 %multiply_reduce_fusion = (f32[7]{0:T(128)S(1)}, f32[7,1024,256]{2,1,0:T(8,128)}) fusion(bf16[7,1024,1024]{2,1,0:T(8,128)(2,1)} %all-gather.4.cloned.1.call-done, bf16[7,1024,256]{2,1,0:T(8,128)(2,1)} %bitcast.52, bf16[4,1024,1024]{2,1,0:T(8,128)(2,1)} %all-gather.8.cloned.1.call-done, bf16[3,1024,1024]{2,1,0:T(8,128)(2,1)} %all-gather.6.cloned.1.call-done), kind=kOutput, calls=%fused_computation.7 | convolution fusion | flops 7529037824 | bytes 40370204 | tf_op jit(solution)/shard_map/cim,cmj->cij/dot_general | solution.py:83
  506.2 6.0 psum.14
  512.3 3.8 multiply_convert_fusion
  518.3 17.2 %all-to-all-done.9 = bf16[4,8,128,256]{3,2,0,1:T(8,128)(2,1)} async-done(((bf16[4,8,128,256]{3,2,0,1:T(8,128)(2,1)}), bf16[4,8,128,256]{3,2,0,1:T(8,128)(2,1)}, u32[]{:S(2)}, u32[]{:S(2)}) %all-to-all-start.9) | async-done | bytes 2097184 | tf_op jit(solution)/shard_map/all_to_all | solution.py:40
  535.5 4.5 all-to-all-start.5
  540.0 5.9 pad_maximum_fusion
  549.0 10.9 %psum.15 = f32[2,2048]{1,0:T(2,128)S(1)} all-reduce(f32[2,2048]{1,0:T(2,128)S(1)} %reshape.95), channel_id=1, replica_groups=mesh['dp'=8,'group'=4] {'group'}, use_global_device_ids=true, to_apply=%region_7.8 | all-reduce | flops 4096 | bytes 32768 | tf_op jit(solution)/shard_map/psum | solution.py:91
  572.5 48.8 %all-to-all-done.5 = bf16[7,8,128,256]{3,2,0,1:T(8,128)(2,1)} async-done(((bf16[7,8,128,256]{3,2,0,1:T(8,128)(2,1)}), bf16[7,8,128,256]{3,2,0,1:T(8,128)(2,1)}, u32[]{:S(2)}, u32[]{:S(2)}) %all-to-all-start.5) | async-done | bytes 3670048 | tf_op jit(solution)/shard_map/all_to_all | solution.py:40
  (75 shorter events, 45.4 us)
Async XLA Ops:
  7.2 215.5 %reduce-scatter.3.cloned.1.call-start = ((), (), s32[]{:S(2)}) async-start(), calls=%async_computation.12 | async-start | bytes 15728640 | tf_op jit(solution)/shard_map/reduce_scatter | solution.py:50
  19.2 251.4 %reduce-scatter.5.cloned.1.call-start = ((), (), s32[]{:S(2)}) async-start(), calls=%async_computation.14 | async-start | bytes 19660800 | tf_op jit(solution)/shard_map/reduce_scatter | solution.py:50
  37.1 2.8 copy-start
  42.6 7.7 %copy-start.1 = (bf16[54,128,256]{2,1,0:T(8,128)(2,1)S(1)}, bf16[54,128,256]{2,1,0:T(8,128)(2,1)}, u32[]{:S(2)}) copy-start(bf16[54,128,256]{2,1,0:T(8,128)(2,1)} %param.13) | copy-start | bytes 10616836
  42.6 89.9 %all-to-all-start = ((bf16[7,8,128,256]{3,2,0,1:T(8,128)(2,1)}), bf16[7,8,128,256]{3,2,0,1:T(8,128)(2,1)}, u32[]{:S(2)}, u32[]{:S(2)}) async-start(bf16[7,8,128,256]{3,2,0,1:T(8,128)(2,1)} %copy.28), calls=%async_computation.1 | async-start | bytes 7340032 | tf_op jit(solution)/shard_map/all_to_all | solution.py:35
  132.5 85.9 %all-to-all-start.1 = ((bf16[7,8,128,256]{3,2,0,1:T(8,128)(2,1)}), bf16[7,8,128,256]{3,2,0,1:T(8,128)(2,1)}, u32[]{:S(2)}, u32[]{:S(2)}) async-start(bf16[7,8,128,256]{3,2,0,1:T(8,128)(2,1)} %copy.30), calls=%async_computation.2 | async-start | bytes 7340032 | tf_op jit(solution)/shard_map/all_to_all | solution.py:35
  137.1 206.9 %all-gather.6.cloned.1.call-start = ((), (), s32[]{:S(2)}) async-start(), calls=%async_computation.15 | async-start | bytes 7864320 | tf_op jit(solution)/shard_map/all_gather | solution.py:69
  270.6 124.2 %all-gather.8.cloned.1.call-start = ((), (), s32[]{:S(2)}) async-start(), calls=%async_computation.16 | async-start | bytes 10485760 | tf_op jit(solution)/shard_map/all_gather | solution.py:69
  331.2 0.7 copy-start.3
  331.2 156.8 %all-gather.4.cloned.1.call-start = ((), (), s32[]{:S(2)}) async-start(), calls=%async_computation.13 | async-start | bytes 18350080 | tf_op jit(solution)/shard_map/all_gather | solution.py:82
  333.0 10.9 %all-to-all-start.2 = ((f32[8,1,4103]{2,1,0:T(1,128)}), f32[8,1,4103]{2,1,0:T(1,128)S(1)}, u32[]{:S(2)}, u32[]{:S(2)}) async-start(f32[8,1,4103]{2,1,0:T(1,128)} %all_to_all.35), calls=%async_computation.4 | async-start | bytes 270336 | tf_op jit(solution)/shard_map/all_to_all | solution.py:62
  344.0 143.9 %copy-start.2 = (f32[4103]{0:T(1024)}, f32[4103]{0:T(1024)S(1)}, u32[]{:S(2)}) copy-start(f32[4103]{0:T(1024)S(1)} %reduce_sum.38) | copy-start | bytes 49240
  350.5 39.9 %all-to-all-start.6 = ((bf16[3,8,128,256]{3,2,0,1:T(8,128)(2,1)}), bf16[3,8,128,256]{3,2,0,1:T(8,128)(2,1)}, u32[]{:S(2)}, u32[]{:S(2)}) async-start(bf16[3,8,128,256]{3,2,0,1:T(8,128)(2,1)} %copy.39), calls=%async_computation.8 | async-start | bytes 3145728 | tf_op jit(solution)/shard_map/all_to_all | solution.py:40
  390.4 40.7 %all-to-all-start.8 = ((bf16[3,8,128,256]{3,2,0,1:T(8,128)(2,1)}), bf16[3,8,128,256]{3,2,0,1:T(8,128)(2,1)}, u32[]{:S(2)}, u32[]{:S(2)}) async-start(bf16[3,8,128,256]{3,2,0,1:T(8,128)(2,1)} %copy.44), calls=%async_computation.10 | async-start | bytes 3145728 | tf_op jit(solution)/shard_map/all_to_all | solution.py:40
  431.1 52.2 %all-to-all-start.7 = ((bf16[4,8,128,256]{3,2,0,1:T(8,128)(2,1)}), bf16[4,8,128,256]{3,2,0,1:T(8,128)(2,1)}, u32[]{:S(2)}, u32[]{:S(2)}) async-start(bf16[4,8,128,256]{3,2,0,1:T(8,128)(2,1)} %copy.41), calls=%async_computation.9 | async-start | bytes 4194304 | tf_op jit(solution)/shard_map/all_to_all | solution.py:40
  483.3 52.3 %all-to-all-start.9 = ((bf16[4,8,128,256]{3,2,0,1:T(8,128)(2,1)}), bf16[4,8,128,256]{3,2,0,1:T(8,128)(2,1)}, u32[]{:S(2)}, u32[]{:S(2)}) async-start(bf16[4,8,128,256]{3,2,0,1:T(8,128)(2,1)} %copy.47), calls=%async_computation.11 | async-start | bytes 4194304 | tf_op jit(solution)/shard_map/all_to_all | solution.py:40
  488.0 18.2 %slice-start.4 = ((f32[4103]{0:T(1024)}), f32[7]{0:T(128)S(1)}, s32[]{:S(2)}) async-start(f32[4103]{0:T(1024)} %copy-done.2), calls=%async_computation.21 | async-start | bytes 1024 | tf_op jit(solution)/shard_map/slice | solution.py:84
  535.5 85.8 %all-to-all-start.5 = ((bf16[7,8,128,256]{3,2,0,1:T(8,128)(2,1)}), bf16[7,8,128,256]{3,2,0,1:T(8,128)(2,1)}, u32[]{:S(2)}, u32[]{:S(2)}) async-start(bf16[7,8,128,256]{3,2,0,1:T(8,128)(2,1)} %copy.37), calls=%async_computation.7 | async-start | bytes 7340032 | tf_op jit(solution)/shard_map/all_to_all | solution.py:40
  545.9 14.0 %copy-start.4 = (f32[2,2048]{1,0:T(2,128)S(1)}, f32[2,2048]{1,0:T(2,128)}, u32[]{:S(2)}) copy-start(f32[2,2048]{1,0:T(2,128)} %param.15) | copy-start | bytes 49156
  560.5 4.2 slice-start
  562.6 2.6 slice-start.1
  562.6 6.2 slice-start.2
  565.3 3.6 slice-start.3
Sparse Core Ops, SparseCore 0:
  19.3 101.7 reduce-scatter.2
  123.7 119.8 reduce-scatter.4
  270.7 46.2 all-gather.5
  331.3 58.3 all-gather.7
  391.7 95.9 all-gather.3

commit v12 on v10

--- a/solution.py
+++ b/solution.py
@@ -40,21 +40,29 @@
         back = lax.all_to_all(owned.reshape(n_slots, n_dp, rows, quarter), "dp", 1, 1, tiled=True)
         return back.reshape(n_slots * n_dp, rows, quarter)
 
-    left_root = to_owners(left_roots, cap)
-    right_root = to_owners(right_roots, cap)
+    def roots_to_owners(blocks):
+        padded = jnp.pad(blocks, ((0, slots - count), (0, 0), (0, 0)))
+        return lax.all_to_all(padded.reshape(cap, n_dp, rows, quarter), "dp", 1, 1, tiled=True)
+
+    left_sent = roots_to_owners(left_roots)
+    right_sent = roots_to_owners(right_roots)
     local_norm = norm_partials[0, 0]
 
     grads, moments, adam_parts = [], [], []
     for index, (s0, s1) in enumerate(bounds):
         b0, b1 = s0 * n_dp, min(s1 * n_dp, count)
         grad = lax.psum_scatter(partials[0, b0:b1], "group", scatter_dimension=2, tiled=True)
+        low = grad.astype(jnp.bfloat16)
         if index == 0:
-            grad, left_root, right_root = lax.optimization_barrier((grad, left_root, right_root))
+            grad, low, left_sent, right_sent = lax.optimization_barrier((grad, low, left_sent, right_sent))
         new_moment = 0.99 * second_moment[b0:b1] + 0.01 * grad * grad
         adam = grad / (jnp.sqrt(new_moment) + EPS_ADAM)
         adam_parts.append(jnp.sum(adam * adam, axis=(1, 2)))
         moments.append(new_moment)
-        grads.append(grad.astype(jnp.bfloat16))
+        grads.append(low)
+
+    left_root = left_sent.reshape(cap, width, quarter)
+    right_root = right_sent.reshape(cap, width, quarter)
 
     adam_cat = jnp.pad(jnp.concatenate(adam_parts), (0, slots - count))
     adam_rows = adam_cat.reshape(cap, n_dp).T

time: 618 us -> 617 us (level)
    all_to_all x3 -> x1, waiting for transfers between devices: 111 us -> 30.7 us  [to_owners(): lax.all_to_all(padded.reshape(n_slots, n_dp, rows, quarter), 'dp', 1, 1,...]
    reduce_scatter x2, waiting for transfers between devices: 68.5 us -> 136 us  [on_device(): lax.psum_scatter(partials[0, b0:b1], 'group', scatter_dimension=2, tiled=...]
    all_to_all x0 -> x2, waiting for transfers between devices: none -> 14.1 us  [roots_to_owners(): lax.all_to_all(padded.reshape(cap, n_dp, rows, quarter), 'dp', 1, 1, tile...]
    all_to_all x3 -> x1, starting transfers between devices: 15.8 us -> 4.34 us  [to_owners(): lax.all_to_all(padded.reshape(n_slots, n_dp, rows, quarter), 'dp', 1, 1,...]
    all_to_all x0 -> x2, starting transfers between devices: none -> 11.5 us  [roots_to_owners(): lax.all_to_all(padded.reshape(cap, n_dp, rows, quarter), 'dp', 1, 1, tile...]
    all_to_all x4 -> x2, local copies, waits for them, and re-layouts: 13 us -> 4.16 us  [to_owners(): lax.all_to_all(padded.reshape(n_slots, n_dp, rows, quarter), 'dp', 1, 1,...]
    optimization_barrier x0 -> x2, local copies, waits for them, and re-layouts: none -> 8.59 us  [on_device(): lax.optimization_barrier((grad, low, left_sent, right_sent))]
  transfers between devices with their start and end apart: 14 -> 14, of which waited for: 10 -> 11; matrix products, arithmetic and copies ran while one was open for 21% -> 22% of each run, Pallas kernels for 0% -> 0%
where the time goes in v12:
time: 617 us; the launch traced here: 616 us
  waiting for transfers between devices  338 us (55%)
  local copies, waits for them, and re-layouts  74.7 us (12%)
  blocking collectives  69 us (11%)
  matrix products  43.9 us (7%)
  starting transfers between devices  42.1 us (7%)
  other arithmetic  34.3 us (6%)
  between operations  14.1 us (2%)
    all_to_all x5, waiting for transfers between devices, to_keepers(): lax.all_to_all(owned.reshape(n_slots, n_dp, rows, quarter), 'dp', 1, 1, t...  156 us
    reduce_scatter x2, waiting for transfers between devices, on_device(): lax.psum_scatter(partials[0, b0:b1], 'group', scatter_dimension=2, tiled=...  136 us
    all_to_all x1, blocking collectives, to_owners(): lax.all_to_all(padded.reshape(n_slots, n_dp, rows, quarter), 'dp', 1, 1,...  51.7 us
    all_to_all x1, waiting for transfers between devices, to_owners(): lax.all_to_all(padded.reshape(n_slots, n_dp, rows, quarter), 'dp', 1, 1,...  30.7 us
    squeeze x2, local copies, waits for them, and re-layouts, on_device(): partials[0, b0:b1]  24.7 us
    all_to_all x5, starting transfers between devices, to_keepers(): lax.all_to_all(owned.reshape(n_slots, n_dp, rows, quarter), 'dp', 1, 1, t...  22.7 us
    dot_general x1, matrix products, on_device(): jnp.einsum('cim,cmj->cij', full_left, half, preferred_element_type=jnp.fl...  17.8 us
    all_to_all x2, waiting for transfers between devices, roots_to_owners(): lax.all_to_all(padded.reshape(cap, n_dp, rows, quarter), 'dp', 1, 1, tile...  14.1 us
  transfers between devices with their start and end apart: 14, of which 11 were waited for; matrix products, arithmetic and copies ran while one was open for 22% of the time, Pallas kernels for 0%

profile of v12, /device:TPU:0, one launch (start us, length us, event | category | flops | bytes accessed | tf_op | source)
XLA Modules:
  0.0 615.8 jit_solution(12724526375430167538)
XLA Ops:
  7.2 11.1 %slice_bitcast_fusion.1 = f32[22,128,1024]{2,1,0:T(8,128)} fusion(f32[1,54,128,1024]{3,2,1,0:T(8,128)} %param.8), kind=kLoop, calls=%fused_computation.5 | loop fusion | bytes 23068672 | tf_op jit(solution)/shard_map/squeeze | solution.py:54
  18.3 13.7 %slice_bitcast_fusion = f32[32,128,1024]{2,1,0:T(8,128)} fusion(f32[1,54,128,1024]{3,2,1,0:T(8,128)} %param.8), kind=kLoop, calls=%fused_computation | loop fusion | bytes 33554432 | tf_op jit(solution)/shard_map/squeeze | solution.py:54
  37.8 7.0 %all-to-all-start = ((bf16[7,8,128,256]{3,2,0,1:T(8,128)(2,1)}), bf16[7,8,128,256]{3,2,0,1:T(8,128)(2,1)}, u32[]{:S(2)}, u32[]{:S(2)}) async-start(bf16[7,8,128,256]{3,2,0,1:T(8,128)(2,1)} %copy.28), calls=%async_computation.1 | async-start | bytes 7340032 | tf_op jit(solution)/shard_map/all_to_all | solution.py:45
  44.8 68.5 %reduce-scatter.5.cloned.1.call-done = f32[22,128,256]{2,1,0:T(8,128)} async-done(((f32[22,128,1024]{2,1,0:T(8,128)}), f32[22,128,256]{2,1,0:T(8,128)}) %reduce-scatter.5.cloned.1.call-update) | async-done | bytes 2883600 | tf_op jit(solution)/shard_map/reduce_scatter | solution.py:54
  113.3 5.4 fusion.11
  120.1 6.6 %all-to-all-done = bf16[7,8,128,256]{3,2,0,1:T(8,128)(2,1)} async-done(((bf16[7,8,128,256]{3,2,0,1:T(8,128)(2,1)}), bf16[7,8,128,256]{3,2,0,1:T(8,128)(2,1)}, u32[]{:S(2)}, u32[]{:S(2)}) %all-to-all-start) | async-done | bytes 3670048 | tf_op jit(solution)/shard_map/all_to_all | solution.py:45
  126.7 4.3 all-to-all-start.4
  136.9 30.7 %all-to-all-done.4 = bf16[3,8,128,256]{3,2,0,1:T(8,128)(2,1)} async-done(((bf16[3,8,128,256]{3,2,0,1:T(8,128)(2,1)}), bf16[3,8,128,256]{3,2,0,1:T(8,128)(2,1)}, u32[]{:S(2)}, u32[]{:S(2)}) %all-to-all-start.4) | async-done | bytes 1572896 | tf_op jit(solution)/shard_map/all_to_all | solution.py:35
  167.6 4.5 all-to-all-start.1
  174.9 67.2 %reduce-scatter.3.cloned.1.call-done = f32[32,128,256]{2,1,0:T(8,128)} async-done(((f32[32,128,1024]{2,1,0:T(8,128)}), f32[32,128,256]{2,1,0:T(8,128)}) %reduce-scatter.3.cloned.1.call-update) | async-done | bytes 4194320 | tf_op jit(solution)/shard_map/reduce_scatter | solution.py:54
  245.9 7.6 %all-to-all-done.1 = bf16[7,8,128,256]{3,2,0,1:T(8,128)(2,1)} async-done(((bf16[7,8,128,256]{3,2,0,1:T(8,128)(2,1)}), bf16[7,8,128,256]{3,2,0,1:T(8,128)(2,1)}, u32[]{:S(2)}, u32[]{:S(2)}) %all-to-all-start.1) | async-done | bytes 3670048 | tf_op jit(solution)/shard_map/all_to_all | solution.py:45
  255.6 51.7 %all_to_all.54 = bf16[4,8,128,256]{3,2,0,1:T(8,128)(2,1)S(1)} all-to-all(bf16[4,8,128,256]{3,2,0,1:T(8,128)(2,1)S(1)} %copy.32), channel_id=1, replica_groups=mesh['dp'=8,'group'=4] {'dp'}, dimensions={1} | all-to-all | bytes 4194304 | tf_op jit(solution)/shard_map/all_to_all | solution.py:35
  308.8 4.3 copy.30
  313.9 7.4 %fusion.4 = (f32[32,128,256]{2,1,0:T(8,128)}, f32[32]{0:T(128)S(1)}) fusion(f32[32,128,256]{2,1,0:T(8,128)} %reduce-scatter.3.cloned.1.call-done, f32[54,128,256]{2,1,0:T(8,128)} %param.9), kind=kLoop, calls=%fused_computation.13 | loop fusion | flops 8388576 | bytes 12583040 | tf_op jit(solution)/shard_map/add | solution.py:58
  325.7 5.2 convolution_convert_fusion.2
  333.0 5.1 all-to-all-start.7
  338.1 5.5 convolution_convert_fusion.1
  345.0 28.8 %all-to-all-done.7 = bf16[3,8,128,256]{3,2,0,1:T(8,128)(2,1)} async-done(((bf16[3,8,128,256]{3,2,0,1:T(8,128)(2,1)}), bf16[3,8,128,256]{3,2,0,1:T(8,128)(2,1)}, u32[]{:S(2)}, u32[]{:S(2)}) %all-to-all-start.7) | async-done | bytes 1572896 | tf_op jit(solution)/shard_map/all_to_all | solution.py:40
  373.8 4.3 all-to-all-start.9
  378.3 8.5 %fusion.14 = bf16[4,1024,256]{2,1,0:T(8,128)(2,1)S(1)} fusion(bf16[4,1024,1024]{2,1,0:T(8,128)(2,1)} %all-gather.6.cloned.1.call-done, s32[]{:T(128)S(6)} %select_n.4), kind=kOutput, calls=%fused_computation.21 | convolution fusion | flops 2148532224 | bytes 12582916 | tf_op jit(solution)/shard_map/cim,cjm->cij/dot_general | solution.py:81
  388.2 26.2 %all-to-all-done.9 = bf16[3,8,128,256]{3,2,0,1:T(8,128)(2,1)} async-done(((bf16[3,8,128,256]{3,2,0,1:T(8,128)(2,1)}), bf16[3,8,128,256]{3,2,0,1:T(8,128)(2,1)}, u32[]{:S(2)}, u32[]{:S(2)}) %all-to-all-start.9) | async-done | bytes 1572896 | tf_op jit(solution)/shard_map/all_to_all | solution.py:40
  414.5 4.4 all-to-all-start.6
  418.8 6.9 %convolution_convert_fusion = bf16[4,1024,256]{2,1,0:T(8,128)(2,1)S(1)} fusion(bf16[4,1024,1024]{2,1,0:T(8,128)(2,1)} %all-gather.6.cloned.1.call-done, bf16[4,1024,256]{2,1,0:T(8,128)(2,1)} %bitcast.42), kind=kOutput, calls=%fused_computation.22 | convolution fusion | flops 2148532224 | bytes 12582912 | tf_op jit(solution)/shard_map/cim,cij->cmj/dot_general | solution.py:82
  427.2 39.4 %all-to-all-done.6 = bf16[4,8,128,256]{3,2,0,1:T(8,128)(2,1)} async-done(((bf16[4,8,128,256]{3,2,0,1:T(8,128)(2,1)}), bf16[4,8,128,256]{3,2,0,1:T(8,128)(2,1)}, u32[]{:S(2)}, u32[]{:S(2)}) %all-to-all-start.6) | async-done | bytes 2097184 | tf_op jit(solution)/shard_map/all_to_all | solution.py:40
  466.6 4.4 all-to-all-start.8
  475.4 17.8 %multiply_reduce_fusion = (f32[7]{0:T(128)S(1)}, f32[7,1024,256]{2,1,0:T(8,128)}) fusion(bf16[7,1024,1024]{2,1,0:T(8,128)(2,1)} %all-gather.4.cloned.1.call-done, bf16[7,1024,256]{2,1,0:T(8,128)(2,1)} %bitcast.52, bf16[3,1024,1024]{2,1,0:T(8,128)(2,1)} %all-gather.8.cloned.1.call-done, bf16[4,1024,1024]{2,1,0:T(8,128)(2,1)} %all-gather.6.cloned.1.call-done), kind=kOutput, calls=%fused_computation.7 | convolution fusion | flops 7529037824 | bytes 40370204 | tf_op jit(solution)/shard_map/cim,cmj->cij/dot_general | solution.py:91
  493.2 6.4 %psum.14 = f32[14]{0:T(128)S(1)} all-reduce(f32[14]{0:T(128)S(1)} %pad_maximum_fusion.2), channel_id=1, replica_groups=mesh['dp'=8,'group'=4] {'group'}, use_global_device_ids=true, to_apply=%region_6.7 | all-reduce | flops 14 | bytes 112 | tf_op jit(solution)/shard_map/psum | solution.py:92
  505.7 13.1 %all-to-all-done.8 = bf16[4,8,128,256]{3,2,0,1:T(8,128)(2,1)} async-done(((bf16[4,8,128,256]{3,2,0,1:T(8,128)(2,1)}), bf16[4,8,128,256]{3,2,0,1:T(8,128)(2,1)}, u32[]{:S(2)}, u32[]{:S(2)}) %all-to-all-start.8) | async-done | bytes 2097184 | tf_op jit(solution)/shard_map/all_to_all | solution.py:40
  518.8 4.5 all-to-all-start.5
  523.3 5.8 pad_maximum_fusion
  544.3 10.9 %psum.15 = f32[2,2048]{1,0:T(2,128)S(1)} all-reduce(f32[2,2048]{1,0:T(2,128)S(1)} %reshape.95), channel_id=1, replica_groups=mesh['dp'=8,'group'=4] {'group'}, use_global_device_ids=true, to_apply=%region_7.8 | all-reduce | flops 4096 | bytes 32768 | tf_op jit(solution)/shard_map/psum | solution.py:99
  555.9 48.8 %all-to-all-done.5 = bf16[7,8,128,256]{3,2,0,1:T(8,128)(2,1)} async-done(((bf16[7,8,128,256]{3,2,0,1:T(8,128)(2,1)}), bf16[7,8,128,256]{3,2,0,1:T(8,128)(2,1)}, u32[]{:S(2)}, u32[]{:S(2)}) %all-to-all-start.5) | async-done | bytes 3670048 | tf_op jit(solution)/shard_map/all_to_all | solution.py:40
  (75 shorter events, 66.0 us)
Async XLA Ops:
  7.2 106.2 %reduce-scatter.5.cloned.1.call-start = ((), (), s32[]{:S(2)}) async-start(), calls=%async_computation.14 | async-start | bytes 14417920 | tf_op jit(solution)/shard_map/reduce_scatter | solution.py:54
  18.3 223.8 %reduce-scatter.3.cloned.1.call-start = ((), (), s32[]{:S(2)}) async-start(), calls=%async_computation.12 | async-start | bytes 20971520 | tf_op jit(solution)/shard_map/reduce_scatter | solution.py:54
  32.0 2.8 copy-start
  37.8 88.8 %all-to-all-start = ((bf16[7,8,128,256]{3,2,0,1:T(8,128)(2,1)}), bf16[7,8,128,256]{3,2,0,1:T(8,128)(2,1)}, u32[]{:S(2)}, u32[]{:S(2)}) async-start(bf16[7,8,128,256]{3,2,0,1:T(8,128)(2,1)} %copy.28), calls=%async_computation.1 | async-start | bytes 7340032 | tf_op jit(solution)/shard_map/all_to_all | solution.py:45
  126.7 40.9 %all-to-all-start.4 = ((bf16[3,8,128,256]{3,2,0,1:T(8,128)(2,1)}), bf16[3,8,128,256]{3,2,0,1:T(8,128)(2,1)}, u32[]{:S(2)}, u32[]{:S(2)}) async-start(bf16[3,8,128,256]{3,2,0,1:T(8,128)(2,1)} %copy.34), calls=%async_computation.6 | async-start | bytes 3145728 | tf_op jit(solution)/shard_map/all_to_all | solution.py:35
  167.6 85.9 %all-to-all-start.1 = ((bf16[7,8,128,256]{3,2,0,1:T(8,128)(2,1)}), bf16[7,8,128,256]{3,2,0,1:T(8,128)(2,1)}, u32[]{:S(2)}, u32[]{:S(2)}) async-start(bf16[7,8,128,256]{3,2,0,1:T(8,128)(2,1)} %copy.29), calls=%async_computation.2 | async-start | bytes 7340032 | tf_op jit(solution)/shard_map/all_to_all | solution.py:45
  172.1 153.6 %all-gather.8.cloned.1.call-start = ((), (), s32[]{:S(2)}) async-start(), calls=%async_computation.16 | async-start | bytes 7864320 | tf_op jit(solution)/shard_map/all_gather | solution.py:77
  174.9 203.4 %all-gather.6.cloned.1.call-start = ((), (), s32[]{:S(2)}) async-start(), calls=%async_computation.15 | async-start | bytes 10485760 | tf_op jit(solution)/shard_map/all_gather | solution.py:77
  308.8 166.6 %all-gather.4.cloned.1.call-start = ((), (), s32[]{:S(2)}) async-start(), calls=%async_computation.13 | async-start | bytes 18350080 | tf_op jit(solution)/shard_map/all_gather | solution.py:90
  313.1 0.7 copy-start.2
  322.3 10.7 %all-to-all-start.2 = ((f32[8,1,4103]{2,1,0:T(1,128)}), f32[8,1,4103]{2,1,0:T(1,128)S(1)}, u32[]{:S(2)}, u32[]{:S(2)}) async-start(f32[8,1,4103]{2,1,0:T(1,128)} %all_to_all.35), calls=%async_computation.4 | async-start | bytes 270336 | tf_op jit(solution)/shard_map/all_to_all | solution.py:70
  333.0 40.8 %all-to-all-start.7 = ((bf16[3,8,128,256]{3,2,0,1:T(8,128)(2,1)}), bf16[3,8,128,256]{3,2,0,1:T(8,128)(2,1)}, u32[]{:S(2)}, u32[]{:S(2)}) async-start(bf16[3,8,128,256]{3,2,0,1:T(8,128)(2,1)} %copy.41), calls=%async_computation.9 | async-start | bytes 3145728 | tf_op jit(solution)/shard_map/all_to_all | solution.py:40
  373.8 40.7 %all-to-all-start.9 = ((bf16[3,8,128,256]{3,2,0,1:T(8,128)(2,1)}), bf16[3,8,128,256]{3,2,0,1:T(8,128)(2,1)}, u32[]{:S(2)}, u32[]{:S(2)}) async-start(bf16[3,8,128,256]{3,2,0,1:T(8,128)(2,1)} %copy.47), calls=%async_computation.11 | async-start | bytes 3145728 | tf_op jit(solution)/shard_map/all_to_all | solution.py:40
  378.2 97.1 %copy-start.1 = (f32[4103]{0:T(1024)}, f32[4103]{0:T(1024)S(1)}, u32[]{:S(2)}) copy-start(f32[4103]{0:T(1024)S(1)} %reduce_sum.38) | copy-start | bytes 49240
  414.5 52.2 %all-to-all-start.6 = ((bf16[4,8,128,256]{3,2,0,1:T(8,128)(2,1)}), bf16[4,8,128,256]{3,2,0,1:T(8,128)(2,1)}, u32[]{:S(2)}, u32[]{:S(2)}) async-start(bf16[4,8,128,256]{3,2,0,1:T(8,128)(2,1)} %copy.39), calls=%async_computation.8 | async-start | bytes 4194304 | tf_op jit(solution)/shard_map/all_to_all | solution.py:40
  466.6 52.2 %all-to-all-start.8 = ((bf16[4,8,128,256]{3,2,0,1:T(8,128)(2,1)}), bf16[4,8,128,256]{3,2,0,1:T(8,128)(2,1)}, u32[]{:S(2)}, u32[]{:S(2)}) async-start(bf16[4,8,128,256]{3,2,0,1:T(8,128)(2,1)} %copy.44), calls=%async_computation.10 | async-start | bytes 4194304 | tf_op jit(solution)/shard_map/all_to_all | solution.py:40
  475.4 17.8 %slice-start.4 = ((f32[4103]{0:T(1024)}), f32[7]{0:T(128)S(1)}, s32[]{:S(2)}) async-start(f32[4103]{0:T(1024)} %copy-done.1), calls=%async_computation.21 | async-start | bytes 1024 | tf_op jit(solution)/shard_map/slice | solution.py:92
  518.8 85.9 %all-to-all-start.5 = ((bf16[7,8,128,256]{3,2,0,1:T(8,128)(2,1)}), bf16[7,8,128,256]{3,2,0,1:T(8,128)(2,1)}, u32[]{:S(2)}, u32[]{:S(2)}) async-start(bf16[7,8,128,256]{3,2,0,1:T(8,128)(2,1)} %copy.37), calls=%async_computation.7 | async-start | bytes 7340032 | tf_op jit(solution)/shard_map/all_to_all | solution.py:40
  530.7 6.2 %slice-start = ((s8[7077888]{0:T(1024)(128)(4,1)}), s8[4194304]{0:T(1024)(128)(4,1)S(1)}, s32[]{:S(2)}) async-start(s8[7077888]{0:T(1024)(128)(4,1)} %bitcast.43), calls=%async_computation.17 | async-start | bytes 8388608
  532.6 4.4 slice-start.1
  532.6 8.0 %slice-start.2 = ((s8[7077888]{0:T(1024)(128)(4,1)}), s8[4194304]{0:T(1024)(128)(4,1)S(1)}, s32[]{:S(2)}) async-start(s8[7077888]{0:T(1024)(128)(4,1)} %bitcast.45), calls=%async_computation.19 | async-start | bytes 8388608
  537.0 3.7 slice-start.3
  540.6 14.6 %copy-start.3 = (f32[2,2048]{1,0:T(2,128)S(1)}, f32[2,2048]{1,0:T(2,128)}, u32[]{:S(2)}) copy-start(f32[2,2048]{1,0:T(2,128)} %param.15) | copy-start | bytes 49156
Sparse Core Ops, SparseCore 0:
  18.4 94.8 reduce-scatter.4
  115.9 126.1 reduce-scatter.2
  244.3 47.2 all-gather.7
  308.9 58.5 all-gather.5
  369.5 95.9 all-gather.3

commit v13 on v12

--- a/solution.py
+++ b/solution.py
@@ -80,8 +80,11 @@
         own_rows = lax.dynamic_slice_in_dim(piece, lower, quarter, 1)
         gram_left = jnp.einsum("cim,cjm->cij", piece, own_rows, preferred_element_type=jnp.float32)
         gram_right = jnp.einsum("cim,cij->cmj", piece, mine, preferred_element_type=jnp.float32)
-        left_terms.append(to_keepers(gram_left.astype(jnp.bfloat16))[: b1 - b0])
-        right_terms.append(to_keepers(gram_right.astype(jnp.bfloat16))[: b1 - b0])
+        both = jnp.concatenate([gram_left.astype(jnp.bfloat16), gram_right.astype(jnp.bfloat16)])
+        back = to_keepers(both)
+        n_blocks = (s1 - s0) * n_dp
+        left_terms.append(back[: b1 - b0])
+        right_terms.append(back[n_blocks : n_blocks + b1 - b0])
         pieces.append(piece)
 
     piece = jnp.concatenate(pieces) if len(pieces) > 1 else pieces[0]

time: 617 us -> 604 us (0.979)
  starting transfers between devices: 42.1 us -> 33.9 us
  local copies, waits for them, and re-layouts: 74.7 us -> 67.7 us
    all_to_all x5 -> x3, waiting for transfers between devices: 156 us -> 86.9 us  [to_keepers(): lax.all_to_all(owned.reshape(n_slots, n_dp, rows, quarter), 'dp', 1, 1, t...]
    all_gather x1, waiting for transfers between devices: 0.01 us -> 46 us  [on_device(): full_left = lax.all_gather(left_root, 'group', axis=2, tiled=True)]
    all_gather x2, waiting for transfers between devices: 0.04 us -> 26.2 us  [on_device(): piece = lax.all_gather(mine, 'group', axis=2, tiled=True)]
    all_to_all x5 -> x3, starting transfers between devices: 22.7 us -> 15 us  [to_keepers(): lax.all_to_all(owned.reshape(n_slots, n_dp, rows, quarter), 'dp', 1, 1, t...]
    all_to_all x5 -> x2, local copies, waits for them, and re-layouts: 9.96 us -> 2.65 us  [to_keepers(): lax.all_to_all(owned.reshape(n_slots, n_dp, rows, quarter), 'dp', 1, 1, t...]
  transfers between devices with their start and end apart: 14 -> 12, of which waited for: 11 -> 10; matrix products, arithmetic and copies ran while one was open for 22% -> 20% of each run, Pallas kernels for 0% -> 0%
where the time goes in v13:
time: 604 us; the launch traced here: 602 us
  waiting for transfers between devices  342 us (57%)
  blocking collectives  68.6 us (11%)
  local copies, waits for them, and re-layouts  67.7 us (11%)
  matrix products  38.8 us (6%)
  other arithmetic  37.8 us (6%)
  starting transfers between devices  33.9 us (6%)
  between operations  14 us (2%)
    reduce_scatter x2, waiting for transfers between devices, on_device(): lax.psum_scatter(partials[0, b0:b1], 'group', scatter_dimension=2, tiled=...  137 us
    all_to_all x3, waiting for transfers between devices, to_keepers(): lax.all_to_all(owned.reshape(n_slots, n_dp, rows, quarter), 'dp', 1, 1, t...  86.9 us
    all_to_all x1, blocking collectives, to_owners(): lax.all_to_all(padded.reshape(n_slots, n_dp, rows, quarter), 'dp', 1, 1,...  51.8 us
    all_gather x1, waiting for transfers between devices, on_device(): full_left = lax.all_gather(left_root, 'group', axis=2, tiled=True)  46 us
    all_to_all x1, waiting for transfers between devices, to_owners(): lax.all_to_all(padded.reshape(n_slots, n_dp, rows, quarter), 'dp', 1, 1,...  31.3 us
    all_gather x2, waiting for transfers between devices, on_device(): piece = lax.all_gather(mine, 'group', axis=2, tiled=True)  26.2 us
    squeeze x2, local copies, waits for them, and re-layouts, on_device(): partials[0, b0:b1]  24.7 us
    dot_general x1, matrix products, on_device(): jnp.einsum('cim,cmj->cij', full_left, half, preferred_element_type=jnp.fl...  17.7 us
  transfers between devices with their start and end apart: 12, of which 10 were waited for; matrix products, arithmetic and copies ran while one was open for 20% of the time, Pallas kernels for 0%

profile of v13, /device:TPU:0, one launch (start us, length us, event | category | flops | bytes accessed | tf_op | source)
XLA Modules:
  0.0 602.5 jit_solution(5952788004856955438)
XLA Ops:
  7.2 11.1 %slice_bitcast_fusion.1 = f32[22,128,1024]{2,1,0:T(8,128)} fusion(f32[1,54,128,1024]{3,2,1,0:T(8,128)} %param.8), kind=kLoop, calls=%fused_computation.5 | loop fusion | bytes 23068672 | tf_op jit(solution)/shard_map/squeeze | solution.py:54
  18.3 13.7 %slice_bitcast_fusion = f32[32,128,1024]{2,1,0:T(8,128)} fusion(f32[1,54,128,1024]{3,2,1,0:T(8,128)} %param.8), kind=kLoop, calls=%fused_computation | loop fusion | bytes 33554432 | tf_op jit(solution)/shard_map/squeeze | solution.py:54
  37.8 7.0 %all-to-all-start = ((bf16[7,8,128,256]{3,2,0,1:T(8,128)(2,1)}), bf16[7,8,128,256]{3,2,0,1:T(8,128)(2,1)}, u32[]{:S(2)}, u32[]{:S(2)}) async-start(bf16[7,8,128,256]{3,2,0,1:T(8,128)(2,1)} %copy.26), calls=%async_computation.1 | async-start | bytes 7340032 | tf_op jit(solution)/shard_map/all_to_all | solution.py:45
  44.8 68.5 %reduce-scatter.5.cloned.1.call-done = f32[22,128,256]{2,1,0:T(8,128)} async-done(((f32[22,128,1024]{2,1,0:T(8,128)}), f32[22,128,256]{2,1,0:T(8,128)}) %reduce-scatter.5.cloned.1.call-update) | async-done | bytes 2883600 | tf_op jit(solution)/shard_map/reduce_scatter | solution.py:54
  113.3 6.9 %fusion.11 = (f32[22,128,256]{2,1,0:T(8,128)}, f32[22]{0:T(128)S(1)}, bf16[22,128,256]{2,1,0:T(8,128)(2,1)S(1)}) fusion(f32[22,128,256]{2,1,0:T(8,128)} %reduce-scatter.5.cloned.1.call-done, f32[54,128,256]{2,1,0:T(8,128)} %param.9), kind=kLoop, calls=%fused_computation.19 | loop fusion | flops 6488042 | bytes 10092632 | tf_op jit(solution)/shard_map/add | solution.py:58
  121.6 5.0 all-to-all-done
  126.7 3.6 all-to-all-start.4
  136.1 31.3 %all-to-all-done.4 = bf16[3,8,128,256]{3,2,0,1:T(8,128)(2,1)S(1)} async-done(((bf16[3,8,128,256]{3,2,0,1:T(8,128)(2,1)}), bf16[3,8,128,256]{3,2,0,1:T(8,128)(2,1)S(1)}, u32[]{:S(2)}, u32[]{:S(2)}) %all-to-all-start.4) | async-done | bytes 1572896 | tf_op jit(solution)/shard_map/all_to_all | solution.py:35
  167.5 4.5 all-to-all-start.1
  173.4 68.7 %reduce-scatter.3.cloned.1.call-done = f32[32,128,256]{2,1,0:T(8,128)} async-done(((f32[32,128,1024]{2,1,0:T(8,128)}), f32[32,128,256]{2,1,0:T(8,128)}) %reduce-scatter.3.cloned.1.call-update) | async-done | bytes 4194320 | tf_op jit(solution)/shard_map/reduce_scatter | solution.py:54
  244.6 8.8 %all-to-all-done.1 = bf16[7,8,128,256]{3,2,0,1:T(8,128)(2,1)} async-done(((bf16[7,8,128,256]{3,2,0,1:T(8,128)(2,1)}), bf16[7,8,128,256]{3,2,0,1:T(8,128)(2,1)}, u32[]{:S(2)}, u32[]{:S(2)}) %all-to-all-start.1) | async-done | bytes 3670048 | tf_op jit(solution)/shard_map/all_to_all | solution.py:45
  253.5 51.8 %all_to_all.44 = bf16[4,8,128,256]{3,2,0,1:T(8,128)(2,1)S(1)} all-to-all(bf16[4,8,128,256]{3,2,0,1:T(8,128)(2,1)S(1)} %copy.30), channel_id=1, replica_groups=mesh['dp'=8,'group'=4] {'dp'}, dimensions={1} | all-to-all | bytes 4194304 | tf_op jit(solution)/shard_map/all_to_all | solution.py:35
  306.8 4.3 copy.28
  311.9 7.5 %fusion.4 = (f32[32,128,256]{2,1,0:T(8,128)}, f32[32]{0:T(128)S(1)}) fusion(f32[32,128,256]{2,1,0:T(8,128)} %reduce-scatter.3.cloned.1.call-done, f32[54,128,256]{2,1,0:T(8,128)} %param.9), kind=kLoop, calls=%fused_computation.13 | loop fusion | flops 8388576 | bytes 12583040 | tf_op jit(solution)/shard_map/add | solution.py:58
  324.0 5.3 convolution_convert_fusion.1
  333.5 5.7 all-to-all-start.7
  339.4 26.1 %all-gather.6.cloned.1.call-done = bf16[4,1024,1024]{2,1,0:T(8,128)(2,1)} async-done(((bf16[4,1024,256]{2,1,0:T(8,128)(2,1)}), bf16[4,1024,1024]{2,1,0:T(8,128)(2,1)}) %all-gather.6.cloned.1.call-update) | async-done | bytes 8388624 | tf_op jit(solution)/shard_map/all_gather | solution.py:77
  365.5 6.5 %fusion.14 = bf16[4,1024,256]{2,1,0:T(8,128)(2,1)S(1)} fusion(bf16[4,1024,1024]{2,1,0:T(8,128)(2,1)} %all-gather.6.cloned.1.call-done, s32[]{:T(128)S(6)} %select_n.4), kind=kOutput, calls=%fused_computation.23 | convolution fusion | flops 2148532224 | bytes 12582916 | tf_op jit(solution)/shard_map/cim,cjm->cij/dot_general | solution.py:81
  372.0 7.4 %convolution_convert_fusion = bf16[4,1024,256]{2,1,0:T(8,128)(2,1)S(1)} fusion(bf16[4,1024,1024]{2,1,0:T(8,128)(2,1)} %all-gather.6.cloned.1.call-done, bf16[4,1024,256]{2,1,0:T(8,128)(2,1)S(1)} %bitcast.42), kind=kOutput, calls=%fused_computation.24 | convolution fusion | flops 2148532224 | bytes 12582912 | tf_op jit(solution)/shard_map/cim,cij->cmj/dot_general | solution.py:82
  382.4 25.9 %all-to-all-done.7 = bf16[6,8,128,256]{3,2,0,1:T(8,128)(2,1)S(1)} async-done(((bf16[6,8,128,256]{3,2,0,1:T(8,128)(2,1)}), bf16[6,8,128,256]{3,2,0,1:T(8,128)(2,1)S(1)}, u32[]{:S(2)}, u32[]{:S(2)}) %all-to-all-start.7) | async-done | bytes 3145760 | tf_op jit(solution)/shard_map/all_to_all | solution.py:40
  408.3 4.8 all-to-all-start.6
  413.1 4.3 copy.34
  417.5 46.0 %all-gather.4.cloned.1.call-done = bf16[7,1024,1024]{2,1,0:T(8,128)(2,1)} async-done(((bf16[7,1024,256]{2,1,0:T(8,128)(2,1)}), bf16[7,1024,1024]{2,1,0:T(8,128)(2,1)}) %all-gather.4.cloned.1.call-update) | async-done | bytes 14680080 | tf_op jit(solution)/shard_map/all_gather | solution.py:93
  463.6 17.7 %multiply_reduce_fusion = (f32[7]{0:T(128)S(1)}, f32[7,1024,256]{2,1,0:T(8,128)}) fusion(bf16[7,1024,1024]{2,1,0:T(8,128)(2,1)} %all-gather.4.cloned.1.call-done, bf16[7,1024,256]{2,1,0:T(8,128)(2,1)} %bitcast.48, bf16[3,1024,1024]{2,1,0:T(8,128)(2,1)} %all-gather.8.cloned.1.call-done, bf16[4,1024,1024]{2,1,0:T(8,128)(2,1)} %all-gather.6.cloned.1.call-done), kind=kOutput, calls=%fused_computation.7 | convolution fusion | flops 7529037824 | bytes 40370204 | tf_op jit(solution)/shard_map/cim,cmj->cij/dot_general | solution.py:94
  481.3 5.9 psum.14
  487.3 3.8 multiply_convert_fusion
  493.3 12.2 %all-to-all-done.6 = bf16[8,8,128,256]{3,2,0,1:T(8,128)(2,1)} async-done(((bf16[8,8,128,256]{3,2,0,1:T(8,128)(2,1)}), bf16[8,8,128,256]{3,2,0,1:T(8,128)(2,1)}, u32[]{:S(2)}, u32[]{:S(2)}) %all-to-all-start.6) | async-done | bytes 4194336 | tf_op jit(solution)/shard_map/all_to_all | solution.py:40
  505.6 4.5 all-to-all-start.5
  510.1 6.8 %pad_maximum_fusion = f32[54,128,256]{2,1,0:T(8,128)} fusion(f32[22,128,256]{2,1,0:T(8,128)} %get-tuple-element.26, f32[32,128,256]{2,1,0:T(8,128)} %get-tuple-element.24), kind=kLoop, calls=%fused_computation.8 | loop fusion | flops 1769472 | bytes 14155776 | tf_op jit(solution)/shard_map/concatenate | solution.py:104
  517.3 10.9 %psum.15 = f32[2,2048]{1,0:T(2,128)S(1)} all-reduce(f32[2,2048]{1,0:T(2,128)S(1)} %reshape.78), channel_id=1, replica_groups=mesh['dp'=8,'group'=4] {'group'}, use_global_device_ids=true, to_apply=%region_7.8 | all-reduce | flops 4096 | bytes 32768 | tf_op jit(solution)/shard_map/psum | solution.py:102
  533.7 8.7 %multiply_add_fusion = (f32[54,128,256]{2,1,0:T(8,128)}, f32[54,128,256]{2,1,0:T(8,128)}) fusion(f32[54,128,256]{2,1,0:T(8,128)S(1)} %bitcast.44, bf16[22,128,256]{2,1,0:T(8,128)(2,1)S(1)} %get-tuple-element.30, bf16[32,128,256]{2,1,0:T(8,128)(2,1)S(1)} %bitcast.38, bf16[22,128,256]{2,1,0:T(8,128)(2,1)S(1)} %get-tuple-element.31, ...), kind=kLoop, calls=%fused_computation.9 | loop fusion | flops 17694720 | bytes 35389440 | tf_op jit(solution)/shard_map/add | solution.py:108
  542.5 48.8 %all-to-all-done.5 = bf16[7,8,128,256]{3,2,0,1:T(8,128)(2,1)} async-done(((bf16[7,8,128,256]{3,2,0,1:T(8,128)(2,1)}), bf16[7,8,128,256]{3,2,0,1:T(8,128)(2,1)}, u32[]{:S(2)}, u32[]{:S(2)}) %all-to-all-start.5) | async-done | bytes 3670048 | tf_op jit(solution)/shard_map/all_to_all | solution.py:40
  (70 shorter events, 44.2 us)
Async XLA Ops:
  7.2 106.2 %reduce-scatter.5.cloned.1.call-start = ((), (), s32[]{:S(2)}) async-start(), calls=%async_computation.12 | async-start | bytes 14417920 | tf_op jit(solution)/shard_map/reduce_scatter | solution.py:54
  18.3 223.8 %reduce-scatter.3.cloned.1.call-start = ((), (), s32[]{:S(2)}) async-start(), calls=%async_computation.10 | async-start | bytes 20971520 | tf_op jit(solution)/shard_map/reduce_scatter | solution.py:54
  32.0 2.8 copy-start.2
  37.8 88.8 %all-to-all-start = ((bf16[7,8,128,256]{3,2,0,1:T(8,128)(2,1)}), bf16[7,8,128,256]{3,2,0,1:T(8,128)(2,1)}, u32[]{:S(2)}, u32[]{:S(2)}) async-start(bf16[7,8,128,256]{3,2,0,1:T(8,128)(2,1)} %copy.26), calls=%async_computation.1 | async-start | bytes 7340032 | tf_op jit(solution)/shard_map/all_to_all | solution.py:45
  126.7 40.8 %all-to-all-start.4 = ((bf16[3,8,128,256]{3,2,0,1:T(8,128)(2,1)}), bf16[3,8,128,256]{3,2,0,1:T(8,128)(2,1)S(1)}, u32[]{:S(2)}, u32[]{:S(2)}) async-start(bf16[3,8,128,256]{3,2,0,1:T(8,128)(2,1)} %copy.32), calls=%async_computation.6 | async-start | bytes 3145728 | tf_op jit(solution)/shard_map/all_to_all | solution.py:35
  167.5 85.9 %all-to-all-start.1 = ((bf16[7,8,128,256]{3,2,0,1:T(8,128)(2,1)}), bf16[7,8,128,256]{3,2,0,1:T(8,128)(2,1)}, u32[]{:S(2)}, u32[]{:S(2)}) async-start(bf16[7,8,128,256]{3,2,0,1:T(8,128)(2,1)} %copy.27), calls=%async_computation.2 | async-start | bytes 7340032 | tf_op jit(solution)/shard_map/all_to_all | solution.py:45
  172.0 152.0 %all-gather.8.cloned.1.call-start = ((), (), s32[]{:S(2)}) async-start(), calls=%async_computation.14 | async-start | bytes 7864320 | tf_op jit(solution)/shard_map/all_gather | solution.py:77
  173.3 192.2 %all-gather.6.cloned.1.call-start = ((), (), s32[]{:S(2)}) async-start(), calls=%async_computation.13 | async-start | bytes 10485760 | tf_op jit(solution)/shard_map/all_gather | solution.py:77
  306.8 156.8 %all-gather.4.cloned.1.call-start = ((), (), s32[]{:S(2)}) async-start(), calls=%async_computation.11 | async-start | bytes 18350080 | tf_op jit(solution)/shard_map/all_gather | solution.py:93
  311.1 0.7 copy-start.4
  311.9 12.1 %copy-start.1 = (bf16[3,8,128,256]{3,2,1,0:T(8,128)(2,1)S(1)}, bf16[3,8,128,256]{3,2,1,0:T(8,128)(2,1)}, u32[]{:S(2)}) copy-start(bf16[3,8,128,256]{3,2,1,0:T(8,128)(2,1)} %copy.33) | copy-start | bytes 4718596
  320.4 13.1 %all-to-all-start.2 = ((f32[8,1,4103]{2,1,0:T(1,128)}), f32[8,1,4103]{2,1,0:T(1,128)S(1)}, u32[]{:S(2)}, u32[]{:S(2)}) async-start(f32[8,1,4103]{2,1,0:T(1,128)} %all_to_all.29), calls=%async_computation.4 | async-start | bytes 270336 | tf_op jit(solution)/shard_map/all_to_all | solution.py:70
  324.0 5.4 copy-start.6
  333.5 74.8 %all-to-all-start.7 = ((bf16[6,8,128,256]{3,2,0,1:T(8,128)(2,1)}), bf16[6,8,128,256]{3,2,0,1:T(8,128)(2,1)S(1)}, u32[]{:S(2)}, u32[]{:S(2)}) async-start(bf16[6,8,128,256]{3,2,0,1:T(8,128)(2,1)} %copy.41), calls=%async_computation.9 | async-start | bytes 6291456 | tf_op jit(solution)/shard_map/all_to_all | solution.py:40
  339.3 78.1 %copy-start.3 = (f32[4103]{0:T(1024)}, f32[4103]{0:T(1024)S(1)}, u32[]{:S(2)}) copy-start(f32[4103]{0:T(1024)S(1)} %reduce_sum.38) | copy-start | bytes 49240
  365.5 6.5 %copy-start = (bf16[4,8,128,256]{3,2,1,0:T(8,128)(2,1)S(1)}, bf16[4,8,128,256]{3,2,1,0:T(8,128)(2,1)}, u32[]{:S(2)}) copy-start(bf16[4,8,128,256]{3,2,1,0:T(8,128)(2,1)} %copy.31) | copy-start | bytes 6291460
  408.3 97.2 %all-to-all-start.6 = ((bf16[8,8,128,256]{3,2,0,1:T(8,128)(2,1)}), bf16[8,8,128,256]{3,2,0,1:T(8,128)(2,1)}, u32[]{:S(2)}, u32[]{:S(2)}) async-start(bf16[8,8,128,256]{3,2,0,1:T(8,128)(2,1)} %copy.38), calls=%async_computation.8 | async-start | bytes 8388608 | tf_op jit(solution)/shard_map/all_to_all | solution.py:40
  463.5 17.7 %slice-start.2 = ((f32[4103]{0:T(1024)}), f32[7]{0:T(128)S(1)}, s32[]{:S(2)}) async-start(f32[4103]{0:T(1024)} %copy-done.3), calls=%async_computation.17 | async-start | bytes 1024 | tf_op jit(solution)/shard_map/slice | solution.py:95
  505.6 85.7 %all-to-all-start.5 = ((bf16[7,8,128,256]{3,2,0,1:T(8,128)(2,1)}), bf16[7,8,128,256]{3,2,0,1:T(8,128)(2,1)}, u32[]{:S(2)}, u32[]{:S(2)}) async-start(bf16[7,8,128,256]{3,2,0,1:T(8,128)(2,1)} %copy.35), calls=%async_computation.7 | async-start | bytes 7340032 | tf_op jit(solution)/shard_map/all_to_all | solution.py:40
  517.1 11.1 %copy-start.5 = (f32[2,2048]{1,0:T(2,128)S(1)}, f32[2,2048]{1,0:T(2,128)}, u32[]{:S(2)}) copy-start(f32[2,2048]{1,0:T(2,128)} %param.15) | copy-start | bytes 49156
  528.9 3.5 slice-start
  531.8 2.0 slice-start.1
Sparse Core Ops, SparseCore 0:
  18.4 94.8 reduce-scatter.4
  115.9 126.1 reduce-scatter.2
  244.3 47.2 all-gather.7
  306.9 58.5 all-gather.5
  367.5 95.9 all-gather.3

commit v14 on v13

--- a/solution.py
+++ b/solution.py
@@ -41,11 +41,11 @@
         return back.reshape(n_slots * n_dp, rows, quarter)
 
     def roots_to_owners(blocks):
-        padded = jnp.pad(blocks, ((0, slots - count), (0, 0), (0, 0)))
-        return lax.all_to_all(padded.reshape(cap, n_dp, rows, quarter), "dp", 1, 1, tiled=True)
+        padded = jnp.pad(blocks.reshape(2, count, rows, quarter), ((0, 0), (0, slots - count), (0, 0), (0, 0)))
+        return lax.all_to_all(padded.reshape(2 * cap, n_dp, rows, quarter), "dp", 1, 1, tiled=True)
 
-    left_sent = roots_to_owners(left_roots)
-    right_sent = roots_to_owners(right_roots)
+    roots_sent = roots_to_owners(jnp.concatenate([left_roots, right_roots]))
+    left_sent, right_sent = roots_sent[:cap], roots_sent[cap:]
     local_norm = norm_partials[0, 0]
 
     grads, moments, adam_parts = [], [], []

time: 604 us -> 688 us (1.14)
  waiting for transfers between devices: 342 us -> 421 us
  other arithmetic: 37.8 us -> 47.4 us
    all_to_all x2 -> x1, waiting for transfers between devices: 13.8 us -> 158 us  [roots_to_owners(): lax.all_to_all(padded.reshape(2 * cap, n_dp, rows, quarter), 'dp', 1, 1,...]
    reduce_scatter x2, waiting for transfers between devices: 137 us -> 81.3 us  [on_device(): lax.psum_scatter(partials[0, b0:b1], 'group', scatter_dimension=2, tiled=...]
    all_to_all x1, waiting for transfers between devices: 31.3 us -> 18.1 us  [to_owners(): lax.all_to_all(padded.reshape(n_slots, n_dp, rows, quarter), 'dp', 1, 1,...]
    concatenate x0 -> x1, other arithmetic: none -> 9.58 us  [on_device(): roots_sent = roots_to_owners(jnp.concatenate([left_roots, right_roots]))]
  transfers between devices with their start and end apart: 12 -> 11, of which waited for: 10 -> 8; matrix products, arithmetic and copies ran while one was open for 20% -> 20% of each run, Pallas kernels for 0% -> 0%
where the time goes in v14:
time: 688 us; the launch traced here: 687 us
  waiting for transfers between devices  421 us (61%)
  blocking collectives  68.6 us (10%)
  local copies, waits for them, and re-layouts  68.2 us (10%)
  other arithmetic  47.4 us (7%)
  matrix products  38.8 us (6%)
  starting transfers between devices  29.1 us (4%)
  between operations  14.1 us (2%)
    all_to_all x1, waiting for transfers between devices, roots_to_owners(): lax.all_to_all(padded.reshape(2 * cap, n_dp, rows, quarter), 'dp', 1, 1,...  158 us
    all_to_all x3, waiting for transfers between devices, to_keepers(): lax.all_to_all(owned.reshape(n_slots, n_dp, rows, quarter), 'dp', 1, 1, t...  87.9 us
    reduce_scatter x2, waiting for transfers between devices, on_device(): lax.psum_scatter(partials[0, b0:b1], 'group', scatter_dimension=2, tiled=...  81.3 us
    all_to_all x1, blocking collectives, to_owners(): lax.all_to_all(padded.reshape(n_slots, n_dp, rows, quarter), 'dp', 1, 1,...  51.8 us
    all_gather x1, waiting for transfers between devices, on_device(): full_left = lax.all_gather(left_root, 'group', axis=2, tiled=True)  49.8 us
    all_gather x2, waiting for transfers between devices, on_device(): piece = lax.all_gather(mine, 'group', axis=2, tiled=True)  25.7 us
    squeeze x2, local copies, waits for them, and re-layouts, on_device(): partials[0, b0:b1]  24.7 us
    all_to_all x1, waiting for transfers between devices, to_owners(): lax.all_to_all(padded.reshape(n_slots, n_dp, rows, quarter), 'dp', 1, 1,...  18.1 us
  transfers between devices with their start and end apart: 11, of which 8 were waited for; matrix products, arithmetic and copies ran while one was open for 20% of the time, Pallas kernels for 0%

profile of v14, /device:TPU:0, one launch (start us, length us, event | category | flops | bytes accessed | tf_op | source)
XLA Modules:
  0.0 687.4 jit_solution(10255290528382215850)
XLA Ops:
  7.2 11.1 %slice_bitcast_fusion.1 = f32[22,128,1024]{2,1,0:T(8,128)} fusion(f32[1,54,128,1024]{3,2,1,0:T(8,128)} %param.8), kind=kLoop, calls=%fused_computation.5 | loop fusion | bytes 23068672 | tf_op jit(solution)/shard_map/squeeze | solution.py:54
  18.4 13.7 %slice_bitcast_fusion = f32[32,128,1024]{2,1,0:T(8,128)} fusion(f32[1,54,128,1024]{3,2,1,0:T(8,128)} %param.8), kind=kLoop, calls=%fused_computation | loop fusion | bytes 33554432 | tf_op jit(solution)/shard_map/squeeze | solution.py:54
  32.0 81.3 %reduce-scatter.5.cloned.1.call-done = f32[22,128,256]{2,1,0:T(8,128)} async-done(((f32[22,128,1024]{2,1,0:T(8,128)}), f32[22,128,256]{2,1,0:T(8,128)}) %reduce-scatter.5.cloned.1.call-update) | async-done | bytes 2883600 | tf_op jit(solution)/shard_map/reduce_scatter | solution.py:54
  113.3 6.8 fusion.11
  121.6 5.5 all-to-all-start.3
  127.1 9.6 %pad_maximum_fusion = bf16[108,128,256]{2,1,0:T(8,128)(2,1)} fusion(bf16[54,128,256]{2,1,0:T(8,128)(2,1)} %param.13, bf16[54,128,256]{2,1,0:T(8,128)(2,1)} %param.12), kind=kLoop, calls=%fused_computation.8 | loop fusion | flops 3538944 | bytes 14155776 | tf_op jit(solution)/shard_map/concatenate | solution.py:47
  136.7 5.3 pad.12
  142.0 4.0 copy.26
  146.0 18.1 %all-to-all-done.3 = bf16[3,8,128,256]{3,2,0,1:T(8,128)(2,1)S(1)} async-done(((bf16[3,8,128,256]{3,2,0,1:T(8,128)(2,1)}), bf16[3,8,128,256]{3,2,0,1:T(8,128)(2,1)S(1)}, u32[]{:S(2)}, u32[]{:S(2)}) %all-to-all-start.3) | async-done | bytes 1572896 | tf_op jit(solution)/shard_map/all_to_all | solution.py:35
  164.1 4.9 all-to-all-start
  170.3 158.3 %all-to-all-done = bf16[14,8,128,256]{3,2,0,1:T(8,128)(2,1)} async-done(((bf16[14,8,128,256]{3,2,0,1:T(8,128)(2,1)}), bf16[14,8,128,256]{3,2,0,1:T(8,128)(2,1)}, u32[]{:S(2)}, u32[]{:S(2)}) %all-to-all-start) | async-done | bytes 7340064 | tf_op jit(solution)/shard_map/all_to_all | solution.py:45
  328.7 5.7 fusion.26
  339.0 51.8 %all_to_all.39 = bf16[4,8,128,256]{3,2,0,1:T(8,128)(2,1)S(1)} all-to-all(bf16[4,8,128,256]{3,2,0,1:T(8,128)(2,1)S(1)} %copy.30), channel_id=1, replica_groups=mesh['dp'=8,'group'=4] {'dp'}, dimensions={1} | all-to-all | bytes 4194304 | tf_op jit(solution)/shard_map/all_to_all | solution.py:35
  392.3 4.3 copy.28
  396.8 7.5 %fusion.4 = (f32[32,128,256]{2,1,0:T(8,128)}, f32[32]{0:T(128)S(1)}) fusion(f32[32,128,256]{2,1,0:T(8,128)} %reduce-scatter.3.cloned.1.call-done, f32[54,128,256]{2,1,0:T(8,128)} %param.9), kind=kLoop, calls=%fused_computation.14 | loop fusion | flops 8388576 | bytes 12583040 | tf_op jit(solution)/shard_map/add | solution.py:58
  408.9 5.3 convolution_convert_fusion.1
  418.4 5.7 all-to-all-start.6
  424.3 25.7 %all-gather.6.cloned.1.call-done = bf16[4,1024,1024]{2,1,0:T(8,128)(2,1)} async-done(((bf16[4,1024,256]{2,1,0:T(8,128)(2,1)}), bf16[4,1024,1024]{2,1,0:T(8,128)(2,1)}) %all-gather.6.cloned.1.call-update) | async-done | bytes 8388624 | tf_op jit(solution)/shard_map/all_gather | solution.py:77
  449.9 6.5 fusion.14
  456.4 7.4 %convolution_convert_fusion = bf16[4,1024,256]{2,1,0:T(8,128)(2,1)S(1)} fusion(bf16[4,1024,1024]{2,1,0:T(8,128)(2,1)} %all-gather.6.cloned.1.call-done, bf16[4,1024,256]{2,1,0:T(8,128)(2,1)S(1)} %bitcast.42), kind=kOutput, calls=%fused_computation.25 | convolution fusion | flops 2148532224 | bytes 12582912 | tf_op jit(solution)/shard_map/cim,cij->cmj/dot_general | solution.py:82
  466.9 26.4 %all-to-all-done.6 = bf16[6,8,128,256]{3,2,0,1:T(8,128)(2,1)S(1)} async-done(((bf16[6,8,128,256]{3,2,0,1:T(8,128)(2,1)}), bf16[6,8,128,256]{3,2,0,1:T(8,128)(2,1)S(1)}, u32[]{:S(2)}, u32[]{:S(2)}) %all-to-all-start.6) | async-done | bytes 3145760 | tf_op jit(solution)/shard_map/all_to_all | solution.py:40
  493.3 4.8 all-to-all-start.5
  498.2 49.8 %all-gather.4.cloned.1.call-done = bf16[7,1024,1024]{2,1,0:T(8,128)(2,1)} async-done(((bf16[7,1024,256]{2,1,0:T(8,128)(2,1)}), bf16[7,1024,1024]{2,1,0:T(8,128)(2,1)}) %all-gather.4.cloned.1.call-update) | async-done | bytes 14680080 | tf_op jit(solution)/shard_map/all_gather | solution.py:93
  548.0 17.8 %multiply_reduce_fusion = (f32[7]{0:T(128)S(1)}, f32[7,1024,256]{2,1,0:T(8,128)}) fusion(bf16[7,1024,1024]{2,1,0:T(8,128)(2,1)} %all-gather.4.cloned.1.call-done, bf16[7,1024,256]{2,1,0:T(8,128)(2,1)} %bitcast.48, bf16[3,1024,1024]{2,1,0:T(8,128)(2,1)} %all-gather.8.cloned.1.call-done, bf16[4,1024,1024]{2,1,0:T(8,128)(2,1)} %all-gather.6.cloned.1.call-done), kind=kOutput, calls=%fused_computation.7 | convolution fusion | flops 7529037824 | bytes 40370204 | tf_op jit(solution)/shard_map/cim,cmj->cij/dot_general | solution.py:94
  565.8 5.9 psum.14
  571.8 3.8 multiply_convert_fusion
  577.8 12.7 %all-to-all-done.5 = bf16[8,8,128,256]{3,2,0,1:T(8,128)(2,1)} async-done(((bf16[8,8,128,256]{3,2,0,1:T(8,128)(2,1)}), bf16[8,8,128,256]{3,2,0,1:T(8,128)(2,1)}, u32[]{:S(2)}, u32[]{:S(2)}) %all-to-all-start.5) | async-done | bytes 4194336 | tf_op jit(solution)/shard_map/all_to_all | solution.py:40
  590.5 4.5 all-to-all-start.4
  595.0 6.8 pad_maximum_fusion.1
  602.3 10.9 %psum.15 = f32[2,2048]{1,0:T(2,128)S(1)} all-reduce(f32[2,2048]{1,0:T(2,128)S(1)} %reshape.78), channel_id=1, replica_groups=mesh['dp'=8,'group'=4] {'group'}, use_global_device_ids=true, to_apply=%region_7.8 | all-reduce | flops 4096 | bytes 32768 | tf_op jit(solution)/shard_map/psum | solution.py:102
  618.7 8.7 %multiply_add_fusion = (f32[54,128,256]{2,1,0:T(8,128)}, f32[54,128,256]{2,1,0:T(8,128)}) fusion(f32[54,128,256]{2,1,0:T(8,128)S(1)} %bitcast.44, bf16[22,128,256]{2,1,0:T(8,128)(2,1)S(1)} %get-tuple-element.32, bf16[32,128,256]{2,1,0:T(8,128)(2,1)S(1)} %bitcast.38, bf16[22,128,256]{2,1,0:T(8,128)(2,1)S(1)} %get-tuple-element.33, ...), kind=kLoop, calls=%fused_computation.10 | loop fusion | flops 17694720 | bytes 35389440 | tf_op jit(solution)/shard_map/add | solution.py:108
  627.4 48.8 %all-to-all-done.4 = bf16[7,8,128,256]{3,2,0,1:T(8,128)(2,1)} async-done(((bf16[7,8,128,256]{3,2,0,1:T(8,128)(2,1)}), bf16[7,8,128,256]{3,2,0,1:T(8,128)(2,1)}, u32[]{:S(2)}, u32[]{:S(2)}) %all-to-all-start.4) | async-done | bytes 3670048 | tf_op jit(solution)/shard_map/all_to_all | solution.py:40
  (66 shorter events, 33.9 us)
Async XLA Ops:
  7.2 106.2 %reduce-scatter.5.cloned.1.call-start = ((), (), s32[]{:S(2)}) async-start(), calls=%async_computation.11 | async-start | bytes 14417920 | tf_op jit(solution)/shard_map/reduce_scatter | solution.py:54
  18.3 318.1 %reduce-scatter.3.cloned.1.call-start = ((), (), s32[]{:S(2)}) async-start(), calls=%async_computation.9 | async-start | bytes 20971520 | tf_op jit(solution)/shard_map/reduce_scatter | solution.py:54
  121.6 42.5 %all-to-all-start.3 = ((bf16[3,8,128,256]{3,2,0,1:T(8,128)(2,1)}), bf16[3,8,128,256]{3,2,0,1:T(8,128)(2,1)S(1)}, u32[]{:S(2)}, u32[]{:S(2)}) async-start(bf16[3,8,128,256]{3,2,0,1:T(8,128)(2,1)} %copy.32), calls=%async_computation.5 | async-start | bytes 3145728 | tf_op jit(solution)/shard_map/all_to_all | solution.py:35
  164.1 164.6 %all-to-all-start = ((bf16[14,8,128,256]{3,2,0,1:T(8,128)(2,1)}), bf16[14,8,128,256]{3,2,0,1:T(8,128)(2,1)}, u32[]{:S(2)}, u32[]{:S(2)}) async-start(bf16[14,8,128,256]{3,2,0,1:T(8,128)(2,1)} %copy.26), calls=%async_computation.1 | async-start | bytes 14680064 | tf_op jit(solution)/shard_map/all_to_all | solution.py:45
  169.0 239.9 %all-gather.8.cloned.1.call-start = ((), (), s32[]{:S(2)}) async-start(), calls=%async_computation.13 | async-start | bytes 7864320 | tf_op jit(solution)/shard_map/all_gather | solution.py:77
  170.3 279.7 %all-gather.6.cloned.1.call-start = ((), (), s32[]{:S(2)}) async-start(), calls=%async_computation.12 | async-start | bytes 10485760 | tf_op jit(solution)/shard_map/all_gather | solution.py:77
  392.3 4.4 copy-start.3
  392.3 155.7 %all-gather.4.cloned.1.call-start = ((), (), s32[]{:S(2)}) async-start(), calls=%async_computation.10 | async-start | bytes 18350080 | tf_op jit(solution)/shard_map/all_gather | solution.py:93
  396.8 12.2 %copy-start.1 = (bf16[3,8,128,256]{3,2,1,0:T(8,128)(2,1)S(1)}, bf16[3,8,128,256]{3,2,1,0:T(8,128)(2,1)}, u32[]{:S(2)}) copy-start(bf16[3,8,128,256]{3,2,1,0:T(8,128)(2,1)} %copy.33) | copy-start | bytes 4718596
  405.3 13.1 %all-to-all-start.1 = ((f32[8,1,4103]{2,1,0:T(1,128)}), f32[8,1,4103]{2,1,0:T(1,128)S(1)}, u32[]{:S(2)}, u32[]{:S(2)}) async-start(f32[8,1,4103]{2,1,0:T(1,128)} %all_to_all.25), calls=%async_computation.3 | async-start | bytes 270336 | tf_op jit(solution)/shard_map/all_to_all | solution.py:70
  408.9 5.3 copy-start.5
  418.4 74.9 %all-to-all-start.6 = ((bf16[6,8,128,256]{3,2,0,1:T(8,128)(2,1)}), bf16[6,8,128,256]{3,2,0,1:T(8,128)(2,1)S(1)}, u32[]{:S(2)}, u32[]{:S(2)}) async-start(bf16[6,8,128,256]{3,2,0,1:T(8,128)(2,1)} %copy.40), calls=%async_computation.8 | async-start | bytes 6291456 | tf_op jit(solution)/shard_map/all_to_all | solution.py:40
  424.3 73.8 %copy-start.2 = (f32[4103]{0:T(1024)}, f32[4103]{0:T(1024)S(1)}, u32[]{:S(2)}) copy-start(f32[4103]{0:T(1024)S(1)} %reduce_sum.38) | copy-start | bytes 49240
  449.9 6.5 copy-start
  493.3 97.2 %all-to-all-start.5 = ((bf16[8,8,128,256]{3,2,0,1:T(8,128)(2,1)}), bf16[8,8,128,256]{3,2,0,1:T(8,128)(2,1)}, u32[]{:S(2)}, u32[]{:S(2)}) async-start(bf16[8,8,128,256]{3,2,0,1:T(8,128)(2,1)} %copy.37), calls=%async_computation.7 | async-start | bytes 8388608 | tf_op jit(solution)/shard_map/all_to_all | solution.py:40
  548.0 17.8 %slice-start.2 = ((f32[4103]{0:T(1024)}), f32[7]{0:T(128)S(1)}, s32[]{:S(2)}) async-start(f32[4103]{0:T(1024)} %copy-done.2), calls=%async_computation.16 | async-start | bytes 1024 | tf_op jit(solution)/shard_map/slice | solution.py:95
  590.5 85.7 %all-to-all-start.4 = ((bf16[7,8,128,256]{3,2,0,1:T(8,128)(2,1)}), bf16[7,8,128,256]{3,2,0,1:T(8,128)(2,1)}, u32[]{:S(2)}, u32[]{:S(2)}) async-start(bf16[7,8,128,256]{3,2,0,1:T(8,128)(2,1)} %copy.34), calls=%async_computation.6 | async-start | bytes 7340032 | tf_op jit(solution)/shard_map/all_to_all | solution.py:40
  602.1 11.1 %copy-start.4 = (f32[2,2048]{1,0:T(2,128)S(1)}, f32[2,2048]{1,0:T(2,128)}, u32[]{:S(2)}) copy-start(f32[2,2048]{1,0:T(2,128)} %param.15) | copy-start | bytes 49156
  613.9 3.5 slice-start
  616.7 2.0 slice-start.1
Sparse Core Ops, SparseCore 0:
  18.4 94.8 reduce-scatter.4
  115.9 126.1 reduce-scatter.2
  244.3 47.2 all-gather.7
  392.4 57.4 all-gather.5
  452.0 95.9 all-gather.3
